TPU v7x, 256 devices: a whole 4x4x8 slice. The times are simulated.
256 devices in a mesh: section: 2 (over y_lo), dp: 4 (over x), tensor: 32 (over z, y_hi, core).
Axes of the slice: x: 4, y: 4 (y_hi: 2, y_lo: 2; y = y_hi * 2 + y_lo), z: 8, core: 2. Of those that a mesh axis runs over, the one named last changes fastest.
Arguments:
- inputs: bfloat16 [2, 1024, 12288], P('section', 'dp', 'tensor'), may hold values from -6 to 6
- queries: bfloat16 [2, 1024, 8192], P('section', 'dp', 'tensor'), may hold values from -8 to 8
- keys: bfloat16 [2, 1024, 8192], P('section', 'dp', 'tensor'), may hold values from -8 to 8
- w_value: bfloat16 [2, 12288, 8192], P('section', None, 'tensor'), may hold values from -0.0546875 to 0.0546875
- w_out: bfloat16 [2, 8192, 12288], P('section', 'tensor'), may hold values from -0.75 to 0.75
Outputs:
- next_inputs: bfloat16 [2, 1024, 12288], P('section', 'dp', 'tensor')
All inputs are finite; a program needn't handle non-finite values.
Results may differ from a plain program's by a relative error of at most 0.023.
Values may be sent and summed in bfloat16 or wider, within the bound.
No kernel may reach another device: no remote copies, remote signals or barrier semaphores. Data moves between devices by JAX's collectives and lax.ppermute only.
A program may use at most 64 MiB of HBM per device.

v0:
```python
import jax
import jax.numpy as jnp
from jax import lax
from jax.sharding import PartitionSpec as P

HEAD_SIZE = 128
LEN = 256


def partner(value, axis, stride):
    mask = 2**stride
    pairs = [(source, source ^ mask) for source in range(lax.axis_size(axis))]
    return lax.ppermute(value, axis, pairs)


def on_device(inputs, queries, keys, w_value, w_out):
    activ = inputs[0]
    weight_v = w_value[0]
    weight_o = w_out[0]
    length = activ.shape[0]
    col_width = activ.shape[1]
    features_all = lax.all_gather(activ, "tensor", axis=1, tiled=True)
    values = jnp.dot(features_all, weight_v, preferred_element_type=jnp.float32)
    values = values.astype(jnp.bfloat16)
    heads_here = weight_v.shape[1] // HEAD_SIZE
    query_rows = queries[0].reshape(length // LEN, LEN, heads_here, HEAD_SIZE)
    key_rows = keys[0].reshape(length // LEN, LEN, heads_here, HEAD_SIZE)
    value_rows = values.reshape(length // LEN, LEN, heads_here, HEAD_SIZE)
    scores = jnp.einsum(
        "bqhd,bkhd->bhqk", query_rows, key_rows, preferred_element_type=jnp.float32
    ) / jnp.sqrt(jnp.float32(HEAD_SIZE))
    rows = lax.broadcasted_iota(jnp.int32, (LEN, LEN), 0)
    cols = lax.broadcasted_iota(jnp.int32, (LEN, LEN), 1)
    scores = jnp.where((cols <= rows)[None, None], scores, jnp.float32(-1e30))
    top = jnp.max(scores, axis=-1, keepdims=True)
    expo = jnp.exp(scores - top)
    probs = (expo / jnp.sum(expo, axis=-1, keepdims=True)).astype(jnp.bfloat16)
    context = jnp.einsum(
        "bhqk,bkhd->bqhd", probs, value_rows, preferred_element_type=jnp.float32
    ).astype(jnp.bfloat16)
    context = context.reshape(length, heads_here * HEAD_SIZE)
    partial_term = jnp.dot(context, weight_o, preferred_element_type=jnp.float32)
    total = lax.psum(partial_term.astype(jnp.bfloat16), "tensor").astype(jnp.float32)
    mine = lax.dynamic_slice_in_dim(total, lax.axis_index("tensor") * col_width, col_width, 1)
    result = (mine + activ.astype(jnp.float32)).astype(jnp.bfloat16)
    passed = partner(result, "section", 0)
    return passed[None]


def solution(mesh):
    return jax.shard_map(
        on_device,
        mesh=mesh,
        in_specs=(
            P("section", "dp", "tensor"),
            P("section", "dp", "tensor"),
            P("section", "dp", "tensor"),
            P("section", None, "tensor"),
            P("section", "tensor", None),
        ),
        out_specs=P("section", "dp", "tensor"),
        check_vma=False,
    )
```

profile of v0, /device:TPU:2, one launch (start us, length us, event | category | flops | bytes accessed | tf_op | source)
XLA Modules:
  0.0 425.6 jit_solution(8691334138822509246)
XLA Ops:
  6.5 0.0 all-gather.3.cloned.1.call-start
  6.5 0.7 all-gather.3.cloned.1.call-update
  7.3 0.0 all-reduce.2.cloned.1.call-start
  7.3 0.9 reshape.47
  8.2 0.9 reshape.48
  9.2 0.3 fusion.23
  9.6 0.2 fusion.7
  9.8 100.3 %all-gather.3.cloned.1.call-done = bf16[1,256,12288]{2,1,0:T(8,128)(2,1)} async-done(((bf16[1,256,384]{2,1,0:T(8,128)(2,1)}), bf16[1,256,12288]{2,1,0:T(8,128)(2,1)}) %all-gather.3.cloned.1.call-update) | async-done | bytes 6291472 | tf_op jit(solution)/shard_map/all_gather | solution.py:22
  110.1 7.1 %fusion.8 = bf16[256,256]{0,1:T(8,128)(2,1)S(1)} fusion(bf16[1,12288,256]{2,1,0:T(8,128)(2,1)} %param.8, bf16[1,256,12288]{2,1,0:T(8,128)(2,1)} %all-gather.3.cloned.1.call-done), kind=kOutput, calls=%fused_computation.11 | convolution fusion | flops 1610678272 | bytes 12713984 | tf_op jit(solution)/shard_map/dot_general | solution.py:23
  117.3 0.3 convolution_convert_fusion.1
  117.5 7.3 %convolution_convert_fusion = bf16[256,12288]{1,0:T(8,128)(2,1)} fusion(bf16[256,256]{0,1:T(8,128)(2,1)S(1)} %bitcast.28, bf16[1,256,12288]{2,1,0:T(8,128)(2,1)} %param.9), kind=kOutput, calls=%fused_computation.1 | convolution fusion | flops 1613758464 | bytes 12713984 | tf_op jit(solution)/shard_map/dot_general | solution.py:42
  124.8 0.0 copy-start
  124.8 0.0 all-reduce.2.cloned.1.call-update
  124.8 286.5 %all-reduce.2.cloned.1.call-done = bf16[256,12288]{1,0:T(8,128)(2,1)} async-done(((bf16[256,12288]{1,0:T(8,128)(2,1)}), bf16[256,12288]{1,0:T(8,128)(2,1)}) %all-reduce.2.cloned.1.call-update) | async-done | bytes 6291472 | tf_op jit(solution)/shard_map/psum | solution.py:43
  411.4 0.0 copy-done
  411.4 1.0 fusion.13
  412.4 0.8 collective-permute-start
  413.1 5.0 %collective-permute-done = bf16[256,384]{1,0:T(8,128)(2,1)S(1)} collective-permute-done((bf16[256,384]{1,0:T(8,128)(2,1)S(1)}, bf16[256,384]{1,0:T(8,128)(2,1)S(1)}, u32[]{:S(2)}, u32[]{:S(2)}) %collective-permute-start) | collective-permute-done | bytes 196640 | tf_op jit(solution)/shard_map/ppermute | solution.py:13
  418.1 0.7 copy.24
  (1 shorter events, 0.0 us)
Async XLA Ops:
  6.5 103.6 %all-gather.3.cloned.1.call-start = ((), (), s32[]{:S(2)}) async-start(), calls=%async_computation.1 | async-start | bytes 6488064 | tf_op jit(solution)/shard_map/all_gather | solution.py:22
  7.3 404.1 %all-reduce.2.cloned.1.call-start = ((), (), s32[]{:S(2)}) async-start(), calls=%async_computation | async-start | bytes 12582912 | tf_op jit(solution)/shard_map/psum | solution.py:43
  124.8 286.6 %copy-start = (bf16[1,256,384]{2,1,0:T(8,128)(2,1)S(1)}, bf16[1,256,384]{2,1,0:T(8,128)(2,1)}, u32[]{:S(2)}) copy-start(bf16[1,256,384]{2,1,0:T(8,128)(2,1)} %param.5) | copy-start | bytes 589828
  412.4 5.8 %collective-permute-start = (bf16[256,384]{1,0:T(8,128)(2,1)S(1)}, bf16[256,384]{1,0:T(8,128)(2,1)S(1)}, u32[]{:S(2)}, u32[]{:S(2)}) collective-permute-start(bf16[256,384]{1,0:T(8,128)(2,1)S(1)} %fusion.13), channel_id=1, source_target_pairs={{0,128},{128,0},{1,129},{129,1},{2,130},{130,2},{3,131},{131,3},{4... | collective-permute-start | bytes 589832 | tf_op jit(solution)/shard_map/ppermute | solution.py:13
Sparse Core Ops, SparseCore 0:
  9.9 100.1 all-gather.2
  125.0 286.3 all-reduce.1
where the time goes:
time: 426 us
  waiting for transfers between devices  393 us (92%)
  matrix products  15.3 us (4%)
  between operations  13.4 us (3%)
    psum x1, waiting for transfers between devices, on_device(): lax.psum(partial_term.astype(jnp.bfloat16), 'tensor').astype(jnp.float32)  287 us
    all_gather x1, waiting for transfers between devices, on_device(): features_all = lax.all_gather(activ, 'tensor', axis=1, tiled=True)  100 us
  transfers between devices with their start and end apart: 3, of which 3 were waited for; matrix products, arithmetic and copies ran while one was open for 1% of the time, Pallas kernels for 0%

commit v1 on v0

v1 whole, which is shorter than its diff:
```python
import jax
import jax.numpy as jnp
from jax import lax
from jax.sharding import Mesh
from jax.sharding import PartitionSpec as P

HEAD_SIZE = 128
LEN = 256
N_Z, N_Y, N_C = 8, 2, 2


def on_device(inputs, queries, keys, w_value, w_out):
    activ = inputs[0]
    weight_v = w_value[0]
    weight_o = w_out[0]
    length = activ.shape[0]
    col_width = activ.shape[1]
    n_feat = weight_v.shape[0]

    gathered = lax.all_gather(activ, "ty", axis=0)
    gathered = lax.all_gather(gathered, "tz", axis=0)
    gathered = lax.all_gather(gathered, "tc", axis=0)
    wv = weight_v.reshape(N_Z, N_Y, N_C, col_width, weight_v.shape[1])
    values = jnp.einsum(
        "czytf,zycfh->th", gathered, wv, preferred_element_type=jnp.float32
    ).astype(jnp.bfloat16)

    heads_here = weight_v.shape[1] // HEAD_SIZE
    query_rows = queries[0].reshape(length // LEN, LEN, heads_here, HEAD_SIZE)
    key_rows = keys[0].reshape(length // LEN, LEN, heads_here, HEAD_SIZE)
    value_rows = values.reshape(length // LEN, LEN, heads_here, HEAD_SIZE)
    scores = jnp.einsum(
        "bqhd,bkhd->bhqk", query_rows, key_rows, preferred_element_type=jnp.float32
    ) / jnp.sqrt(jnp.float32(HEAD_SIZE))
    rows = lax.broadcasted_iota(jnp.int32, (LEN, LEN), 0)
    cols = lax.broadcasted_iota(jnp.int32, (LEN, LEN), 1)
    scores = jnp.where((cols <= rows)[None, None], scores, jnp.float32(-1e30))
    top = jnp.max(scores, axis=-1, keepdims=True)
    expo = jnp.exp(scores - top)
    probs = (expo / jnp.sum(expo, axis=-1, keepdims=True)).astype(jnp.bfloat16)
    context = jnp.einsum(
        "bhqk,bkhd->bqhd", probs, value_rows, preferred_element_type=jnp.float32
    ).astype(jnp.bfloat16)
    context = context.reshape(length, heads_here * HEAD_SIZE)

    wo = weight_o.reshape(weight_o.shape[0], N_Z, N_Y, N_C, col_width)
    partial_term = jnp.einsum(
        "tk,kzycf->czytf", context, wo, preferred_element_type=jnp.float32
    ).astype(jnp.bfloat16)
    part = lax.psum_scatter(partial_term, "tc", scatter_dimension=0, tiled=False)
    part = lax.psum_scatter(part, "tz", scatter_dimension=0, tiled=False)
    part = lax.psum_scatter(part, "ty", scatter_dimension=0, tiled=False)
    result = (part.astype(jnp.float32) + activ.astype(jnp.float32)).astype(jnp.bfloat16)
    passed = lax.ppermute(result, "section", [(0, 1), (1, 0)])
    return passed[None]


def solution(mesh):
    n_sec, n_dp, n_t = mesh.devices.shape
    sub = Mesh(
        mesh.devices.reshape(n_sec, n_dp, N_Z, N_Y, N_C),
        ("section", "dp", "tz", "ty", "tc"),
    )
    spec = P("section", "dp", ("tz", "ty", "tc"))
    return jax.shard_map(
        on_device,
        mesh=sub,
        in_specs=(
            spec,
            spec,
            spec,
            P("section", None, ("tz", "ty", "tc")),
            P("section", ("tz", "ty", "tc"), None),
        ),
        out_specs=spec,
        check_vma=False,
    )
```

time: 426 us -> 238 us (0.56)
  waiting for transfers between devices: 393 us -> 170 us
  local copies, waits for them, and re-layouts: 2.56 us -> 23.1 us
  blocking collectives: 0 us -> 11.4 us
    psum x1 -> x0, waiting for transfers between devices: 287 us -> none  [on_device(): lax.psum(partial_term.astype(jnp.bfloat16), 'tensor').astype(jnp.float32)]
    reduce_scatter x0 -> x2, waiting for transfers between devices: none -> 70.1 us  [the longest x1 48.4 us: on_device(): part = lax.psum_scatter(part, 'tz', scatter_dimension=0, tiled=False)]
    all_gather x1 -> x2, waiting for transfers between devices: 100 us -> 51.2 us  [the longest x1 45.9 us: on_device(): gathered = lax.all_gather(gathered, 'tz', axis=0)]
    unnamed x2 -> x6, waiting for transfers between devices: 0.73 us -> 43.3 us
    another operation x2 -> x3, local copies, waits for them, and re-layouts: 1.88 us -> 16.6 us  [the longest x1 14.7 us: on_device(): wo = weight_o.reshape(weight_o.shape[0], N_Z, N_Y, N_C, col_width)]
    all_gather x0 -> x1, blocking collectives: none -> 11.4 us  [on_device(): gathered = lax.all_gather(activ, 'ty', axis=0)]
    reduce_scatter x0 -> x1, local copies, waits for them, and re-layouts: none -> 4.65 us  [on_device(): lax.psum_scatter(partial_term, 'tc', scatter_dimension=0, tiled=False)]
  transfers between devices with their start and end apart: 3 -> 6, of which waited for: 3 -> 6; matrix products, arithmetic and copies ran while one was open for 1% -> 7% of each run, Pallas kernels for 0% -> 0%
where the time goes in v1:
time: 238 us
  waiting for transfers between devices  170 us (71%)
  local copies, waits for them, and re-layouts  23.1 us (10%)
  matrix products  17.6 us (7%)
  between operations  13.2 us (6%)
  blocking collectives  11.4 us (5%)
    reduce_scatter x1, waiting for transfers between devices, on_device(): part = lax.psum_scatter(part, 'tz', scatter_dimension=0, tiled=False)  48.4 us
    all_gather x1, waiting for transfers between devices, on_device(): gathered = lax.all_gather(gathered, 'tz', axis=0)  45.9 us
    unnamed x6, waiting for transfers between devices  43.3 us
    reduce_scatter x1, waiting for transfers between devices, on_device(): part = lax.psum_scatter(part, 'ty', scatter_dimension=0, tiled=False)  21.7 us
    another operation x1, local copies, waits for them, and re-layouts, on_device(): wo = weight_o.reshape(weight_o.shape[0], N_Z, N_Y, N_C, col_width)  14.7 us
    all_gather x1, blocking collectives, on_device(): gathered = lax.all_gather(activ, 'ty', axis=0)  11.4 us
    dot_general x1, matrix products, on_device(): jnp.einsum('tk,kzycf->czytf', context, wo, preferred_element_type=jnp.flo...  9.62 us
    dot_general x1, matrix products, on_device(): jnp.einsum('czytf,zycfh->th', gathered, wv, preferred_element_type=jnp.fl...  7.15 us
  transfers between devices with their start and end apart: 6, of which 6 were waited for; matrix products, arithmetic and copies ran while one was open for 7% of the time, Pallas kernels for 0%

profile of v1, /device:TPU:2, one launch (start us, length us, event | category | flops | bytes accessed | tf_op | source)
XLA Modules:
  0.0 237.6 jit_solution(9289622451744424759)
XLA Ops:
  6.5 11.4 %all_gather.15 = bf16[2,256,384]{2,1,0:T(8,128)(2,1)} all-gather(bf16[1,256,384]{2,1,0:T(8,128)(2,1)} %param.5), channel_id=1, replica_groups=mesh['section'=2,'dp'=4,'tz'=8,'ty'=2,'tc'=2] {'ty'}, dimensions={0}, use_global_device_ids=true | all-gather | bytes 589824 | tf_op jit(solution)/shard_map/all_gather | solution.py:20
  17.9 0.0 all-gather.7.cloned.1.call-start
  18.0 45.9 %all-gather.5.cloned.1.call-done = bf16[16,256,384]{2,1,0:T(8,128)(2,1)} async-done(((bf16[2,256,384]{2,1,0:T(8,128)(2,1)}), bf16[16,256,384]{2,1,0:T(8,128)(2,1)}) %all-gather.5.cloned.1.call-update) | async-done | bytes 3145744 | tf_op jit(solution)/shard_map/all_gather | solution.py:21
  64.0 0.9 reshape.51
  64.9 0.9 reshape.52
  65.9 14.7 %reshape_squeeze.9 = bf16[256,8,2,2,384]{4,3,2,1,0:T(2,128)(2,1)} reshape(bf16[1,256,12288]{2,1,0:T(8,128)(2,1)} %param.9) | data formatting | bytes 12582912 | tf_op jit(solution)/shard_map/reshape;squeeze | solution.py:46
  80.6 0.3 fusion.31
  80.9 0.2 fusion.10
  81.2 5.3 %all-gather.7.cloned.1.call-done = bf16[16,2,256,384]{3,2,1,0:T(8,128)(2,1)} async-done(((bf16[8,2,256,384]{3,2,1,0:T(8,128)(2,1)}), bf16[16,2,256,384]{3,2,1,0:T(8,128)(2,1)}) %all-gather.7.cloned.1.call-update) | async-done | bytes 6291472 | tf_op jit(solution)/shard_map/all_gather | solution.py:22
  86.5 7.1 %fusion.16 = bf16[256,256]{0,1:T(8,128)(2,1)S(1)} fusion(bf16[8,2,2,384,256]{4,3,2,1,0:T(8,128)(2,1)} %bitcast.39, bf16[2,8,2,256,384]{4,3,2,1,0:T(8,128)(2,1)} %bitcast.40), kind=kOutput, calls=%fused_computation.14 | convolution fusion | flops 1610678272 | bytes 12713984 | tf_op jit(solution)/shard_map/czytf,zycfh->th/dot_general | solution.py:24
  93.6 0.3 convolution_convert_fusion
  93.9 9.6 %convert_bitcast_fusion = bf16[2,8,2,256,384]{4,3,0,2,1:T(8,128)(2,1)} fusion(bf16[256,256,1,1,1]{0,1,4,3,2:T(8,128)(2,1)S(1)} %bitcast.38, bf16[256,8,2,2,384]{4,3,2,1,0:T(2,128)(2,1)} %reshape_squeeze.9), kind=kOutput, calls=%fused_computation.6 | convolution fusion | flops 1613758464 | bytes 12713984 | tf_op jit(solution)/shard_map/tk,kzycf->czytf/dot_general | solution.py:47
  103.6 0.0 reduce-scatter.6.cloned.1.call-start
  103.6 0.6 copy-done.1
  104.2 0.6 dynamic-slice
  104.8 43.2 %all-reduce.3.cloned.1.call-done = bf16[2,8,2,256,384]{4,3,0,2,1:T(8,128)(2,1)} async-done(((bf16[2,8,2,256,384]{4,3,0,2,1:T(8,128)(2,1)}), bf16[2,8,2,256,384]{4,3,0,2,1:T(8,128)(2,1)}) %all-reduce.3.cloned.1.call-update) | async-done | bytes 6291472
  148.0 4.6 %dynamic-slice_bitcast_fusion = bf16[8,2,256,384]{3,2,1,0:T(8,128)(2,1)} fusion(bf16[2,8,2,256,384]{4,3,0,2,1:T(8,128)(2,1)} %all-reduce.3.cloned.1.call-done, u32[]{:T(128)} %bitcast.25), kind=kLoop, calls=%fused_computation.7 | loop fusion | bytes 6291460 | tf_op jit(solution)/shard_map/reduce_scatter | solution.py:50
  152.7 0.0 reduce-scatter.8.cloned.1.call-start
  152.7 48.4 %reduce-scatter.6.cloned.1.call-done = bf16[1,2,256,384]{3,2,1,0:T(8,128)(2,1)} async-done(((bf16[8,2,256,384]{3,2,1,0:T(8,128)(2,1)}), bf16[1,2,256,384]{3,2,1,0:T(8,128)(2,1)}) %reduce-scatter.6.cloned.1.call-update) | async-done | bytes 393232 | tf_op jit(solution)/shard_map/reduce_scatter | solution.py:51
  201.1 21.7 %reduce-scatter.8.cloned.1.call-done = bf16[1,256,384]{2,1,0:T(8,128)(2,1)} async-done(((bf16[2,256,384]{2,1,0:T(8,128)(2,1)}), bf16[1,256,384]{2,1,0:T(8,128)(2,1)}) %reduce-scatter.8.cloned.1.call-update) | async-done | bytes 196624 | tf_op jit(solution)/shard_map/reduce_scatter | solution.py:52
  222.8 1.0 fusion.21
  223.8 0.7 collective-permute-start
  224.5 5.9 %collective-permute-done = bf16[256,384]{1,0:T(8,128)(2,1)S(1)} collective-permute-done((bf16[256,384]{1,0:T(8,128)(2,1)S(1)}, bf16[256,384]{1,0:T(8,128)(2,1)S(1)}, u32[]{:S(2)}, u32[]{:S(2)}) %collective-permute-start) | collective-permute-done | bytes 196640 | tf_op jit(solution)/shard_map/ppermute | solution.py:54
  230.4 0.7 copy.64
  (11 shorter events, 0.2 us)
Async XLA Ops:
  6.5 57.4 %all-gather.5.cloned.1.call-start = ((), (), s32[]{:S(2)}) async-start(), calls=%async_computation.4 | async-start | bytes 3538944 | tf_op jit(solution)/shard_map/all_gather | solution.py:21
  17.9 68.5 %all-gather.7.cloned.1.call-start = ((), (), s32[]{:S(2)}) async-start(), calls=%async_computation.5 | async-start | bytes 9437184 | tf_op jit(solution)/shard_map/all_gather | solution.py:22
  63.9 84.0 %all-reduce.3.cloned.1.call-start = ((), (), s32[]{:S(2)}) async-start(), calls=%async_computation.6 | async-start | bytes 12582912
  103.5 0.7 copy-start.1
  103.5 119.3 %copy-start = (bf16[1,256,384]{2,1,0:T(8,128)(2,1)S(1)}, bf16[1,256,384]{2,1,0:T(8,128)(2,1)}, u32[]{:S(2)}) copy-start(bf16[1,256,384]{2,1,0:T(8,128)(2,1)} %param.5) | copy-start | bytes 589828
  103.6 97.5 %reduce-scatter.6.cloned.1.call-start = ((), (), s32[]{:S(2)}) async-start(), calls=%async_computation.2 | async-start | bytes 3538944 | tf_op jit(solution)/shard_map/reduce_scatter | solution.py:51
  152.7 70.1 %reduce-scatter.8.cloned.1.call-start = ((), (), s32[]{:S(2)}) async-start(), calls=%async_computation.3 | async-start | bytes 589824 | tf_op jit(solution)/shard_map/reduce_scatter | solution.py:52
  223.8 6.6 %collective-permute-start = (bf16[256,384]{1,0:T(8,128)(2,1)S(1)}, bf16[256,384]{1,0:T(8,128)(2,1)S(1)}, u32[]{:S(2)}, u32[]{:S(2)}) collective-permute-start(bf16[256,384]{1,0:T(8,128)(2,1)S(1)} %fusion.21), channel_id=1, source_target_pairs={{0,128},{128,0},{1,129},{129,1},{2,130},{130,2},{3,131},{131,3},{4... | collective-permute-start | bytes 589832 | tf_op jit(solution)/shard_map/ppermute | solution.py:54
Sparse Core Ops, SparseCore 0:
  18.1 45.8 all-gather.4
  65.7 20.7 all-gather.6
  103.7 44.2 all-reduce.2
  152.8 48.2 reduce-scatter.5
  203.4 19.3 reduce-scatter.7

commit v2 on v1

--- a/solution.py
+++ b/solution.py
@@ -1,12 +1,56 @@
 import jax
 import jax.numpy as jnp
 from jax import lax
+from jax.experimental import pallas as pl
+from jax.experimental.pallas import tpu as pltpu
 from jax.sharding import Mesh
 from jax.sharding import PartitionSpec as P
 
 HEAD_SIZE = 128
 LEN = 256
 N_Z, N_Y, N_C = 8, 2, 2
+GROUPS_PER_STEP = 4
+
+
+def swap(value, axis):
+    return lax.ppermute(value, axis, [(0, 1), (1, 0)])
+
+
+def out_proj_kernel(core_ref, ctx_ref, w_ref, mine_ref, sib_ref):
+    width = mine_ref.shape[2]
+    is_zero = core_ref[0] == 0
+    ctx = ctx_ref[...]
+    for i in range(mine_ref.shape[0]):
+        lo = i * 2 * width
+        d0 = jnp.dot(ctx, w_ref[:, lo:lo + width], preferred_element_type=jnp.float32)
+        d1 = jnp.dot(ctx, w_ref[:, lo + width:lo + 2 * width], preferred_element_type=jnp.float32)
+        d0 = d0.astype(jnp.bfloat16)
+        d1 = d1.astype(jnp.bfloat16)
+        mine_ref[i] = jnp.where(is_zero, d0, d1)
+        sib_ref[i] = jnp.where(is_zero, d1, d0)
+
+
+def out_proj(core, context, weight_o, width):
+    tokens, inner = context.shape
+    n_groups = weight_o.shape[1] // (N_C * width)
+    step = GROUPS_PER_STEP
+    out = jax.ShapeDtypeStruct((n_groups, tokens, width), jnp.bfloat16)
+    return pl.pallas_call(
+        out_proj_kernel,
+        out_shape=(out, out),
+        grid_spec=pltpu.PrefetchScalarGridSpec(
+            num_scalar_prefetch=1,
+            grid=(n_groups // step,),
+            in_specs=[
+                pl.BlockSpec((tokens, inner), lambda i, c: (0, 0)),
+                pl.BlockSpec((inner, step * N_C * width), lambda i, c: (0, i)),
+            ],
+            out_specs=[
+                pl.BlockSpec((step, tokens, width), lambda i, c: (i, 0, 0)),
+                pl.BlockSpec((step, tokens, width), lambda i, c: (i, 0, 0)),
+            ],
+        ),
+    )(core, context, weight_o)
 
 
 def on_device(inputs, queries, keys, w_value, w_out):
@@ -17,7 +61,9 @@
     col_width = activ.shape[1]
     n_feat = weight_v.shape[0]
 
-    gathered = lax.all_gather(activ, "ty", axis=0)
+    y_first = lax.axis_index("ty") == 0
+    other = swap(activ, "ty")
+    gathered = jnp.stack([jnp.where(y_first, activ, other), jnp.where(y_first, other, activ)])
     gathered = lax.all_gather(gathered, "tz", axis=0)
     gathered = lax.all_gather(gathered, "tc", axis=0)
     wv = weight_v.reshape(N_Z, N_Y, N_C, col_width, weight_v.shape[1])
@@ -43,15 +89,17 @@
     ).astype(jnp.bfloat16)
     context = context.reshape(length, heads_here * HEAD_SIZE)
 
-    wo = weight_o.reshape(weight_o.shape[0], N_Z, N_Y, N_C, col_width)
-    partial_term = jnp.einsum(
-        "tk,kzycf->czytf", context, wo, preferred_element_type=jnp.float32
-    ).astype(jnp.bfloat16)
-    part = lax.psum_scatter(partial_term, "tc", scatter_dimension=0, tiled=False)
+    core = lax.axis_index("tc").astype(jnp.int32).reshape(1)
+    mine, sib = out_proj(core, context, weight_o, col_width)
+    part = mine.astype(jnp.float32) + swap(sib, "tc").astype(jnp.float32)
+    part = part.astype(jnp.bfloat16).reshape(N_Z, N_Y, length, col_width)
     part = lax.psum_scatter(part, "tz", scatter_dimension=0, tiled=False)
-    part = lax.psum_scatter(part, "ty", scatter_dimension=0, tiled=False)
-    result = (part.astype(jnp.float32) + activ.astype(jnp.float32)).astype(jnp.bfloat16)
-    passed = lax.ppermute(result, "section", [(0, 1), (1, 0)])
+    y_index = lax.axis_index("ty")
+    keep = lax.dynamic_index_in_dim(part, y_index, 0, keepdims=False)
+    send = lax.dynamic_index_in_dim(part, 1 - y_index, 0, keepdims=False)
+    result = keep.astype(jnp.float32) + swap(send, "ty").astype(jnp.float32)
+    result = (result + activ.astype(jnp.float32)).astype(jnp.bfloat16)
+    passed = swap(result, "section")
     return passed[None]
 
 

time: 238 us -> 185 us (0.78)
  waiting for transfers between devices: 170 us -> 136 us
  local copies, waits for them, and re-layouts: 23.1 us -> 4.27 us
  blocking collectives: 11.4 us -> 0 us
  matrix products: 17.6 us -> 8 us
  Pallas kernels: 0 us -> 7.31 us
  starting transfers between devices: 0.84 us -> 7.97 us
  other arithmetic: 1 us -> 7.34 us
    unnamed x6 -> x3, waiting for transfers between devices: 43.3 us -> 0.05 us
    reduce_scatter x1 -> x0, waiting for transfers between devices: 21.7 us -> none  [on_device(): part = lax.psum_scatter(part, 'ty', scatter_dimension=0, tiled=False)]
    another operation x3 -> x2, local copies, waits for them, and re-layouts: 16.6 us -> 1.88 us  [the longest x1 14.7 us: on_device(): wo = weight_o.reshape(weight_o.shape[0], N_Z, N_Y, N_C, col_width)]
    all_gather x1, waiting for transfers between devices: 5.3 us -> 20 us  [on_device(): gathered = lax.all_gather(gathered, 'tc', axis=0)]
    ppermute x1 -> x4, waiting for transfers between devices: 5.89 us -> 19.4 us  [swap(): return lax.ppermute(value, axis, [(0, 1), (1, 0)])]
    all_gather x1 -> x0, blocking collectives: 11.4 us -> none  [on_device(): gathered = lax.all_gather(activ, 'ty', axis=0)]
    dot_general x1 -> x0, matrix products: 9.62 us -> none  [on_device(): jnp.einsum('tk,kzycf->czytf', context, wo, preferred_element_type=jnp.flo...]
    pallas_call x0 -> x1, Pallas kernels: none -> 7.31 us  [out_proj(): pl.pallas_call(out_proj_kernel, out_shape=(out, out), grid_spec=pltpu.Pre...]
  transfers between devices with their start and end apart: 6 -> 7, of which waited for: 6 -> 7; matrix products, arithmetic and copies ran while one was open for 7% -> 1% of each run, Pallas kernels for 0% -> 0%
where the time goes in v2:
time: 185 us; the launch traced here: 184 us
  waiting for transfers between devices  136 us (74%)
  between operations  13.2 us (7%)
  matrix products  8 us (4%)
  starting transfers between devices  7.97 us (4%)
  other arithmetic  7.34 us (4%)
  Pallas kernels  7.31 us (4%)
  local copies, waits for them, and re-layouts  4.27 us (2%)
    reduce_scatter x1, waiting for transfers between devices, on_device(): part = lax.psum_scatter(part, 'tz', scatter_dimension=0, tiled=False)  48.5 us
    all_gather x1, waiting for transfers between devices, on_device(): gathered = lax.all_gather(gathered, 'tz', axis=0)  48 us
    all_gather x1, waiting for transfers between devices, on_device(): gathered = lax.all_gather(gathered, 'tc', axis=0)  20 us
    ppermute x4, waiting for transfers between devices, swap(): return lax.ppermute(value, axis, [(0, 1), (1, 0)])  19.4 us
    ppermute x4, starting transfers between devices, swap(): return lax.ppermute(value, axis, [(0, 1), (1, 0)])  7.89 us
    pallas_call x1, Pallas kernels, out_proj(): pl.pallas_call(out_proj_kernel, out_shape=(out, out), grid_spec=pltpu.Pre...  7.31 us
    dot_general x1, matrix products, on_device(): jnp.einsum('czytf,zycfh->th', gathered, wv, preferred_element_type=jnp.fl...  7.15 us
    convert_element_type x1, other arithmetic, on_device(): part = part.astype(jnp.bfloat16).reshape(N_Z, N_Y, length, col_width)  4.55 us
  transfers between devices with their start and end apart: 7, of which 7 were waited for; matrix products, arithmetic and copies ran while one was open for 1% of the time, Pallas kernels for 0%

profile of v2, /device:TPU:2, one launch (start us, length us, event | category | flops | bytes accessed | tf_op | source)
XLA Modules:
  0.0 184.0 jit_solution(4857236653600892921)
XLA Ops:
  6.5 3.2 %collective-permute-start = (bf16[256,384]{1,0:T(8,128)(2,1)}, bf16[256,384]{1,0:T(8,128)(2,1)S(1)}, u32[]{:S(2)}, u32[]{:S(2)}) collective-permute-start(bf16[256,384]{1,0:T(8,128)(2,1)} %bitcast.37), channel_id=1, source_target_pairs={{0,2},{2,0},{1,3},{3,1},{4,6},{6,4},{5,7},{7,5},{8,10},{10,8},{9,1... | collective-permute-start | bytes 589832 | tf_op jit(solution)/shard_map/ppermute | solution.py:16
  9.7 5.2 %collective-permute-done = bf16[256,384]{1,0:T(8,128)(2,1)S(1)} collective-permute-done((bf16[256,384]{1,0:T(8,128)(2,1)}, bf16[256,384]{1,0:T(8,128)(2,1)S(1)}, u32[]{:S(2)}, u32[]{:S(2)}) %collective-permute-start) | collective-permute-done | bytes 196640 | tf_op jit(solution)/shard_map/ppermute | solution.py:16
  14.9 1.0 select_bitcast_fusion.1
  15.9 0.8 pad_maximum_fusion
  16.7 48.0 %all-gather.5.cloned.1.call-done = bf16[16,256,384]{2,1,0:T(8,128)(2,1)} async-done(((bf16[2,256,384]{2,1,0:T(8,128)(2,1)}), bf16[16,256,384]{2,1,0:T(8,128)(2,1)}) %all-gather.5.cloned.1.call-update) | async-done | bytes 3145744 | tf_op jit(solution)/shard_map/all_gather | solution.py:67
  64.9 0.9 reshape.60
  65.8 0.9 reshape.61
  66.8 0.3 fusion.28
  67.4 20.0 %all-gather.7.cloned.1.call-done = bf16[16,2,256,384]{3,2,1,0:T(8,128)(2,1)} async-done(((bf16[8,2,256,384]{3,2,1,0:T(8,128)(2,1)}), bf16[16,2,256,384]{3,2,1,0:T(8,128)(2,1)}) %all-gather.7.cloned.1.call-update) | async-done | bytes 6291472 | tf_op jit(solution)/shard_map/all_gather | solution.py:68
  87.3 7.1 %fusion.12 = bf16[256,256]{0,1:T(8,128)(2,1)S(1)} fusion(bf16[8,2,2,384,256]{4,3,2,1,0:T(8,128)(2,1)} %bitcast.40, bf16[2,8,2,256,384]{4,3,2,1,0:T(8,128)(2,1)} %bitcast.41), kind=kOutput, calls=%fused_computation.11 | convolution fusion | flops 1610678272 | bytes 12713984 | tf_op jit(solution)/shard_map/czytf,zycfh->th/dot_general | solution.py:70
  94.5 0.3 convolution_convert_fusion
  94.8 0.8 copy.27.ctx_ref
  95.5 7.3 %shard_map.55 = (bf16[16,256,384]{2,1,0:T(8,128)(2,1)}, bf16[16,256,384]{2,1,0:T(8,128)(2,1)}) custom-call(s32[1]{0:T(128)} %bitcast.core_ref, bf16[256,256]{1,0:T(8,128)(2,1)} %copy.27.ctx_ref, bf16[256,12288]{1,0:T(8,128)(2,1)} %bitcast.35), custom_call_target="tpu_custom_call" | custom-call | tf_op jit(solution)/shard_map/pallas_call | solution.py:38
  102.8 0.3 collective-permute-start.1
  103.1 5.6 %collective-permute-done.1 = bf16[16,256,384]{2,1,0:T(8,128)(2,1)S(1)} collective-permute-done((bf16[16,256,384]{2,1,0:T(8,128)(2,1)}, bf16[16,256,384]{2,1,0:T(8,128)(2,1)S(1)}, u32[]{:S(2)}, u32[]{:S(2)}) %collective-permute-start.1) | collective-permute-done | bytes 3145760 | tf_op jit(solution)/shard_map/ppermute | solution.py:16
  108.7 4.6 %add_convert_fusion = bf16[16,256,384]{2,1,0:T(8,128)(2,1)} fusion(bf16[16,256,384]{2,1,0:T(8,128)(2,1)S(1)} %collective-permute-done.1, bf16[16,256,384]{2,1,0:T(8,128)(2,1)} %get-tuple-element.7), kind=kLoop, calls=%fused_computation.4 | loop fusion | flops 6291456 | bytes 9437184 | tf_op jit(solution)/shard_map/convert_element_type | solution.py:95
  113.3 48.5 %reduce-scatter.2.cloned.1.call-done = bf16[1,2,256,384]{3,2,1,0:T(8,128)(2,1)} async-done(((bf16[8,2,256,384]{3,2,1,0:T(8,128)(2,1)}), bf16[1,2,256,384]{3,2,1,0:T(8,128)(2,1)}) %reduce-scatter.2.cloned.1.call-update) | async-done | bytes 393232 | tf_op jit(solution)/shard_map/reduce_scatter | solution.py:96
  161.8 0.9 dynamic-slice_bitcast_fusion
  162.7 3.0 %collective-permute-start.2 = (bf16[256,384]{1,0:T(8,128)(2,1)S(1)}, bf16[256,384]{1,0:T(8,128)(2,1)S(1)}, u32[]{:S(2)}, u32[]{:S(2)}) collective-permute-start(bf16[256,384]{1,0:T(8,128)(2,1)S(1)} %dynamic-slice_bitcast_fusion), channel_id=1, source_target_pairs={{0,2},{2,0},{1,3},{3,1},{4,6},{6,4},{5,7},{7,5},{8,10},{10,8},{9,1... | collective-permute-start | bytes 589832 | tf_op jit(solution)/shard_map/ppermute | solution.py:16
  165.7 4.3 %collective-permute-done.2 = bf16[256,384]{1,0:T(8,128)(2,1)S(1)} collective-permute-done((bf16[256,384]{1,0:T(8,128)(2,1)S(1)}, bf16[256,384]{1,0:T(8,128)(2,1)S(1)}, u32[]{:S(2)}, u32[]{:S(2)}) %collective-permute-start.2) | collective-permute-done | bytes 196640 | tf_op jit(solution)/shard_map/ppermute | solution.py:16
  170.0 1.0 fusion.18
  171.0 1.4 collective-permute-start.3
  172.4 4.3 %collective-permute-done.3 = bf16[256,384]{1,0:T(8,128)(2,1)S(1)} collective-permute-done((bf16[256,384]{1,0:T(8,128)(2,1)S(1)}, bf16[256,384]{1,0:T(8,128)(2,1)S(1)}, u32[]{:S(2)}, u32[]{:S(2)}) %collective-permute-start.3) | collective-permute-done | bytes 196640 | tf_op jit(solution)/shard_map/ppermute | solution.py:16
  176.8 0.7 copy.53
  (10 shorter events, 0.4 us)
Async XLA Ops:
  6.5 58.2 %all-gather.5.cloned.1.call-start = ((), (), s32[]{:S(2)}) async-start(), calls=%async_computation.2 | async-start | bytes 3538944 | tf_op jit(solution)/shard_map/all_gather | solution.py:67
  6.5 8.4 %collective-permute-start = (bf16[256,384]{1,0:T(8,128)(2,1)}, bf16[256,384]{1,0:T(8,128)(2,1)S(1)}, u32[]{:S(2)}, u32[]{:S(2)}) collective-permute-start(bf16[256,384]{1,0:T(8,128)(2,1)} %bitcast.37), channel_id=1, source_target_pairs={{0,2},{2,0},{1,3},{3,1},{4,6},{6,4},{5,7},{7,5},{8,10},{10,8},{9,1... | collective-permute-start | bytes 589832 | tf_op jit(solution)/shard_map/ppermute | solution.py:16
  16.7 70.6 %all-gather.7.cloned.1.call-start = ((), (), s32[]{:S(2)}) async-start(), calls=%async_computation.3 | async-start | bytes 9437184 | tf_op jit(solution)/shard_map/all_gather | solution.py:68
  64.8 97.0 %reduce-scatter.2.cloned.1.call-start = ((), (), s32[]{:S(2)}) async-start(), calls=%async_computation.1 | async-start | bytes 3538944 | tf_op jit(solution)/shard_map/reduce_scatter | solution.py:96
  102.8 5.9 %collective-permute-start.1 = (bf16[16,256,384]{2,1,0:T(8,128)(2,1)}, bf16[16,256,384]{2,1,0:T(8,128)(2,1)S(1)}, u32[]{:S(2)}, u32[]{:S(2)}) collective-permute-start(bf16[16,256,384]{2,1,0:T(8,128)(2,1)} %get-tuple-element.8), channel_id=1, source_target_pairs={{0,1},{1,0},{2,3},{3,2},{4,5},{5,4},{6,7},{7,6},{8,9},{9,8},{10,11... | collective-permute-start | bytes 9437192 | tf_op jit(solution)/shard_map/ppermute | solution.py:16
  108.7 61.3 %copy-start = (bf16[1,256,384]{2,1,0:T(8,128)(2,1)S(1)}, bf16[1,256,384]{2,1,0:T(8,128)(2,1)}, u32[]{:S(2)}) copy-start(bf16[1,256,384]{2,1,0:T(8,128)(2,1)} %param.5) | copy-start | bytes 589828
  162.7 7.3 %collective-permute-start.2 = (bf16[256,384]{1,0:T(8,128)(2,1)S(1)}, bf16[256,384]{1,0:T(8,128)(2,1)S(1)}, u32[]{:S(2)}, u32[]{:S(2)}) collective-permute-start(bf16[256,384]{1,0:T(8,128)(2,1)S(1)} %dynamic-slice_bitcast_fusion), channel_id=1, source_target_pairs={{0,2},{2,0},{1,3},{3,1},{4,6},{6,4},{5,7},{7,5},{8,10},{10,8},{9,1... | collective-permute-start | bytes 589832 | tf_op jit(solution)/shard_map/ppermute | solution.py:16
  171.0 5.8 %collective-permute-start.3 = (bf16[256,384]{1,0:T(8,128)(2,1)S(1)}, bf16[256,384]{1,0:T(8,128)(2,1)S(1)}, u32[]{:S(2)}, u32[]{:S(2)}) collective-permute-start(bf16[256,384]{1,0:T(8,128)(2,1)S(1)} %fusion.18), channel_id=1, source_target_pairs={{0,128},{128,0},{1,129},{129,1},{2,130},{130,2},{3,131},{131,3},{4... | collective-permute-start | bytes 589832 | tf_op jit(solution)/shard_map/ppermute | solution.py:16
Sparse Core Ops, SparseCore 0:
  16.8 47.9 all-gather.4
  66.6 20.7 all-gather.6
  113.4 48.3 reduce-scatter.1

commit v3 on v2

--- a/solution.py
+++ b/solution.py
@@ -53,6 +53,38 @@
     )(core, context, weight_o)
 
 
+def value_proj_kernel(core_ref, f_ref, *refs):
+    w_refs, o_ref = refs[:-1], refs[-1]
+
+    @pl.when(pl.program_id(0) == 0)
+    def _():
+        o_ref[...] = jnp.zeros(o_ref.shape, o_ref.dtype)
+
+    acc = o_ref[...]
+    for k, w_ref in enumerate(w_refs):
+        acc = acc + jnp.dot(f_ref[k], w_ref[...], preferred_element_type=jnp.float32)
+    o_ref[...] = acc
+
+
+def value_proj(core, feats, weight_v):
+    n_groups, tokens, width = feats.shape
+    step = GROUPS_PER_STEP
+    w_specs = [
+        pl.BlockSpec((width, weight_v.shape[1]), lambda i, c, k=k: (N_C * (i * step + k) + c[0], 0))
+        for k in range(step)
+    ]
+    return pl.pallas_call(
+        value_proj_kernel,
+        out_shape=jax.ShapeDtypeStruct((tokens, weight_v.shape[1]), jnp.float32),
+        grid_spec=pltpu.PrefetchScalarGridSpec(
+            num_scalar_prefetch=1,
+            grid=(n_groups // step,),
+            in_specs=[pl.BlockSpec((step, tokens, width), lambda i, c: (i, 0, 0))] + w_specs,
+            out_specs=pl.BlockSpec((tokens, weight_v.shape[1]), lambda i, c: (0, 0)),
+        ),
+    )(core, feats, *([weight_v] * step))
+
+
 def on_device(inputs, queries, keys, w_value, w_out):
     activ = inputs[0]
     weight_v = w_value[0]
@@ -65,11 +97,12 @@
     other = swap(activ, "ty")
     gathered = jnp.stack([jnp.where(y_first, activ, other), jnp.where(y_first, other, activ)])
     gathered = lax.all_gather(gathered, "tz", axis=0)
-    gathered = lax.all_gather(gathered, "tc", axis=0)
-    wv = weight_v.reshape(N_Z, N_Y, N_C, col_width, weight_v.shape[1])
-    values = jnp.einsum(
-        "czytf,zycfh->th", gathered, wv, preferred_element_type=jnp.float32
-    ).astype(jnp.bfloat16)
+    from_sib = swap(gathered, "tc").reshape(N_Z * N_Y, length, col_width)
+    gathered = gathered.reshape(N_Z * N_Y, length, col_width)
+    c_index = lax.axis_index("tc").astype(jnp.int32)
+    values = value_proj(c_index.reshape(1), gathered, weight_v)
+    values = values + value_proj((1 - c_index).reshape(1), from_sib, weight_v)
+    values = values.astype(jnp.bfloat16)
 
     heads_here = weight_v.shape[1] // HEAD_SIZE
     query_rows = queries[0].reshape(length // LEN, LEN, heads_here, HEAD_SIZE)

time: 185 us -> 171 us (0.924)
  waiting for transfers between devices: 136 us -> 113 us
  Pallas kernels: 7.31 us -> 17.3 us
  matrix products: 8 us -> 2.84 us
    all_gather x1 -> x0, waiting for transfers between devices: 20 us -> none  [on_device(): gathered = lax.all_gather(gathered, 'tc', axis=0)]
    pallas_call x0 -> x2, Pallas kernels: none -> 10 us  [value_proj(): pl.pallas_call(value_proj_kernel, out_shape=jax.ShapeDtypeStruct((tokens,...]
    dot_general x1 -> x0, matrix products: 7.15 us -> none  [on_device(): jnp.einsum('czytf,zycfh->th', gathered, wv, preferred_element_type=jnp.fl...]
    reduce_scatter x1, waiting for transfers between devices: 48.5 us -> 45.8 us  [on_device(): part = lax.psum_scatter(part, 'tz', scatter_dimension=0, tiled=False)]
    ppermute x4 -> x5, starting transfers between devices: 7.89 us -> 8.63 us  [swap(): return lax.ppermute(value, axis, [(0, 1), (1, 0)])]
    ppermute x4 -> x5, waiting for transfers between devices: 19.4 us -> 18.8 us  [swap(): return lax.ppermute(value, axis, [(0, 1), (1, 0)])]
  transfers between devices with their start and end apart: 7 -> 7, of which waited for: 7 -> 6; matrix products, arithmetic and copies ran while one was open for 1% -> 2% of each run, Pallas kernels for 0% -> 3%
where the time goes in v3:
time: 171 us; the launch traced here: 169 us
  waiting for transfers between devices  113 us (66%)
  Pallas kernels  17.3 us (10%)
  between operations  13.5 us (8%)
  starting transfers between devices  8.67 us (5%)
  other arithmetic  8.28 us (5%)
  local copies, waits for them, and re-layouts  6.01 us (4%)
  matrix products  2.84 us (2%)
    all_gather x1, waiting for transfers between devices, on_device(): gathered = lax.all_gather(gathered, 'tz', axis=0)  48 us
    reduce_scatter x1, waiting for transfers between devices, on_device(): part = lax.psum_scatter(part, 'tz', scatter_dimension=0, tiled=False)  45.8 us
    ppermute x5, waiting for transfers between devices, swap(): return lax.ppermute(value, axis, [(0, 1), (1, 0)])  18.8 us
    pallas_call x2, Pallas kernels, value_proj(): pl.pallas_call(value_proj_kernel, out_shape=jax.ShapeDtypeStruct((tokens,...  10 us
    ppermute x5, starting transfers between devices, swap(): return lax.ppermute(value, axis, [(0, 1), (1, 0)])  8.63 us
    pallas_call x1, Pallas kernels, out_proj(): pl.pallas_call(out_proj_kernel, out_shape=(out, out), grid_spec=pltpu.Pre...  7.31 us
    convert_element_type x1, other arithmetic, on_device(): part = part.astype(jnp.bfloat16).reshape(N_Z, N_Y, length, col_width)  4.51 us
  transfers between devices with their start and end apart: 7, of which 6 were waited for; matrix products, arithmetic and copies ran while one was open for 2% of the time, Pallas kernels for 3%

profile of v3, /device:TPU:2, one launch (start us, length us, event | category | flops | bytes accessed | tf_op | source)
XLA Modules:
  0.0 169.3 jit_solution(13340334668744853183)
XLA Ops:
  6.5 3.2 %collective-permute-start = (bf16[256,384]{1,0:T(8,128)(2,1)}, bf16[256,384]{1,0:T(8,128)(2,1)S(1)}, u32[]{:S(2)}, u32[]{:S(2)}) collective-permute-start(bf16[256,384]{1,0:T(8,128)(2,1)} %bitcast.41), channel_id=1, source_target_pairs={{0,2},{2,0},{1,3},{3,1},{4,6},{6,4},{5,7},{7,5},{8,10},{10,8},{9,1... | collective-permute-start | bytes 589832 | tf_op jit(solution)/shard_map/ppermute | solution.py:16
  9.7 5.2 %collective-permute-done = bf16[256,384]{1,0:T(8,128)(2,1)S(1)} collective-permute-done((bf16[256,384]{1,0:T(8,128)(2,1)}, bf16[256,384]{1,0:T(8,128)(2,1)S(1)}, u32[]{:S(2)}, u32[]{:S(2)}) %collective-permute-start) | collective-permute-done | bytes 196640 | tf_op jit(solution)/shard_map/ppermute | solution.py:16
  14.9 1.0 select_bitcast_fusion.1
  15.9 0.8 pad_maximum_fusion
  16.7 48.0 %all-gather.3.cloned.1.call-done.f_ref = bf16[16,256,384]{2,1,0:T(8,128)(2,1)} async-done(((bf16[2,256,384]{2,1,0:T(8,128)(2,1)}), bf16[16,256,384]{2,1,0:T(8,128)(2,1)}) %all-gather.3.cloned.1.call-update) | async-done | bytes 3145744 | tf_op jit(solution)/shard_map/all_gather | solution.py:99
  64.8 0.9 reshape.73
  65.7 0.9 reshape.74
  67.0 1.0 fusion.3
  68.1 5.0 %shard_map.55 = f32[256,256]{1,0:T(8,128)} custom-call(s32[1]{0:T(128)} %bitcast.core_ref, bf16[16,256,384]{2,1,0:T(8,128)(2,1)} %all-gather.3.cloned.1.call-done.f_ref, bf16[12288,256]{1,0:T(8,128)(2,1)} %bitcast.29, bf16[12288,256]{1,0:T(8,128)(2,1)} %bitcast.30, bf16[12288,256]{1,0:T(8,128)(2,1)} %bitcast.31, bf16[12288,256]{1,0:T(8,128)(2,1)} %bitcast.32), custom_call_target="tpu_custom_call" | custom-call | tf_op jit(solution)/shard_map/pallas_call | solution.py:76
  73.1 1.6 copy-done
  74.7 5.0 %shard_map.56 = f32[256,256]{1,0:T(8,128)} custom-call(s32[1]{0:T(128)} %bitcast.5.core_ref, bf16[16,256,384]{2,1,0:T(8,128)(2,1)} %bitcast.40, bf16[12288,256]{1,0:T(8,128)(2,1)} %bitcast.33, bf16[12288,256]{1,0:T(8,128)(2,1)} %bitcast.34, bf16[12288,256]{1,0:T(8,128)(2,1)} %bitcast.35, bf16[12288,256]{1,0:T(8,128)(2,1)} %bitcast.36), custom_call_target="tpu_custom_call" | custom-call | tf_op jit(solution)/shard_map/pallas_call | solution.py:76
  79.8 1.0 add_convert_fusion.1
  80.8 1.5 convolution_convert_fusion
  82.3 0.8 copy.18.ctx_ref
  83.1 7.3 %shard_map.57 = (bf16[16,256,384]{2,1,0:T(8,128)(2,1)}, bf16[16,256,384]{2,1,0:T(8,128)(2,1)}) custom-call(s32[1]{0:T(128)} %bitcast.core_ref, bf16[256,256]{1,0:T(8,128)(2,1)} %copy.18.ctx_ref, bf16[256,12288]{1,0:T(8,128)(2,1)} %bitcast.38), custom_call_target="tpu_custom_call" | custom-call | tf_op jit(solution)/shard_map/pallas_call | solution.py:38
  90.9 5.5 %collective-permute-done.2 = bf16[16,256,384]{2,1,0:T(8,128)(2,1)S(1)} collective-permute-done((bf16[16,256,384]{2,1,0:T(8,128)(2,1)}, bf16[16,256,384]{2,1,0:T(8,128)(2,1)S(1)}, u32[]{:S(2)}, u32[]{:S(2)}) %collective-permute-start.2) | collective-permute-done | bytes 3145760 | tf_op jit(solution)/shard_map/ppermute | solution.py:16
  96.4 4.5 %add_convert_fusion = bf16[16,256,384]{2,1,0:T(8,128)(2,1)} fusion(bf16[16,256,384]{2,1,0:T(8,128)(2,1)S(1)} %collective-permute-done.2, bf16[16,256,384]{2,1,0:T(8,128)(2,1)} %get-tuple-element.7), kind=kLoop, calls=%fused_computation.1 | loop fusion | flops 6291456 | bytes 9437184 | tf_op jit(solution)/shard_map/convert_element_type | solution.py:128
  101.0 45.8 %reduce-scatter.2.cloned.1.call-done = bf16[1,2,256,384]{3,2,1,0:T(8,128)(2,1)} async-done(((bf16[8,2,256,384]{3,2,1,0:T(8,128)(2,1)}), bf16[1,2,256,384]{3,2,1,0:T(8,128)(2,1)}) %reduce-scatter.2.cloned.1.call-update) | async-done | bytes 393232 | tf_op jit(solution)/shard_map/reduce_scatter | solution.py:129
  146.7 0.9 dynamic-slice_bitcast_fusion
  147.7 3.2 %collective-permute-start.3 = (bf16[256,384]{1,0:T(8,128)(2,1)S(1)}, bf16[256,384]{1,0:T(8,128)(2,1)S(1)}, u32[]{:S(2)}, u32[]{:S(2)}) collective-permute-start(bf16[256,384]{1,0:T(8,128)(2,1)S(1)} %dynamic-slice_bitcast_fusion), channel_id=1, source_target_pairs={{0,2},{2,0},{1,3},{3,1},{4,6},{6,4},{5,7},{7,5},{8,10},{10,8},{9,1... | collective-permute-start | bytes 589832 | tf_op jit(solution)/shard_map/ppermute | solution.py:16
  150.9 4.1 %collective-permute-done.3 = bf16[256,384]{1,0:T(8,128)(2,1)S(1)} collective-permute-done((bf16[256,384]{1,0:T(8,128)(2,1)S(1)}, bf16[256,384]{1,0:T(8,128)(2,1)S(1)}, u32[]{:S(2)}, u32[]{:S(2)}) %collective-permute-start.3) | collective-permute-done | bytes 196640 | tf_op jit(solution)/shard_map/ppermute | solution.py:16
  155.0 1.0 fusion.5
  156.0 1.7 %collective-permute-start.4 = (bf16[256,384]{1,0:T(8,128)(2,1)S(1)}, bf16[256,384]{1,0:T(8,128)(2,1)S(1)}, u32[]{:S(2)}, u32[]{:S(2)}) collective-permute-start(bf16[256,384]{1,0:T(8,128)(2,1)S(1)} %fusion.5), channel_id=1, source_target_pairs={{0,128},{128,0},{1,129},{129,1},{2,130},{130,2},{3,131},{131,3},{4... | collective-permute-start | bytes 589832 | tf_op jit(solution)/shard_map/ppermute | solution.py:16
  157.7 4.0 %collective-permute-done.4 = bf16[256,384]{1,0:T(8,128)(2,1)S(1)} collective-permute-done((bf16[256,384]{1,0:T(8,128)(2,1)S(1)}, bf16[256,384]{1,0:T(8,128)(2,1)S(1)}, u32[]{:S(2)}, u32[]{:S(2)}) %collective-permute-start.4) | collective-permute-done | bytes 196640 | tf_op jit(solution)/shard_map/ppermute | solution.py:16
  (16 shorter events, 1.7 us)
Async XLA Ops:
  6.5 58.2 %all-gather.3.cloned.1.call-start = ((), (), s32[]{:S(2)}) async-start(), calls=%async_computation.2 | async-start | bytes 3538944 | tf_op jit(solution)/shard_map/all_gather | solution.py:99
  6.5 8.4 %collective-permute-start = (bf16[256,384]{1,0:T(8,128)(2,1)}, bf16[256,384]{1,0:T(8,128)(2,1)S(1)}, u32[]{:S(2)}, u32[]{:S(2)}) collective-permute-start(bf16[256,384]{1,0:T(8,128)(2,1)} %bitcast.41), channel_id=1, source_target_pairs={{0,2},{2,0},{1,3},{3,1},{4,6},{6,4},{5,7},{7,5},{8,10},{10,8},{9,1... | collective-permute-start | bytes 589832 | tf_op jit(solution)/shard_map/ppermute | solution.py:16
  16.7 130.0 %reduce-scatter.2.cloned.1.call-start = ((), (), s32[]{:S(2)}) async-start(), calls=%async_computation.1 | async-start | bytes 3538944 | tf_op jit(solution)/shard_map/reduce_scatter | solution.py:129
  64.8 8.3 %collective-permute-start.1 = (bf16[8,2,256,384]{3,2,1,0:T(8,128)(2,1)}, bf16[8,2,256,384]{3,2,1,0:T(8,128)(2,1)S(1)}, u32[]{:S(2)}, u32[]{:S(2)}) collective-permute-start(bf16[8,2,256,384]{3,2,1,0:T(8,128)(2,1)} %bitcast.39), channel_id=1, source_target_pairs={{0,1},{1,0},{2,3},{3,2},{4,5},{5,4},{6,7},{7,6},{8,9},{9,8},{10,11... | collective-permute-start | bytes 9437192 | tf_op jit(solution)/shard_map/ppermute | solution.py:16
  73.1 1.6 copy-start
  74.7 5.0 %copy-start.1 = (f32[256,256]{1,0:T(8,128)S(1)}, f32[256,256]{1,0:T(8,128)}, u32[]{:S(2)}) copy-start(f32[256,256]{1,0:T(8,128)} %shard_map.55) | copy-start | bytes 786436
  90.4 6.0 %collective-permute-start.2 = (bf16[16,256,384]{2,1,0:T(8,128)(2,1)}, bf16[16,256,384]{2,1,0:T(8,128)(2,1)S(1)}, u32[]{:S(2)}, u32[]{:S(2)}) collective-permute-start(bf16[16,256,384]{2,1,0:T(8,128)(2,1)} %get-tuple-element.8), channel_id=1, source_target_pairs={{0,1},{1,0},{2,3},{3,2},{4,5},{5,4},{6,7},{7,6},{8,9},{9,8},{10,11... | collective-permute-start | bytes 9437192 | tf_op jit(solution)/shard_map/ppermute | solution.py:16
  100.9 54.1 %copy-start.2 = (bf16[1,256,384]{2,1,0:T(8,128)(2,1)S(1)}, bf16[1,256,384]{2,1,0:T(8,128)(2,1)}, u32[]{:S(2)}) copy-start(bf16[1,256,384]{2,1,0:T(8,128)(2,1)} %param.5) | copy-start | bytes 589828
  147.7 7.3 %collective-permute-start.3 = (bf16[256,384]{1,0:T(8,128)(2,1)S(1)}, bf16[256,384]{1,0:T(8,128)(2,1)S(1)}, u32[]{:S(2)}, u32[]{:S(2)}) collective-permute-start(bf16[256,384]{1,0:T(8,128)(2,1)S(1)} %dynamic-slice_bitcast_fusion), channel_id=1, source_target_pairs={{0,2},{2,0},{1,3},{3,1},{4,6},{6,4},{5,7},{7,5},{8,10},{10,8},{9,1... | collective-permute-start | bytes 589832 | tf_op jit(solution)/shard_map/ppermute | solution.py:16
  156.0 5.8 %collective-permute-start.4 = (bf16[256,384]{1,0:T(8,128)(2,1)S(1)}, bf16[256,384]{1,0:T(8,128)(2,1)S(1)}, u32[]{:S(2)}, u32[]{:S(2)}) collective-permute-start(bf16[256,384]{1,0:T(8,128)(2,1)S(1)} %fusion.5), channel_id=1, source_target_pairs={{0,128},{128,0},{1,129},{129,1},{2,130},{130,2},{3,131},{131,3},{4... | collective-permute-start | bytes 589832 | tf_op jit(solution)/shard_map/ppermute | solution.py:16
Sparse Core Ops, SparseCore 0:
  16.8 47.9 all-gather.2
  101.1 45.5 reduce-scatter.1

commit v4 on v3

--- a/solution.py
+++ b/solution.py
@@ -85,55 +85,68 @@
     )(core, feats, *([weight_v] * step))
 
 
+def attend(query_rows, key_rows, value_rows, offset):
+    scores = jnp.einsum(
+        "qhd,khd->hqk", query_rows, key_rows, preferred_element_type=jnp.float32
+    ) / jnp.sqrt(jnp.float32(HEAD_SIZE))
+    shape = (query_rows.shape[0], key_rows.shape[0])
+    rows = lax.broadcasted_iota(jnp.int32, shape, 0) + offset
+    cols = lax.broadcasted_iota(jnp.int32, shape, 1)
+    scores = jnp.where((cols <= rows)[None], scores, jnp.float32(-1e30))
+    top = jnp.max(scores, axis=-1, keepdims=True)
+    expo = jnp.exp(scores - top)
+    probs = (expo / jnp.sum(expo, axis=-1, keepdims=True)).astype(jnp.bfloat16)
+    context = jnp.einsum("hqk,khd->qhd", probs, value_rows, preferred_element_type=jnp.float32)
+    return context.astype(jnp.bfloat16).reshape(query_rows.shape[0], -1)
+
+
 def on_device(inputs, queries, keys, w_value, w_out):
     activ = inputs[0]
     weight_v = w_value[0]
     weight_o = w_out[0]
     length = activ.shape[0]
     col_width = activ.shape[1]
-    n_feat = weight_v.shape[0]
+    heads_here = weight_v.shape[1] // HEAD_SIZE
+    half = LEN // 2
+    c_index = lax.axis_index("tc").astype(jnp.int32)
+    y_index = lax.axis_index("ty")
 
-    y_first = lax.axis_index("ty") == 0
+    y_first = y_index == 0
     other = swap(activ, "ty")
     gathered = jnp.stack([jnp.where(y_first, activ, other), jnp.where(y_first, other, activ)])
-    gathered = lax.all_gather(gathered, "tz", axis=0)
-    from_sib = swap(gathered, "tc").reshape(N_Z * N_Y, length, col_width)
-    gathered = gathered.reshape(N_Z * N_Y, length, col_width)
-    c_index = lax.axis_index("tc").astype(jnp.int32)
-    values = value_proj(c_index.reshape(1), gathered, weight_v)
-    values = values + value_proj((1 - c_index).reshape(1), from_sib, weight_v)
-    values = values.astype(jnp.bfloat16)
+    query_rows = queries[0].reshape(length, heads_here, HEAD_SIZE)
+    key_rows = keys[0].reshape(length, heads_here, HEAD_SIZE)
 
-    heads_here = weight_v.shape[1] // HEAD_SIZE
-    query_rows = queries[0].reshape(length // LEN, LEN, heads_here, HEAD_SIZE)
-    key_rows = keys[0].reshape(length // LEN, LEN, heads_here, HEAD_SIZE)
-    value_rows = values.reshape(length // LEN, LEN, heads_here, HEAD_SIZE)
-    scores = jnp.einsum(
-        "bqhd,bkhd->bhqk", query_rows, key_rows, preferred_element_type=jnp.float32
-    ) / jnp.sqrt(jnp.float32(HEAD_SIZE))
-    rows = lax.broadcasted_iota(jnp.int32, (LEN, LEN), 0)
-    cols = lax.broadcasted_iota(jnp.int32, (LEN, LEN), 1)
-    scores = jnp.where((cols <= rows)[None, None], scores, jnp.float32(-1e30))
-    top = jnp.max(scores, axis=-1, keepdims=True)
-    expo = jnp.exp(scores - top)
-    probs = (expo / jnp.sum(expo, axis=-1, keepdims=True)).astype(jnp.bfloat16)
-    context = jnp.einsum(
-        "bhqk,bkhd->bqhd", probs, value_rows, preferred_element_type=jnp.float32
-    ).astype(jnp.bfloat16)
-    context = context.reshape(length, heads_here * HEAD_SIZE)
+    def finish(part, lo):
+        part = lax.psum_scatter(part, "tz", scatter_dimension=0, tiled=False)
+        keep = lax.dynamic_index_in_dim(part, y_index, 0, keepdims=False)
+        send = lax.dynamic_index_in_dim(part, 1 - y_index, 0, keepdims=False)
+        result = keep.astype(jnp.float32) + swap(send, "ty").astype(jnp.float32)
+        result = (result + activ[lo:lo + half].astype(jnp.float32)).astype(jnp.bfloat16)
+        return swap(result, "section")
 
-    core = lax.axis_index("tc").astype(jnp.int32).reshape(1)
-    mine, sib = out_proj(core, context, weight_o, col_width)
-    part = mine.astype(jnp.float32) + swap(sib, "tc").astype(jnp.float32)
-    part = part.astype(jnp.bfloat16).reshape(N_Z, N_Y, length, col_width)
-    part = lax.psum_scatter(part, "tz", scatter_dimension=0, tiled=False)
-    y_index = lax.axis_index("ty")
-    keep = lax.dynamic_index_in_dim(part, y_index, 0, keepdims=False)
-    send = lax.dynamic_index_in_dim(part, 1 - y_index, 0, keepdims=False)
-    result = keep.astype(jnp.float32) + swap(send, "ty").astype(jnp.float32)
-    result = (result + activ.astype(jnp.float32)).astype(jnp.bfloat16)
-    passed = swap(result, "section")
-    return passed[None]
+    value_parts = []
+    results = []
+    pending = None
+    for lo in range(0, length, half):
+        feats = lax.all_gather(gathered[:, lo:lo + half], "tz", axis=0)
+        if pending is not None:
+            feats, part = lax.optimization_barrier((feats, pending[0]))
+            results.append(finish(part, pending[1]))
+        from_sib = swap(feats, "tc").reshape(N_Z * N_Y, half, col_width)
+        feats = feats.reshape(N_Z * N_Y, half, col_width)
+        values = value_proj(c_index.reshape(1), feats, weight_v)
+        values = values + value_proj((1 - c_index).reshape(1), from_sib, weight_v)
+        value_parts.append(values.astype(jnp.bfloat16).reshape(half, heads_here, HEAD_SIZE))
+        seen = lo + half
+        value_rows = jnp.concatenate(value_parts, axis=0) if len(value_parts) > 1 else value_parts[0]
+        context = attend(query_rows[lo:seen], key_rows[:seen], value_rows, lo)
+
+        mine, sib = out_proj(c_index.reshape(1), context, weight_o, col_width)
+        part = mine.astype(jnp.float32) + swap(sib, "tc").astype(jnp.float32)
+        pending = (part.astype(jnp.bfloat16).reshape(N_Z, N_Y, half, col_width), lo)
+    results.append(finish(*pending))
+    return jnp.concatenate(results, axis=0)[None]
 
 
 def solution(mesh):

time: 171 us -> 206 us (1.20)
  waiting for transfers between devices: 113 us -> 131 us
  Pallas kernels: 17.3 us -> 28.8 us
  starting transfers between devices: 8.67 us -> 12.7 us
  other arithmetic: 8.28 us -> 11.6 us
    all_gather x1 -> x2, waiting for transfers between devices: 48 us -> 57.5 us  [on_device(): feats = lax.all_gather(gathered[:, lo:lo + half], 'tz', axis=0)]
    reduce_scatter x1 -> x2, waiting for transfers between devices: 45.8 us -> 53.8 us  [finish(): part = lax.psum_scatter(part, 'tz', scatter_dimension=0, tiled=False)]
    pallas_call x2 -> x4, Pallas kernels: 10 us -> 17.3 us  [value_proj(): pl.pallas_call(value_proj_kernel, out_shape=jax.ShapeDtypeStruct((tokens,...]
    pallas_call x1 -> x2, Pallas kernels: 7.31 us -> 11.5 us  [out_proj(): pl.pallas_call(out_proj_kernel, out_shape=(out, out), grid_spec=pltpu.Pre...]
    ppermute x5 -> x9, starting transfers between devices: 8.63 us -> 12.5 us  [swap(): return lax.ppermute(value, axis, [(0, 1), (1, 0)])]
    convert_element_type x3 -> x5, other arithmetic: 6.49 us -> 8.93 us  [the longest x2 6.07 us: on_device(): pending = (part.astype(jnp.bfloat16).reshape(N_Z, N_Y, half, col_width), lo)]
    ppermute x5 -> x9, waiting for transfers between devices: 18.8 us -> 19.4 us  [swap(): return lax.ppermute(value, axis, [(0, 1), (1, 0)])]
  transfers between devices with their start and end apart: 7 -> 13, of which waited for: 6 -> 10; matrix products, arithmetic and copies ran while one was open for 2% -> 7% of each run, Pallas kernels for 3% -> 14%
where the time goes in v4:
time: 206 us; the launch traced here: 205 us
  waiting for transfers between devices  131 us (64%)
  Pallas kernels  28.8 us (14%)
  between operations  13.3 us (6%)
  starting transfers between devices  12.7 us (6%)
  other arithmetic  11.6 us (6%)
  local copies, waits for them, and re-layouts  6.23 us (3%)
    all_gather x2, waiting for transfers between devices, on_device(): feats = lax.all_gather(gathered[:, lo:lo + half], 'tz', axis=0)  57.5 us
    reduce_scatter x2, waiting for transfers between devices, finish(): part = lax.psum_scatter(part, 'tz', scatter_dimension=0, tiled=False)  53.8 us
    ppermute x9, waiting for transfers between devices, swap(): return lax.ppermute(value, axis, [(0, 1), (1, 0)])  19.4 us
    pallas_call x4, Pallas kernels, value_proj(): pl.pallas_call(value_proj_kernel, out_shape=jax.ShapeDtypeStruct((tokens,...  17.3 us
    ppermute x9, starting transfers between devices, swap(): return lax.ppermute(value, axis, [(0, 1), (1, 0)])  12.5 us
    pallas_call x2, Pallas kernels, out_proj(): pl.pallas_call(out_proj_kernel, out_shape=(out, out), grid_spec=pltpu.Pre...  11.5 us
    convert_element_type x2, other arithmetic, on_device(): pending = (part.astype(jnp.bfloat16).reshape(N_Z, N_Y, half, col_width), lo)  6.07 us
  transfers between devices with their start and end apart: 13, of which 10 were waited for; matrix products, arithmetic and copies ran while one was open for 7% of the time, Pallas kernels for 14%

profile of v4, /device:TPU:2, one launch (start us, length us, event | category | flops | bytes accessed | tf_op | source)
XLA Modules:
  0.0 204.9 jit_solution(10591940059457483560)
XLA Ops:
  6.5 3.2 %collective-permute-start = (bf16[256,384]{1,0:T(8,128)(2,1)}, bf16[256,384]{1,0:T(8,128)(2,1)S(1)}, u32[]{:S(2)}, u32[]{:S(2)}) collective-permute-start(bf16[256,384]{1,0:T(8,128)(2,1)} %bitcast.79), channel_id=1, source_target_pairs={{0,2},{2,0},{1,3},{3,1},{4,6},{6,4},{5,7},{7,5},{8,10},{10,8},{9,1... | collective-permute-start | bytes 589832 | tf_op jit(solution)/shard_map/ppermute | solution.py:16
  9.7 5.2 %collective-permute-done = bf16[256,384]{1,0:T(8,128)(2,1)S(1)} collective-permute-done((bf16[256,384]{1,0:T(8,128)(2,1)}, bf16[256,384]{1,0:T(8,128)(2,1)S(1)}, u32[]{:S(2)}, u32[]{:S(2)}) %collective-permute-start) | collective-permute-done | bytes 196640 | tf_op jit(solution)/shard_map/ppermute | solution.py:16
  16.7 42.6 %all-gather.7.cloned.1.call-done.f_ref = bf16[16,128,384]{2,1,0:T(8,128)(2,1)} async-done(((bf16[2,128,384]{2,1,0:T(8,128)(2,1)}), bf16[16,128,384]{2,1,0:T(8,128)(2,1)}) %all-gather.7.cloned.1.call-update) | async-done | bytes 1572880 | tf_op jit(solution)/shard_map/all_gather | solution.py:132
  60.0 4.3 %shard_map.55 = f32[128,256]{1,0:T(8,128)} custom-call(s32[1]{0:T(128)} %bitcast.4.core_ref, bf16[16,128,384]{2,1,0:T(8,128)(2,1)} %all-gather.7.cloned.1.call-done.f_ref, bf16[12288,256]{1,0:T(8,128)(2,1)} %bitcast.55, bf16[12288,256]{1,0:T(8,128)(2,1)} %bitcast.56, bf16[12288,256]{1,0:T(8,128)(2,1)} %bitcast.57, bf16[12288,256]{1,0:T(8,128)(2,1)} %bitcast.58), custom_call_target="tpu_custom_call" | custom-call | tf_op jit(solution)/shard_map/pallas_call | solution.py:76
  64.3 1.2 copy-done
  65.5 4.3 %shard_map.56 = f32[128,256]{1,0:T(8,128)} custom-call(s32[1]{0:T(128)} %bitcast.6.core_ref, bf16[16,128,384]{2,1,0:T(8,128)(2,1)} %bitcast.77, bf16[12288,256]{1,0:T(8,128)(2,1)} %bitcast.59, bf16[12288,256]{1,0:T(8,128)(2,1)} %bitcast.60, bf16[12288,256]{1,0:T(8,128)(2,1)} %bitcast.61, bf16[12288,256]{1,0:T(8,128)(2,1)} %bitcast.62), custom_call_target="tpu_custom_call" | custom-call | tf_op jit(solution)/shard_map/pallas_call | solution.py:76
  71.8 5.8 %shard_map.57 = (bf16[16,128,384]{2,1,0:T(8,128)(2,1)}, bf16[16,128,384]{2,1,0:T(8,128)(2,1)}) custom-call(s32[1]{0:T(128)} %bitcast.4.core_ref, bf16[128,256]{1,0:T(8,128)(2,1)} %copy.43.ctx_ref, bf16[256,12288]{1,0:T(8,128)(2,1)} %bitcast.71), custom_call_target="tpu_custom_call" | custom-call | tf_op jit(solution)/shard_map/pallas_call | solution.py:38
  78.1 3.2 %collective-permute-done.2 = bf16[16,128,384]{2,1,0:T(8,128)(2,1)S(1)} collective-permute-done((bf16[16,128,384]{2,1,0:T(8,128)(2,1)}, bf16[16,128,384]{2,1,0:T(8,128)(2,1)S(1)}, u32[]{:S(2)}, u32[]{:S(2)}) %collective-permute-start.2) | collective-permute-done | bytes 1572896 | tf_op jit(solution)/shard_map/ppermute | solution.py:16
  81.3 3.0 %add_convert_fusion.1 = bf16[16,128,384]{2,1,0:T(8,128)(2,1)} fusion(bf16[16,128,384]{2,1,0:T(8,128)(2,1)S(1)} %collective-permute-done.2, bf16[16,128,384]{2,1,0:T(8,128)(2,1)} %get-tuple-element.11), kind=kLoop, calls=%fused_computation.3 | loop fusion | flops 3145728 | bytes 4718592 | tf_op jit(solution)/shard_map/convert_element_type | solution.py:147
  84.4 14.9 %all-gather.5.cloned.1.call-done = bf16[16,128,384]{2,1,0:T(8,128)(2,1)} async-done(((bf16[2,128,384]{2,1,0:T(8,128)(2,1)}), bf16[16,128,384]{2,1,0:T(8,128)(2,1)}) %all-gather.5.cloned.1.call-update) | async-done | bytes 1572880 | tf_op jit(solution)/shard_map/all_gather | solution.py:132
  100.3 4.3 %shard_map.58 = f32[128,256]{1,0:T(8,128)} custom-call(s32[1]{0:T(128)} %bitcast.4.core_ref, bf16[16,128,384]{2,1,0:T(8,128)(2,1)} %all-gather.5.cloned.1.call-done, bf16[12288,256]{1,0:T(8,128)(2,1)} %bitcast.63, bf16[12288,256]{1,0:T(8,128)(2,1)} %bitcast.64, bf16[12288,256]{1,0:T(8,128)(2,1)} %bitcast.65, bf16[12288,256]{1,0:T(8,128)(2,1)} %bitcast.66), custom_call_target="tpu_custom_call" | custom-call | tf_op jit(solution)/shard_map/pallas_call | solution.py:76
  104.7 1.1 copy-done.1
  105.8 4.3 %shard_map.59 = f32[128,256]{1,0:T(8,128)} custom-call(s32[1]{0:T(128)} %bitcast.6.core_ref, bf16[16,128,384]{2,1,0:T(8,128)(2,1)} %bitcast.78, bf16[12288,256]{1,0:T(8,128)(2,1)} %bitcast.67, bf16[12288,256]{1,0:T(8,128)(2,1)} %bitcast.68, bf16[12288,256]{1,0:T(8,128)(2,1)} %bitcast.69, bf16[12288,256]{1,0:T(8,128)(2,1)} %bitcast.70), custom_call_target="tpu_custom_call" | custom-call | tf_op jit(solution)/shard_map/pallas_call | solution.py:76
  112.5 5.7 %shard_map.60 = (bf16[16,128,384]{2,1,0:T(8,128)(2,1)}, bf16[16,128,384]{2,1,0:T(8,128)(2,1)}) custom-call(s32[1]{0:T(128)} %bitcast.4.core_ref, bf16[128,256]{1,0:T(8,128)(2,1)} %copy.45.ctx_ref, bf16[256,12288]{1,0:T(8,128)(2,1)} %bitcast.72), custom_call_target="tpu_custom_call" | custom-call | tf_op jit(solution)/shard_map/pallas_call | solution.py:38
  118.8 3.2 %collective-permute-done.6 = bf16[16,128,384]{2,1,0:T(8,128)(2,1)S(1)} collective-permute-done((bf16[16,128,384]{2,1,0:T(8,128)(2,1)}, bf16[16,128,384]{2,1,0:T(8,128)(2,1)S(1)}, u32[]{:S(2)}, u32[]{:S(2)}) %collective-permute-start.6) | collective-permute-done | bytes 1572896 | tf_op jit(solution)/shard_map/ppermute | solution.py:16
  122.0 3.0 %add_convert_fusion = bf16[16,128,384]{2,1,0:T(8,128)(2,1)} fusion(bf16[16,128,384]{2,1,0:T(8,128)(2,1)S(1)} %collective-permute-done.6, bf16[16,128,384]{2,1,0:T(8,128)(2,1)} %get-tuple-element.15), kind=kLoop, calls=%fused_computation.2 | loop fusion | flops 3145728 | bytes 4718592 | tf_op jit(solution)/shard_map/convert_element_type | solution.py:147
  125.1 16.0 %reduce-scatter.3.cloned.1.call-done = bf16[1,2,128,384]{3,2,1,0:T(8,128)(2,1)} async-done(((bf16[8,2,128,384]{3,2,1,0:T(8,128)(2,1)}), bf16[1,2,128,384]{3,2,1,0:T(8,128)(2,1)}) %reduce-scatter.3.cloned.1.call-update) | async-done | bytes 196624 | tf_op jit(solution)/shard_map/reduce_scatter | solution.py:121
  142.0 3.1 %collective-permute-start.3 = (bf16[128,384]{1,0:T(8,128)(2,1)S(1)}, bf16[128,384]{1,0:T(8,128)(2,1)S(1)}, u32[]{:S(2)}, u32[]{:S(2)}) collective-permute-start(bf16[128,384]{1,0:T(8,128)(2,1)S(1)} %dynamic-slice_bitcast_fusion.1), channel_id=1, source_target_pairs={{0,2},{2,0},{1,3},{3,1},{4,6},{6,4},{5,7},{7,5},{8,10},{10,8},{9,1... | collective-permute-start | bytes 294920 | tf_op jit(solution)/shard_map/ppermute | solution.py:16
  145.1 37.7 %reduce-scatter.5.cloned.1.call-done = bf16[1,2,128,384]{3,2,1,0:T(8,128)(2,1)} async-done(((bf16[8,2,128,384]{3,2,1,0:T(8,128)(2,1)}), bf16[1,2,128,384]{3,2,1,0:T(8,128)(2,1)}) %reduce-scatter.5.cloned.1.call-update) | async-done | bytes 196624 | tf_op jit(solution)/shard_map/reduce_scatter | solution.py:121
  183.8 3.1 %collective-permute-start.7 = (bf16[128,384]{1,0:T(8,128)(2,1)S(1)}, bf16[128,384]{1,0:T(8,128)(2,1)S(1)}, u32[]{:S(2)}, u32[]{:S(2)}) collective-permute-start(bf16[128,384]{1,0:T(8,128)(2,1)S(1)} %dynamic-slice_bitcast_fusion), channel_id=1, source_target_pairs={{0,2},{2,0},{1,3},{3,1},{4,6},{6,4},{5,7},{7,5},{8,10},{10,8},{9,1... | collective-permute-start | bytes 294920 | tf_op jit(solution)/shard_map/ppermute | solution.py:16
  186.8 3.2 %collective-permute-done.7 = bf16[128,384]{1,0:T(8,128)(2,1)S(1)} collective-permute-done((bf16[128,384]{1,0:T(8,128)(2,1)S(1)}, bf16[128,384]{1,0:T(8,128)(2,1)S(1)}, u32[]{:S(2)}, u32[]{:S(2)}) %collective-permute-start.7) | collective-permute-done | bytes 98336 | tf_op jit(solution)/shard_map/ppermute | solution.py:16
  191.0 2.0 collective-permute-start.4
  193.2 2.6 %collective-permute-done.4 = bf16[128,384]{1,0:T(8,128)(2,1)S(1)} collective-permute-done((bf16[128,384]{1,0:T(8,128)(2,1)S(1)}, bf16[128,384]{1,0:T(8,128)(2,1)S(1)}, u32[]{:S(2)}, u32[]{:S(2)}) %collective-permute-start.4) | collective-permute-done | bytes 98336 | tf_op jit(solution)/shard_map/ppermute | solution.py:16
  195.7 1.9 collective-permute-done.8
  (56 shorter events, 12.4 us)
Async XLA Ops:
  6.5 52.8 %copy-start.6 = (bf16[1,256,256]{2,1,0:T(8,128)(2,1)S(1)}, bf16[1,256,256]{2,1,0:T(8,128)(2,1)}, u32[]{:S(2)}) copy-start(bf16[1,256,256]{2,1,0:T(8,128)(2,1)} %param.6) | copy-start | bytes 393220
  6.5 53.0 %slice-start = ((bf16[1,256,256]{2,1,0:T(8,128)(2,1)}), bf16[1,128,256]{2,1,0:T(8,128)(2,1)S(1)}, s32[]{:S(2)}) async-start(bf16[1,256,256]{2,1,0:T(8,128)(2,1)} %param.7), calls=%async_computation.6 | async-start | bytes 131072 | tf_op jit(solution)/shard_map/slice | solution.py:143
  6.5 52.8 %all-gather.7.cloned.1.call-start = ((), (), s32[]{:S(2)}) async-start(), calls=%async_computation.5 | async-start | bytes 1769472 | tf_op jit(solution)/shard_map/all_gather | solution.py:132
  6.5 8.4 %collective-permute-start = (bf16[256,384]{1,0:T(8,128)(2,1)}, bf16[256,384]{1,0:T(8,128)(2,1)S(1)}, u32[]{:S(2)}, u32[]{:S(2)}) collective-permute-start(bf16[256,384]{1,0:T(8,128)(2,1)} %bitcast.79), channel_id=1, source_target_pairs={{0,2},{2,0},{1,3},{3,1},{4,6},{6,4},{5,7},{7,5},{8,10},{10,8},{9,1... | collective-permute-start | bytes 589832 | tf_op jit(solution)/shard_map/ppermute | solution.py:16
  16.7 82.6 %all-gather.5.cloned.1.call-start = ((), (), s32[]{:S(2)}) async-start(), calls=%async_computation.4 | async-start | bytes 1769472 | tf_op jit(solution)/shard_map/all_gather | solution.py:132
  59.3 5.0 %collective-permute-start.1 = (bf16[8,2,128,384]{3,2,1,0:T(8,128)(2,1)}, bf16[8,2,128,384]{3,2,1,0:T(8,128)(2,1)S(1)}, u32[]{:S(2)}, u32[]{:S(2)}) collective-permute-start(bf16[8,2,128,384]{3,2,1,0:T(8,128)(2,1)} %bitcast.76), channel_id=1, source_target_pairs={{0,1},{1,0},{2,3},{3,2},{4,5},{5,4},{6,7},{7,6},{8,9},{9,8},{10,11... | collective-permute-start | bytes 4718600 | tf_op jit(solution)/shard_map/ppermute | solution.py:16
  59.4 81.7 %reduce-scatter.3.cloned.1.call-start = ((), (), s32[]{:S(2)}) async-start(), calls=%async_computation.2 | async-start | bytes 1769472 | tf_op jit(solution)/shard_map/reduce_scatter | solution.py:121
  64.3 1.2 copy-start
  65.5 4.3 %copy-start.4 = (f32[128,256]{1,0:T(8,128)S(1)}, f32[128,256]{1,0:T(8,128)}, u32[]{:S(2)}) copy-start(f32[128,256]{1,0:T(8,128)} %shard_map.55) | copy-start | bytes 393220
  77.6 3.8 %collective-permute-start.2 = (bf16[16,128,384]{2,1,0:T(8,128)(2,1)}, bf16[16,128,384]{2,1,0:T(8,128)(2,1)S(1)}, u32[]{:S(2)}, u32[]{:S(2)}) collective-permute-start(bf16[16,128,384]{2,1,0:T(8,128)(2,1)} %get-tuple-element.12), channel_id=1, source_target_pairs={{0,1},{1,0},{2,3},{3,2},{4,5},{5,4},{6,7},{7,6},{8,9},{9,8},{10,11... | collective-permute-start | bytes 4718600 | tf_op jit(solution)/shard_map/ppermute | solution.py:16
  84.4 15.0 %copy-start.5 = (bf16[1,256,256]{2,1,0:T(8,128)(2,1)S(1)}, bf16[1,256,256]{2,1,0:T(8,128)(2,1)}, u32[]{:S(2)}) copy-start(bf16[1,256,256]{2,1,0:T(8,128)(2,1)} %param.7) | copy-start | bytes 393220
  99.3 5.4 %collective-permute-start.5 = (bf16[8,2,128,384]{3,2,1,0:T(8,128)(2,1)}, bf16[8,2,128,384]{3,2,1,0:T(8,128)(2,1)S(1)}, u32[]{:S(2)}, u32[]{:S(2)}) collective-permute-start(bf16[8,2,128,384]{3,2,1,0:T(8,128)(2,1)} %bitcast.75), channel_id=1, source_target_pairs={{0,1},{1,0},{2,3},{3,2},{4,5},{5,4},{6,7},{7,6},{8,9},{9,8},{10,11... | collective-permute-start | bytes 4718600 | tf_op jit(solution)/shard_map/ppermute | solution.py:16
  99.3 83.5 %reduce-scatter.5.cloned.1.call-start = ((), (), s32[]{:S(2)}) async-start(), calls=%async_computation.3 | async-start | bytes 1769472 | tf_op jit(solution)/shard_map/reduce_scatter | solution.py:121
  104.6 1.2 copy-start.1
  105.8 4.3 %copy-start.3 = (f32[128,256]{1,0:T(8,128)S(1)}, f32[128,256]{1,0:T(8,128)}, u32[]{:S(2)}) copy-start(f32[128,256]{1,0:T(8,128)} %shard_map.58) | copy-start | bytes 393220
  118.3 3.8 %collective-permute-start.6 = (bf16[16,128,384]{2,1,0:T(8,128)(2,1)}, bf16[16,128,384]{2,1,0:T(8,128)(2,1)S(1)}, u32[]{:S(2)}, u32[]{:S(2)}) collective-permute-start(bf16[16,128,384]{2,1,0:T(8,128)(2,1)} %get-tuple-element.16), channel_id=1, source_target_pairs={{0,1},{1,0},{2,3},{3,2},{4,5},{5,4},{6,7},{7,6},{8,9},{9,8},{10,11... | collective-permute-start | bytes 4718600 | tf_op jit(solution)/shard_map/ppermute | solution.py:16
  125.1 65.0 %copy-start.2 = (bf16[1,256,384]{2,1,0:T(8,128)(2,1)S(1)}, bf16[1,256,384]{2,1,0:T(8,128)(2,1)}, u32[]{:S(2)}) copy-start(bf16[1,256,384]{2,1,0:T(8,128)(2,1)} %param.5) | copy-start | bytes 589828
  142.0 44.8 %collective-permute-start.3 = (bf16[128,384]{1,0:T(8,128)(2,1)S(1)}, bf16[128,384]{1,0:T(8,128)(2,1)S(1)}, u32[]{:S(2)}, u32[]{:S(2)}) collective-permute-start(bf16[128,384]{1,0:T(8,128)(2,1)S(1)} %dynamic-slice_bitcast_fusion.1), channel_id=1, source_target_pairs={{0,2},{2,0},{1,3},{3,1},{4,6},{6,4},{5,7},{7,5},{8,10},{10,8},{9,1... | collective-permute-start | bytes 294920 | tf_op jit(solution)/shard_map/ppermute | solution.py:16
  183.8 6.3 %collective-permute-start.7 = (bf16[128,384]{1,0:T(8,128)(2,1)S(1)}, bf16[128,384]{1,0:T(8,128)(2,1)S(1)}, u32[]{:S(2)}, u32[]{:S(2)}) collective-permute-start(bf16[128,384]{1,0:T(8,128)(2,1)S(1)} %dynamic-slice_bitcast_fusion), channel_id=1, source_target_pairs={{0,2},{2,0},{1,3},{3,1},{4,6},{6,4},{5,7},{7,5},{8,10},{10,8},{9,1... | collective-permute-start | bytes 294920 | tf_op jit(solution)/shard_map/ppermute | solution.py:16
  191.0 4.7 %collective-permute-start.4 = (bf16[128,384]{1,0:T(8,128)(2,1)S(1)}, bf16[128,384]{1,0:T(8,128)(2,1)S(1)}, u32[]{:S(2)}, u32[]{:S(2)}) collective-permute-start(bf16[128,384]{1,0:T(8,128)(2,1)S(1)} %get-tuple-element.21), channel_id=1, source_target_pairs={{0,128},{128,0},{1,129},{129,1},{2,130},{130,2},{3,131},{131,3},{4... | collective-permute-start | bytes 294920 | tf_op jit(solution)/shard_map/ppermute | solution.py:16
  193.1 4.6 %collective-permute-start.8 = (bf16[128,384]{1,0:T(8,128)(2,1)S(1)}, bf16[128,384]{1,0:T(8,128)(2,1)S(1)}, u32[]{:S(2)}, u32[]{:S(2)}) collective-permute-start(bf16[128,384]{1,0:T(8,128)(2,1)S(1)} %get-tuple-element.22), channel_id=1, source_target_pairs={{0,128},{128,0},{1,129},{129,1},{2,130},{130,2},{3,131},{131,3},{4... | collective-permute-start | bytes 294920 | tf_op jit(solution)/shard_map/ppermute | solution.py:16
Sparse Core Ops, SparseCore 0:
  16.8 42.4 all-gather.6
  61.1 38.1 all-gather.4
  101.9 39.2 reduce-scatter.2
  143.5 39.2 reduce-scatter.4

commit v5 on v3

--- a/solution.py
+++ b/solution.py
@@ -130,10 +130,10 @@
     y_index = lax.axis_index("ty")
     keep = lax.dynamic_index_in_dim(part, y_index, 0, keepdims=False)
     send = lax.dynamic_index_in_dim(part, 1 - y_index, 0, keepdims=False)
-    result = keep.astype(jnp.float32) + swap(send, "ty").astype(jnp.float32)
-    result = (result + activ.astype(jnp.float32)).astype(jnp.bfloat16)
-    passed = swap(result, "section")
-    return passed[None]
+    keep = (keep.astype(jnp.float32) + activ.astype(jnp.float32)).astype(jnp.bfloat16)
+    across = lax.ppermute(send, ("section", "ty"), [(i, 3 - i) for i in range(4)])
+    result = swap(keep, "section").astype(jnp.float32) + across.astype(jnp.float32)
+    return result.astype(jnp.bfloat16)[None]
 
 
 def solution(mesh):

time: 171 us -> 165 us (0.965)
  waiting for transfers between devices: 113 us -> 109 us
    ppermute x5 -> x4, waiting for transfers between devices: 18.8 us -> 11.6 us  [swap(): return lax.ppermute(value, axis, [(0, 1), (1, 0)])]
    ppermute x0 -> x1, waiting for transfers between devices: none -> 3.96 us  [on_device(): lax.ppermute(send, ('section', 'ty'), [(i, 3 - i) for i in range(4)])]
    ppermute x5 -> x4, starting transfers between devices: 8.63 us -> 5.5 us  [swap(): return lax.ppermute(value, axis, [(0, 1), (1, 0)])]
    ppermute x0 -> x1, starting transfers between devices: none -> 2.05 us  [on_device(): lax.ppermute(send, ('section', 'ty'), [(i, 3 - i) for i in range(4)])]
  transfers between devices with their start and end apart: 7 -> 7, of which waited for: 6 -> 6; matrix products, arithmetic and copies ran while one was open for 2% -> 3% of each run, Pallas kernels for 3% -> 3%
where the time goes in v5:
time: 165 us
  waiting for transfers between devices  109 us (66%)
  Pallas kernels  17.3 us (10%)
  between operations  13.5 us (8%)
  other arithmetic  8.98 us (5%)
  starting transfers between devices  7.59 us (5%)
  local copies, waits for them, and re-layouts  5.33 us (3%)
  matrix products  2.84 us (2%)
    all_gather x1, waiting for transfers between devices, on_device(): gathered = lax.all_gather(gathered, 'tz', axis=0)  48 us
    reduce_scatter x1, waiting for transfers between devices, on_device(): part = lax.psum_scatter(part, 'tz', scatter_dimension=0, tiled=False)  45.8 us
    ppermute x4, waiting for transfers between devices, swap(): return lax.ppermute(value, axis, [(0, 1), (1, 0)])  11.6 us
    pallas_call x2, Pallas kernels, value_proj(): pl.pallas_call(value_proj_kernel, out_shape=jax.ShapeDtypeStruct((tokens,...  10 us
    pallas_call x1, Pallas kernels, out_proj(): pl.pallas_call(out_proj_kernel, out_shape=(out, out), grid_spec=pltpu.Pre...  7.31 us
    ppermute x4, starting transfers between devices, swap(): return lax.ppermute(value, axis, [(0, 1), (1, 0)])  5.5 us
    convert_element_type x1, other arithmetic, on_device(): part = part.astype(jnp.bfloat16).reshape(N_Z, N_Y, length, col_width)  4.51 us
    ppermute x1, waiting for transfers between devices, on_device(): lax.ppermute(send, ('section', 'ty'), [(i, 3 - i) for i in range(4)])  3.96 us
  transfers between devices with their start and end apart: 7, of which 6 were waited for; matrix products, arithmetic and copies ran while one was open for 3% of the time, Pallas kernels for 3%

profile of v5, /device:TPU:2, one launch (start us, length us, event | category | flops | bytes accessed | tf_op | source)
XLA Modules:
  0.0 165.0 jit_solution(8707343606857135513)
XLA Ops:
  6.5 3.2 %collective-permute-start = (bf16[256,384]{1,0:T(8,128)(2,1)}, bf16[256,384]{1,0:T(8,128)(2,1)S(1)}, u32[]{:S(2)}, u32[]{:S(2)}) collective-permute-start(bf16[256,384]{1,0:T(8,128)(2,1)} %bitcast.42), channel_id=1, source_target_pairs={{0,2},{2,0},{1,3},{3,1},{4,6},{6,4},{5,7},{7,5},{8,10},{10,8},{9,1... | collective-permute-start | bytes 589832 | tf_op jit(solution)/shard_map/ppermute | solution.py:16
  9.7 5.2 %collective-permute-done = bf16[256,384]{1,0:T(8,128)(2,1)S(1)} collective-permute-done((bf16[256,384]{1,0:T(8,128)(2,1)}, bf16[256,384]{1,0:T(8,128)(2,1)S(1)}, u32[]{:S(2)}, u32[]{:S(2)}) %collective-permute-start) | collective-permute-done | bytes 196640 | tf_op jit(solution)/shard_map/ppermute | solution.py:16
  14.9 1.0 select_bitcast_fusion.1
  15.9 0.8 pad_maximum_fusion
  16.7 48.0 %all-gather.3.cloned.1.call-done.f_ref = bf16[16,256,384]{2,1,0:T(8,128)(2,1)} async-done(((bf16[2,256,384]{2,1,0:T(8,128)(2,1)}), bf16[16,256,384]{2,1,0:T(8,128)(2,1)}) %all-gather.3.cloned.1.call-update) | async-done | bytes 3145744 | tf_op jit(solution)/shard_map/all_gather | solution.py:99
  64.8 0.9 reshape.73
  65.7 0.9 reshape.74
  67.0 1.0 fusion.3
  68.1 5.0 %shard_map.55 = f32[256,256]{1,0:T(8,128)} custom-call(s32[1]{0:T(128)} %bitcast.core_ref, bf16[16,256,384]{2,1,0:T(8,128)(2,1)} %all-gather.3.cloned.1.call-done.f_ref, bf16[12288,256]{1,0:T(8,128)(2,1)} %bitcast.30, bf16[12288,256]{1,0:T(8,128)(2,1)} %bitcast.31, bf16[12288,256]{1,0:T(8,128)(2,1)} %bitcast.32, bf16[12288,256]{1,0:T(8,128)(2,1)} %bitcast.33), custom_call_target="tpu_custom_call" | custom-call | tf_op jit(solution)/shard_map/pallas_call | solution.py:76
  73.1 1.6 copy-done
  74.7 5.0 %shard_map.56 = f32[256,256]{1,0:T(8,128)} custom-call(s32[1]{0:T(128)} %bitcast.5.core_ref, bf16[16,256,384]{2,1,0:T(8,128)(2,1)} %bitcast.41, bf16[12288,256]{1,0:T(8,128)(2,1)} %bitcast.34, bf16[12288,256]{1,0:T(8,128)(2,1)} %bitcast.35, bf16[12288,256]{1,0:T(8,128)(2,1)} %bitcast.36, bf16[12288,256]{1,0:T(8,128)(2,1)} %bitcast.37), custom_call_target="tpu_custom_call" | custom-call | tf_op jit(solution)/shard_map/pallas_call | solution.py:76
  79.8 1.0 add_convert_fusion.2
  80.8 1.5 convolution_convert_fusion
  82.3 0.8 copy.18.ctx_ref
  83.1 7.3 %shard_map.57 = (bf16[16,256,384]{2,1,0:T(8,128)(2,1)}, bf16[16,256,384]{2,1,0:T(8,128)(2,1)}) custom-call(s32[1]{0:T(128)} %bitcast.core_ref, bf16[256,256]{1,0:T(8,128)(2,1)} %copy.18.ctx_ref, bf16[256,12288]{1,0:T(8,128)(2,1)} %bitcast.39), custom_call_target="tpu_custom_call" | custom-call | tf_op jit(solution)/shard_map/pallas_call | solution.py:38
  90.9 5.5 %collective-permute-done.2 = bf16[16,256,384]{2,1,0:T(8,128)(2,1)S(1)} collective-permute-done((bf16[16,256,384]{2,1,0:T(8,128)(2,1)}, bf16[16,256,384]{2,1,0:T(8,128)(2,1)S(1)}, u32[]{:S(2)}, u32[]{:S(2)}) %collective-permute-start.2) | collective-permute-done | bytes 3145760 | tf_op jit(solution)/shard_map/ppermute | solution.py:16
  96.4 4.5 %add_convert_fusion = bf16[16,256,384]{2,1,0:T(8,128)(2,1)} fusion(bf16[16,256,384]{2,1,0:T(8,128)(2,1)S(1)} %collective-permute-done.2, bf16[16,256,384]{2,1,0:T(8,128)(2,1)} %get-tuple-element.7), kind=kLoop, calls=%fused_computation.1 | loop fusion | flops 6291456 | bytes 9437184 | tf_op jit(solution)/shard_map/convert_element_type | solution.py:128
  101.0 45.8 %reduce-scatter.2.cloned.1.call-done = bf16[1,2,256,384]{3,2,1,0:T(8,128)(2,1)} async-done(((bf16[8,2,256,384]{3,2,1,0:T(8,128)(2,1)}), bf16[1,2,256,384]{3,2,1,0:T(8,128)(2,1)}) %reduce-scatter.2.cloned.1.call-update) | async-done | bytes 393232 | tf_op jit(solution)/shard_map/reduce_scatter | solution.py:129
  146.7 1.0 fusion.4
  147.7 1.8 %collective-permute-start.3 = (bf16[256,384]{1,0:T(8,128)(2,1)S(1)}, bf16[256,384]{1,0:T(8,128)(2,1)S(1)}, u32[]{:S(2)}, u32[]{:S(2)}) collective-permute-start(bf16[256,384]{1,0:T(8,128)(2,1)S(1)} %fusion.4), channel_id=1, source_target_pairs={{0,128},{128,0},{1,129},{129,1},{2,130},{130,2},{3,131},{131,3},{4... | collective-permute-start | bytes 589832 | tf_op jit(solution)/shard_map/ppermute | solution.py:16
  149.5 0.9 dynamic-slice_bitcast_fusion
  150.4 2.0 %collective-permute-start.4 = (bf16[256,384]{1,0:T(8,128)(2,1)S(1)}, bf16[256,384]{1,0:T(8,128)(2,1)S(1)}, u32[]{:S(2)}, u32[]{:S(2)}) collective-permute-start(bf16[256,384]{1,0:T(8,128)(2,1)S(1)} %dynamic-slice_bitcast_fusion), channel_id=1, source_target_pairs={{0,130},{2,128},{128,2},{130,0},{1,131},{3,129},{129,3},{131,1},{4... | collective-permute-start | bytes 589832 | tf_op jit(solution)/shard_map/ppermute | solution.py:134
  152.5 1.0 collective-permute-done.3
  153.4 4.0 %collective-permute-done.4 = bf16[256,384]{1,0:T(8,128)(2,1)S(1)} collective-permute-done((bf16[256,384]{1,0:T(8,128)(2,1)S(1)}, bf16[256,384]{1,0:T(8,128)(2,1)S(1)}, u32[]{:S(2)}, u32[]{:S(2)}) %collective-permute-start.4) | collective-permute-done | bytes 196640 | tf_op jit(solution)/shard_map/ppermute | solution.py:134
  (16 shorter events, 1.8 us)
Async XLA Ops:
  6.5 58.2 %all-gather.3.cloned.1.call-start = ((), (), s32[]{:S(2)}) async-start(), calls=%async_computation.2 | async-start | bytes 3538944 | tf_op jit(solution)/shard_map/all_gather | solution.py:99
  6.5 8.4 %collective-permute-start = (bf16[256,384]{1,0:T(8,128)(2,1)}, bf16[256,384]{1,0:T(8,128)(2,1)S(1)}, u32[]{:S(2)}, u32[]{:S(2)}) collective-permute-start(bf16[256,384]{1,0:T(8,128)(2,1)} %bitcast.42), channel_id=1, source_target_pairs={{0,2},{2,0},{1,3},{3,1},{4,6},{6,4},{5,7},{7,5},{8,10},{10,8},{9,1... | collective-permute-start | bytes 589832 | tf_op jit(solution)/shard_map/ppermute | solution.py:16
  16.7 130.0 %reduce-scatter.2.cloned.1.call-start = ((), (), s32[]{:S(2)}) async-start(), calls=%async_computation.1 | async-start | bytes 3538944 | tf_op jit(solution)/shard_map/reduce_scatter | solution.py:129
  64.8 8.3 %collective-permute-start.1 = (bf16[8,2,256,384]{3,2,1,0:T(8,128)(2,1)}, bf16[8,2,256,384]{3,2,1,0:T(8,128)(2,1)S(1)}, u32[]{:S(2)}, u32[]{:S(2)}) collective-permute-start(bf16[8,2,256,384]{3,2,1,0:T(8,128)(2,1)} %bitcast.40), channel_id=1, source_target_pairs={{0,1},{1,0},{2,3},{3,2},{4,5},{5,4},{6,7},{7,6},{8,9},{9,8},{10,11... | collective-permute-start | bytes 9437192 | tf_op jit(solution)/shard_map/ppermute | solution.py:16
  73.1 1.6 copy-start
  74.7 5.0 %copy-start.1 = (f32[256,256]{1,0:T(8,128)S(1)}, f32[256,256]{1,0:T(8,128)}, u32[]{:S(2)}) copy-start(f32[256,256]{1,0:T(8,128)} %shard_map.55) | copy-start | bytes 786436
  90.4 6.0 %collective-permute-start.2 = (bf16[16,256,384]{2,1,0:T(8,128)(2,1)}, bf16[16,256,384]{2,1,0:T(8,128)(2,1)S(1)}, u32[]{:S(2)}, u32[]{:S(2)}) collective-permute-start(bf16[16,256,384]{2,1,0:T(8,128)(2,1)} %get-tuple-element.8), channel_id=1, source_target_pairs={{0,1},{1,0},{2,3},{3,2},{4,5},{5,4},{6,7},{7,6},{8,9},{9,8},{10,11... | collective-permute-start | bytes 9437192 | tf_op jit(solution)/shard_map/ppermute | solution.py:16
  100.9 45.8 %copy-start.2 = (bf16[1,256,384]{2,1,0:T(8,128)(2,1)S(1)}, bf16[1,256,384]{2,1,0:T(8,128)(2,1)}, u32[]{:S(2)}) copy-start(bf16[1,256,384]{2,1,0:T(8,128)(2,1)} %param.5) | copy-start | bytes 589828
  147.7 5.8 %collective-permute-start.3 = (bf16[256,384]{1,0:T(8,128)(2,1)S(1)}, bf16[256,384]{1,0:T(8,128)(2,1)S(1)}, u32[]{:S(2)}, u32[]{:S(2)}) collective-permute-start(bf16[256,384]{1,0:T(8,128)(2,1)S(1)} %fusion.4), channel_id=1, source_target_pairs={{0,128},{128,0},{1,129},{129,1},{2,130},{130,2},{3,131},{131,3},{4... | collective-permute-start | bytes 589832 | tf_op jit(solution)/shard_map/ppermute | solution.py:16
  150.4 7.0 %collective-permute-start.4 = (bf16[256,384]{1,0:T(8,128)(2,1)S(1)}, bf16[256,384]{1,0:T(8,128)(2,1)S(1)}, u32[]{:S(2)}, u32[]{:S(2)}) collective-permute-start(bf16[256,384]{1,0:T(8,128)(2,1)S(1)} %dynamic-slice_bitcast_fusion), channel_id=1, source_target_pairs={{0,130},{2,128},{128,2},{130,0},{1,131},{3,129},{129,3},{131,1},{4... | collective-permute-start | bytes 589832 | tf_op jit(solution)/shard_map/ppermute | solution.py:134
Sparse Core Ops, SparseCore 0:
  16.8 47.9 all-gather.2
  101.1 45.5 reduce-scatter.1

commit v6 on v5

--- a/solution.py
+++ b/solution.py
@@ -53,7 +53,7 @@
     )(core, context, weight_o)
 
 
-def value_proj_kernel(core_ref, f_ref, *refs):
+def gathered_proj_kernel(f_ref, *refs):
     w_refs, o_ref = refs[:-1], refs[-1]
 
     @pl.when(pl.program_id(0) == 0)
@@ -66,23 +66,22 @@
     o_ref[...] = acc
 
 
-def value_proj(core, feats, weight_v):
-    n_groups, tokens, width = feats.shape
-    step = GROUPS_PER_STEP
+def gathered_proj(feats, weight_v):
+    tokens, width = feats.shape[-2:]
+    feats = feats.reshape(-1, tokens, width)
+    step = N_C * N_Y
     w_specs = [
-        pl.BlockSpec((width, weight_v.shape[1]), lambda i, c, k=k: (N_C * (i * step + k) + c[0], 0))
-        for k in range(step)
+        pl.BlockSpec((width, weight_v.shape[1]), lambda i, c=c, y=y: (i * step + y * N_C + c, 0))
+        for c in range(N_C)
+        for y in range(N_Y)
     ]
     return pl.pallas_call(
-        value_proj_kernel,
+        gathered_proj_kernel,
         out_shape=jax.ShapeDtypeStruct((tokens, weight_v.shape[1]), jnp.float32),
-        grid_spec=pltpu.PrefetchScalarGridSpec(
-            num_scalar_prefetch=1,
-            grid=(n_groups // step,),
-            in_specs=[pl.BlockSpec((step, tokens, width), lambda i, c: (i, 0, 0))] + w_specs,
-            out_specs=pl.BlockSpec((tokens, weight_v.shape[1]), lambda i, c: (0, 0)),
-        ),
-    )(core, feats, *([weight_v] * step))
+        grid=(N_Z,),
+        in_specs=[pl.BlockSpec((step, tokens, width), lambda i: (i, 0, 0))] + w_specs,
+        out_specs=pl.BlockSpec((tokens, weight_v.shape[1]), lambda i: (0, 0)),
+    )(feats, *([weight_v] * step))
 
 
 def on_device(inputs, queries, keys, w_value, w_out):
@@ -96,12 +95,8 @@
     y_first = lax.axis_index("ty") == 0
     other = swap(activ, "ty")
     gathered = jnp.stack([jnp.where(y_first, activ, other), jnp.where(y_first, other, activ)])
-    gathered = lax.all_gather(gathered, "tz", axis=0)
-    from_sib = swap(gathered, "tc").reshape(N_Z * N_Y, length, col_width)
-    gathered = gathered.reshape(N_Z * N_Y, length, col_width)
-    c_index = lax.axis_index("tc").astype(jnp.int32)
-    values = value_proj(c_index.reshape(1), gathered, weight_v)
-    values = values + value_proj((1 - c_index).reshape(1), from_sib, weight_v)
+    gathered = lax.all_gather(gathered, ("tz", "tc"), axis=0)
+    values = gathered_proj(gathered, weight_v)
     values = values.astype(jnp.bfloat16)
 
     heads_here = weight_v.shape[1] // HEAD_SIZE

time: 165 us -> 159 us (0.964)
  matrix products: 2.84 us -> 0.86 us
    ppermute x4 -> x3, waiting for transfers between devices: 11.6 us -> 13.4 us  [swap(): return lax.ppermute(value, axis, [(0, 1), (1, 0)])]
    ppermute x4 -> x3, starting transfers between devices: 5.5 us -> 3.74 us  [swap(): return lax.ppermute(value, axis, [(0, 1), (1, 0)])]
    pallas_call x2 -> x1, Pallas kernels: 10 us -> 8.81 us  [gathered_proj(): pl.pallas_call(gathered_proj_kernel, out_shape=jax.ShapeDtypeStruct((toke...]
  transfers between devices with their start and end apart: 7 -> 6, of which waited for: 6 -> 6; matrix products, arithmetic and copies ran while one was open for 3% -> 2% of each run, Pallas kernels for 3% -> 0%
where the time goes in v6:
time: 159 us; the launch traced here: 158 us
  waiting for transfers between devices  109 us (69%)
  Pallas kernels  16.1 us (10%)
  between operations  13.5 us (8%)
  other arithmetic  8.99 us (6%)
  starting transfers between devices  6.62 us (4%)
  local copies, waits for them, and re-layouts  3.69 us (2%)
    all_gather x1, waiting for transfers between devices, on_device(): gathered = lax.all_gather(gathered, ('tz', 'tc'), axis=0)  46.6 us
    reduce_scatter x1, waiting for transfers between devices, on_device(): part = lax.psum_scatter(part, 'tz', scatter_dimension=0, tiled=False)  45.8 us
    ppermute x3, waiting for transfers between devices, swap(): return lax.ppermute(value, axis, [(0, 1), (1, 0)])  13.4 us
    pallas_call x1, Pallas kernels, gathered_proj(): pl.pallas_call(gathered_proj_kernel, out_shape=jax.ShapeDtypeStruct((toke...  8.81 us
    pallas_call x1, Pallas kernels, out_proj(): pl.pallas_call(out_proj_kernel, out_shape=(out, out), grid_spec=pltpu.Pre...  7.32 us
    convert_element_type x1, other arithmetic, on_device(): part = part.astype(jnp.bfloat16).reshape(N_Z, N_Y, length, col_width)  4.52 us
    ppermute x3, starting transfers between devices, swap(): return lax.ppermute(value, axis, [(0, 1), (1, 0)])  3.74 us
  transfers between devices with their start and end apart: 6, of which 6 were waited for; matrix products, arithmetic and copies ran while one was open for 2% of the time, Pallas kernels for 0%

profile of v6, /device:TPU:2, one launch (start us, length us, event | category | flops | bytes accessed | tf_op | source)
XLA Modules:
  0.0 158.4 jit_solution(3875309616633397511)
XLA Ops:
  6.5 3.2 %collective-permute-start = (bf16[256,384]{1,0:T(8,128)(2,1)}, bf16[256,384]{1,0:T(8,128)(2,1)S(1)}, u32[]{:S(2)}, u32[]{:S(2)}) collective-permute-start(bf16[256,384]{1,0:T(8,128)(2,1)} %bitcast.33), channel_id=1, source_target_pairs={{0,2},{2,0},{1,3},{3,1},{4,6},{6,4},{5,7},{7,5},{8,10},{10,8},{9,1... | collective-permute-start | bytes 589832 | tf_op jit(solution)/shard_map/ppermute | solution.py:16
  9.7 5.2 %collective-permute-done = bf16[256,384]{1,0:T(8,128)(2,1)S(1)} collective-permute-done((bf16[256,384]{1,0:T(8,128)(2,1)}, bf16[256,384]{1,0:T(8,128)(2,1)S(1)}, u32[]{:S(2)}, u32[]{:S(2)}) %collective-permute-start) | collective-permute-done | bytes 196640 | tf_op jit(solution)/shard_map/ppermute | solution.py:16
  14.9 1.0 select_bitcast_fusion.1
  15.9 0.8 pad_maximum_fusion
  16.7 0.9 reshape.64
  17.7 0.9 reshape.65
  18.7 0.3 fusion.15
  19.0 0.2 fusion.3
  19.3 46.6 %all-gather.3.cloned.1.call-done.f_ref = bf16[32,256,384]{2,1,0:T(8,128)(2,1)} async-done(((bf16[2,256,384]{2,1,0:T(8,128)(2,1)}), bf16[32,256,384]{2,1,0:T(8,128)(2,1)}) %all-gather.3.cloned.1.call-update) | async-done | bytes 6291472 | tf_op jit(solution)/shard_map/all_gather | solution.py:98
  65.8 8.8 %shard_map.55 = f32[256,256]{1,0:T(8,128)} custom-call(bf16[32,256,384]{2,1,0:T(8,128)(2,1)} %all-gather.3.cloned.1.call-done.f_ref, bf16[12288,256]{1,0:T(8,128)(2,1)} %bitcast.27, bf16[12288,256]{1,0:T(8,128)(2,1)} %bitcast.28, bf16[12288,256]{1,0:T(8,128)(2,1)} %bitcast.29, bf16[12288,256]{1,0:T(8,128)(2,1)} %bitcast.30), custom_call_target="tpu_custom_call" | custom-call | tf_op jit(solution)/shard_map/pallas_call | solution.py:78
  74.7 1.0 convert_element_type.46
  75.7 0.3 convolution_convert_fusion
  76.0 0.8 copy.18.ctx_ref
  76.8 7.3 %shard_map.56 = (bf16[16,256,384]{2,1,0:T(8,128)(2,1)}, bf16[16,256,384]{2,1,0:T(8,128)(2,1)}) custom-call(s32[1]{0:T(128)} %bitcast.core_ref, bf16[256,256]{1,0:T(8,128)(2,1)} %copy.18.ctx_ref, bf16[256,12288]{1,0:T(8,128)(2,1)} %bitcast.32), custom_call_target="tpu_custom_call" | custom-call | tf_op jit(solution)/shard_map/pallas_call | solution.py:38
  84.3 5.6 %collective-permute-done.1 = bf16[16,256,384]{2,1,0:T(8,128)(2,1)S(1)} collective-permute-done((bf16[16,256,384]{2,1,0:T(8,128)(2,1)}, bf16[16,256,384]{2,1,0:T(8,128)(2,1)S(1)}, u32[]{:S(2)}, u32[]{:S(2)}) %collective-permute-start.1) | collective-permute-done | bytes 3145760 | tf_op jit(solution)/shard_map/ppermute | solution.py:16
  90.0 4.5 %add_convert_fusion = bf16[16,256,384]{2,1,0:T(8,128)(2,1)} fusion(bf16[16,256,384]{2,1,0:T(8,128)(2,1)S(1)} %collective-permute-done.1, bf16[16,256,384]{2,1,0:T(8,128)(2,1)} %get-tuple-element.7), kind=kLoop, calls=%fused_computation.1 | loop fusion | flops 6291456 | bytes 9437184 | tf_op jit(solution)/shard_map/convert_element_type | solution.py:123
  94.5 45.8 %reduce-scatter.2.cloned.1.call-done = bf16[1,2,256,384]{3,2,1,0:T(8,128)(2,1)} async-done(((bf16[8,2,256,384]{3,2,1,0:T(8,128)(2,1)}), bf16[1,2,256,384]{3,2,1,0:T(8,128)(2,1)}) %reduce-scatter.2.cloned.1.call-update) | async-done | bytes 393232 | tf_op jit(solution)/shard_map/reduce_scatter | solution.py:124
  140.4 0.9 dynamic-slice_bitcast_fusion
  141.3 2.8 %collective-permute-start.3 = (bf16[256,384]{1,0:T(8,128)(2,1)S(1)}, bf16[256,384]{1,0:T(8,128)(2,1)S(1)}, u32[]{:S(2)}, u32[]{:S(2)}) collective-permute-start(bf16[256,384]{1,0:T(8,128)(2,1)S(1)} %dynamic-slice_bitcast_fusion), channel_id=1, source_target_pairs={{0,130},{2,128},{128,2},{130,0},{1,131},{3,129},{129,3},{131,1},{4... | collective-permute-start | bytes 589832 | tf_op jit(solution)/shard_map/ppermute | solution.py:129
  144.1 1.0 fusion.4
  145.1 0.3 collective-permute-start.2
  145.4 2.8 %collective-permute-done.3 = bf16[256,384]{1,0:T(8,128)(2,1)S(1)} collective-permute-done((bf16[256,384]{1,0:T(8,128)(2,1)S(1)}, bf16[256,384]{1,0:T(8,128)(2,1)S(1)}, u32[]{:S(2)}, u32[]{:S(2)}) %collective-permute-start.3) | collective-permute-done | bytes 196640 | tf_op jit(solution)/shard_map/ppermute | solution.py:129
  148.3 2.6 %collective-permute-done.2 = bf16[256,384]{1,0:T(8,128)(2,1)S(1)} collective-permute-done((bf16[256,384]{1,0:T(8,128)(2,1)S(1)}, bf16[256,384]{1,0:T(8,128)(2,1)S(1)}, u32[]{:S(2)}, u32[]{:S(2)}) %collective-permute-start.2) | collective-permute-done | bytes 196640 | tf_op jit(solution)/shard_map/ppermute | solution.py:16
  150.9 0.7 fusion.5
  (9 shorter events, 0.4 us)
Async XLA Ops:
  6.5 59.3 %all-gather.3.cloned.1.call-start = ((), (), s32[]{:S(2)}) async-start(), calls=%async_computation.2 | async-start | bytes 6684672 | tf_op jit(solution)/shard_map/all_gather | solution.py:98
  6.5 8.4 %collective-permute-start = (bf16[256,384]{1,0:T(8,128)(2,1)}, bf16[256,384]{1,0:T(8,128)(2,1)S(1)}, u32[]{:S(2)}, u32[]{:S(2)}) collective-permute-start(bf16[256,384]{1,0:T(8,128)(2,1)} %bitcast.33), channel_id=1, source_target_pairs={{0,2},{2,0},{1,3},{3,1},{4,6},{6,4},{5,7},{7,5},{8,10},{10,8},{9,1... | collective-permute-start | bytes 589832 | tf_op jit(solution)/shard_map/ppermute | solution.py:16
  16.7 123.7 %reduce-scatter.2.cloned.1.call-start = ((), (), s32[]{:S(2)}) async-start(), calls=%async_computation.1 | async-start | bytes 3538944 | tf_op jit(solution)/shard_map/reduce_scatter | solution.py:124
  84.1 5.9 %collective-permute-start.1 = (bf16[16,256,384]{2,1,0:T(8,128)(2,1)}, bf16[16,256,384]{2,1,0:T(8,128)(2,1)S(1)}, u32[]{:S(2)}, u32[]{:S(2)}) collective-permute-start(bf16[16,256,384]{2,1,0:T(8,128)(2,1)} %get-tuple-element.8), channel_id=1, source_target_pairs={{0,1},{1,0},{2,3},{3,2},{4,5},{5,4},{6,7},{7,6},{8,9},{9,8},{10,11... | collective-permute-start | bytes 9437192 | tf_op jit(solution)/shard_map/ppermute | solution.py:16
  94.5 49.6 %copy-start = (bf16[1,256,384]{2,1,0:T(8,128)(2,1)S(1)}, bf16[1,256,384]{2,1,0:T(8,128)(2,1)}, u32[]{:S(2)}) copy-start(bf16[1,256,384]{2,1,0:T(8,128)(2,1)} %param.5) | copy-start | bytes 589828
  141.3 7.0 %collective-permute-start.3 = (bf16[256,384]{1,0:T(8,128)(2,1)S(1)}, bf16[256,384]{1,0:T(8,128)(2,1)S(1)}, u32[]{:S(2)}, u32[]{:S(2)}) collective-permute-start(bf16[256,384]{1,0:T(8,128)(2,1)S(1)} %dynamic-slice_bitcast_fusion), channel_id=1, source_target_pairs={{0,130},{2,128},{128,2},{130,0},{1,131},{3,129},{129,3},{131,1},{4... | collective-permute-start | bytes 589832 | tf_op jit(solution)/shard_map/ppermute | solution.py:129
  145.1 5.8 %collective-permute-start.2 = (bf16[256,384]{1,0:T(8,128)(2,1)S(1)}, bf16[256,384]{1,0:T(8,128)(2,1)S(1)}, u32[]{:S(2)}, u32[]{:S(2)}) collective-permute-start(bf16[256,384]{1,0:T(8,128)(2,1)S(1)} %fusion.4), channel_id=1, source_target_pairs={{0,128},{128,0},{1,129},{129,1},{2,130},{130,2},{3,131},{131,3},{4... | collective-permute-start | bytes 589832 | tf_op jit(solution)/shard_map/ppermute | solution.py:16
Sparse Core Ops, SparseCore 0:
  16.8 48.9 all-gather.2
  94.6 45.6 reduce-scatter.1

commit v7 on v6

--- a/solution.py
+++ b/solution.py
@@ -10,47 +10,39 @@
 LEN = 256
 N_Z, N_Y, N_C = 8, 2, 2
 GROUPS_PER_STEP = 4
+Z_PER_STEP = 2
 
 
 def swap(value, axis):
     return lax.ppermute(value, axis, [(0, 1), (1, 0)])
 
 
-def out_proj_kernel(core_ref, ctx_ref, w_ref, mine_ref, sib_ref):
-    width = mine_ref.shape[2]
-    is_zero = core_ref[0] == 0
+def out_proj_kernel(core_ref, ctx_ref, *refs):
+    w_refs, o_ref = refs[:-1], refs[-1]
     ctx = ctx_ref[...]
-    for i in range(mine_ref.shape[0]):
-        lo = i * 2 * width
-        d0 = jnp.dot(ctx, w_ref[:, lo:lo + width], preferred_element_type=jnp.float32)
-        d1 = jnp.dot(ctx, w_ref[:, lo + width:lo + 2 * width], preferred_element_type=jnp.float32)
-        d0 = d0.astype(jnp.bfloat16)
-        d1 = d1.astype(jnp.bfloat16)
-        mine_ref[i] = jnp.where(is_zero, d0, d1)
-        sib_ref[i] = jnp.where(is_zero, d1, d0)
+    for k, w_ref in enumerate(w_refs):
+        d = jnp.dot(ctx, w_ref[...], preferred_element_type=jnp.float32)
+        o_ref[k] = d.astype(jnp.bfloat16)
 
 
 def out_proj(core, context, weight_o, width):
     tokens, inner = context.shape
     n_groups = weight_o.shape[1] // (N_C * width)
     step = GROUPS_PER_STEP
-    out = jax.ShapeDtypeStruct((n_groups, tokens, width), jnp.bfloat16)
+    w_specs = [
+        pl.BlockSpec((inner, width), lambda i, c, k=k: (0, N_C * (i * step + k) + c[0]))
+        for k in range(step)
+    ]
     return pl.pallas_call(
         out_proj_kernel,
-        out_shape=(out, out),
+        out_shape=jax.ShapeDtypeStruct((n_groups, tokens, width), jnp.bfloat16),
         grid_spec=pltpu.PrefetchScalarGridSpec(
             num_scalar_prefetch=1,
             grid=(n_groups // step,),
-            in_specs=[
-                pl.BlockSpec((tokens, inner), lambda i, c: (0, 0)),
-                pl.BlockSpec((inner, step * N_C * width), lambda i, c: (0, i)),
-            ],
-            out_specs=[
-                pl.BlockSpec((step, tokens, width), lambda i, c: (i, 0, 0)),
-                pl.BlockSpec((step, tokens, width), lambda i, c: (i, 0, 0)),
-            ],
+            in_specs=[pl.BlockSpec((tokens, inner), lambda i, c: (0, 0))] + w_specs,
+            out_specs=pl.BlockSpec((step, tokens, width), lambda i, c: (i, 0, 0)),
         ),
-    )(core, context, weight_o)
+    )(core, context, *([weight_o] * step))
 
 
 def gathered_proj_kernel(f_ref, *refs):
@@ -69,16 +61,21 @@
 def gathered_proj(feats, weight_v):
     tokens, width = feats.shape[-2:]
     feats = feats.reshape(-1, tokens, width)
-    step = N_C * N_Y
+    per_z = N_C * N_Y
+    step = Z_PER_STEP * per_z
     w_specs = [
-        pl.BlockSpec((width, weight_v.shape[1]), lambda i, c=c, y=y: (i * step + y * N_C + c, 0))
+        pl.BlockSpec(
+            (width, weight_v.shape[1]),
+            lambda i, z=z, c=c, y=y: ((i * Z_PER_STEP + z) * per_z + y * N_C + c, 0),
+        )
+        for z in range(Z_PER_STEP)
         for c in range(N_C)
         for y in range(N_Y)
     ]
     return pl.pallas_call(
         gathered_proj_kernel,
         out_shape=jax.ShapeDtypeStruct((tokens, weight_v.shape[1]), jnp.float32),
-        grid=(N_Z,),
+        grid=(N_Z // Z_PER_STEP,),
         in_specs=[pl.BlockSpec((step, tokens, width), lambda i: (i, 0, 0))] + w_specs,
         out_specs=pl.BlockSpec((tokens, weight_v.shape[1]), lambda i: (0, 0)),
     )(feats, *([weight_v] * step))
@@ -118,8 +115,10 @@
     context = context.reshape(length, heads_here * HEAD_SIZE)
 
     core = lax.axis_index("tc").astype(jnp.int32).reshape(1)
-    mine, sib = out_proj(core, context, weight_o, col_width)
-    part = mine.astype(jnp.float32) + swap(sib, "tc").astype(jnp.float32)
+    sib = out_proj(1 - core, context, weight_o, col_width)
+    from_sib = swap(sib, "tc")
+    mine = out_proj(core, context, weight_o, col_width)
+    part = mine.astype(jnp.float32) + from_sib.astype(jnp.float32)
     part = part.astype(jnp.bfloat16).reshape(N_Z, N_Y, length, col_width)
     part = lax.psum_scatter(part, "tz", scatter_dimension=0, tiled=False)
     y_index = lax.axis_index("ty")

time: 159 us -> 155 us (0.975)
  waiting for transfers between devices: 109 us -> 103 us
  Pallas kernels: 16.1 us -> 17.8 us
    ppermute x3, waiting for transfers between devices: 13.4 us -> 6.36 us  [swap(): return lax.ppermute(value, axis, [(0, 1), (1, 0)])]
    pallas_call x1 -> x2, Pallas kernels: 7.32 us -> 10.8 us  [out_proj(): pl.pallas_call(out_proj_kernel, out_shape=jax.ShapeDtypeStruct((n_groups,...]
    pallas_call x1, Pallas kernels: 8.81 us -> 7.04 us  [gathered_proj(): pl.pallas_call(gathered_proj_kernel, out_shape=jax.ShapeDtypeStruct((toke...]
  transfers between devices with their start and end apart: 6 -> 6, of which waited for: 6 -> 6; matrix products, arithmetic and copies ran while one was open for 2% -> 2% of each run, Pallas kernels for 0% -> 3%
where the time goes in v7:
time: 155 us
  waiting for transfers between devices  103 us (66%)
  Pallas kernels  17.8 us (11%)
  between operations  13.5 us (9%)
  other arithmetic  9 us (6%)
  starting transfers between devices  7.31 us (5%)
  local copies, waits for them, and re-layouts  3.69 us (2%)
    all_gather x1, waiting for transfers between devices, on_device(): gathered = lax.all_gather(gathered, ('tz', 'tc'), axis=0)  46.6 us
    reduce_scatter x1, waiting for transfers between devices, on_device(): part = lax.psum_scatter(part, 'tz', scatter_dimension=0, tiled=False)  45.8 us
    pallas_call x2, Pallas kernels, out_proj(): pl.pallas_call(out_proj_kernel, out_shape=jax.ShapeDtypeStruct((n_groups,...  10.8 us
    pallas_call x1, Pallas kernels, gathered_proj(): pl.pallas_call(gathered_proj_kernel, out_shape=jax.ShapeDtypeStruct((toke...  7.04 us
    ppermute x3, waiting for transfers between devices, swap(): return lax.ppermute(value, axis, [(0, 1), (1, 0)])  6.36 us
    ppermute x3, starting transfers between devices, swap(): return lax.ppermute(value, axis, [(0, 1), (1, 0)])  5.09 us
    convert_element_type x1, other arithmetic, on_device(): part = part.astype(jnp.bfloat16).reshape(N_Z, N_Y, length, col_width)  4.53 us
    ppermute x1, waiting for transfers between devices, on_device(): lax.ppermute(send, ('section', 'ty'), [(i, 3 - i) for i in range(4)])  3.82 us
  transfers between devices with their start and end apart: 6, of which 6 were waited for; matrix products, arithmetic and copies ran while one was open for 2% of the time, Pallas kernels for 3%

profile of v7, /device:TPU:2, one launch (start us, length us, event | category | flops | bytes accessed | tf_op | source)
XLA Modules:
  0.0 154.8 jit_solution(13166536188727514169)
XLA Ops:
  6.5 3.2 %collective-permute-start = (bf16[256,384]{1,0:T(8,128)(2,1)}, bf16[256,384]{1,0:T(8,128)(2,1)S(1)}, u32[]{:S(2)}, u32[]{:S(2)}) collective-permute-start(bf16[256,384]{1,0:T(8,128)(2,1)} %bitcast.44), channel_id=1, source_target_pairs={{0,2},{2,0},{1,3},{3,1},{4,6},{6,4},{5,7},{7,5},{8,10},{10,8},{9,1... | collective-permute-start | bytes 589832 | tf_op jit(solution)/shard_map/ppermute | solution.py:17
  9.7 5.2 %collective-permute-done = bf16[256,384]{1,0:T(8,128)(2,1)S(1)} collective-permute-done((bf16[256,384]{1,0:T(8,128)(2,1)}, bf16[256,384]{1,0:T(8,128)(2,1)S(1)}, u32[]{:S(2)}, u32[]{:S(2)}) %collective-permute-start) | collective-permute-done | bytes 196640 | tf_op jit(solution)/shard_map/ppermute | solution.py:17
  14.9 1.0 select_bitcast_fusion.1
  15.9 0.8 pad_maximum_fusion
  16.7 0.9 reshape.64
  17.7 0.9 reshape.65
  18.7 0.3 fusion.15
  19.3 46.6 %all-gather.3.cloned.1.call-done.f_ref = bf16[32,256,384]{2,1,0:T(8,128)(2,1)} async-done(((bf16[2,256,384]{2,1,0:T(8,128)(2,1)}), bf16[32,256,384]{2,1,0:T(8,128)(2,1)}) %all-gather.3.cloned.1.call-update) | async-done | bytes 6291472 | tf_op jit(solution)/shard_map/all_gather | solution.py:95
  65.8 7.0 %shard_map.55 = f32[256,256]{1,0:T(8,128)} custom-call(bf16[32,256,384]{2,1,0:T(8,128)(2,1)} %all-gather.3.cloned.1.call-done.f_ref, bf16[12288,256]{1,0:T(8,128)(2,1)} %bitcast.27, bf16[12288,256]{1,0:T(8,128)(2,1)} %bitcast.28, bf16[12288,256]{1,0:T(8,128)(2,1)} %bitcast.29, bf16[12288,256]{1,0:T(8,128)(2,1)} %bitcast.30, bf16[12288,256]{1,0:T(8,128)(2,1)} %bitcast.31, ...), custom_call_target="tpu_custom_call" | custom-call | tf_op jit(solution)/shard_map/pallas_call | solution.py:75
  72.9 1.0 convert_element_type.46
  74.0 0.3 convolution_convert_fusion
  74.2 0.8 copy.18.ctx_ref
  75.0 5.4 %shard_map.57 = bf16[16,256,384]{2,1,0:T(8,128)(2,1)} custom-call(s32[1]{0:T(128)S(6)} %sub.17.core_ref, bf16[256,256]{1,0:T(8,128)(2,1)} %copy.18.ctx_ref, bf16[256,12288]{1,0:T(8,128)(2,1)} %bitcast.35, bf16[256,12288]{1,0:T(8,128)(2,1)} %bitcast.36, bf16[256,12288]{1,0:T(8,128)(2,1)} %bitcast.37, bf16[256,12288]{1,0:T(8,128)(2,1)} %bitcast.38), custom_call_target="tpu_custom_call" | custom-call | tf_op jit(solution)/shard_map/pallas_call | solution.py:36
  80.4 0.2 collective-permute-start.1
  80.6 5.4 %shard_map.56 = bf16[16,256,384]{2,1,0:T(8,128)(2,1)} custom-call(s32[1]{0:T(128)} %bitcast.core_ref, bf16[256,256]{1,0:T(8,128)(2,1)} %copy.18.ctx_ref, bf16[256,12288]{1,0:T(8,128)(2,1)} %bitcast.39, bf16[256,12288]{1,0:T(8,128)(2,1)} %bitcast.40, bf16[256,12288]{1,0:T(8,128)(2,1)} %bitcast.41, bf16[256,12288]{1,0:T(8,128)(2,1)} %bitcast.42), custom_call_target="tpu_custom_call" | custom-call | tf_op jit(solution)/shard_map/pallas_call | solution.py:36
  86.2 4.5 %add_convert_fusion = bf16[16,256,384]{2,1,0:T(8,128)(2,1)} fusion(bf16[16,256,384]{2,1,0:T(8,128)(2,1)S(1)} %collective-permute-done.1, bf16[16,256,384]{2,1,0:T(8,128)(2,1)} %shard_map.56), kind=kLoop, calls=%fused_computation.1 | loop fusion | flops 6291456 | bytes 9437184 | tf_op jit(solution)/shard_map/convert_element_type | solution.py:122
  90.8 45.8 %reduce-scatter.2.cloned.1.call-done = bf16[1,2,256,384]{3,2,1,0:T(8,128)(2,1)} async-done(((bf16[8,2,256,384]{3,2,1,0:T(8,128)(2,1)}), bf16[1,2,256,384]{3,2,1,0:T(8,128)(2,1)}) %reduce-scatter.2.cloned.1.call-update) | async-done | bytes 393232 | tf_op jit(solution)/shard_map/reduce_scatter | solution.py:123
  136.6 1.0 fusion.4
  137.6 1.7 %collective-permute-start.2 = (bf16[256,384]{1,0:T(8,128)(2,1)S(1)}, bf16[256,384]{1,0:T(8,128)(2,1)S(1)}, u32[]{:S(2)}, u32[]{:S(2)}) collective-permute-start(bf16[256,384]{1,0:T(8,128)(2,1)S(1)} %fusion.4), channel_id=1, source_target_pairs={{0,128},{128,0},{1,129},{129,1},{2,130},{130,2},{3,131},{131,3},{4... | collective-permute-start | bytes 589832 | tf_op jit(solution)/shard_map/ppermute | solution.py:17
  139.3 0.9 dynamic-slice_bitcast_fusion
  140.2 2.2 %collective-permute-start.3 = (bf16[256,384]{1,0:T(8,128)(2,1)S(1)}, bf16[256,384]{1,0:T(8,128)(2,1)S(1)}, u32[]{:S(2)}, u32[]{:S(2)}) collective-permute-start(bf16[256,384]{1,0:T(8,128)(2,1)S(1)} %dynamic-slice_bitcast_fusion), channel_id=1, source_target_pairs={{0,130},{2,128},{128,2},{130,0},{1,131},{3,129},{129,3},{131,1},{4... | collective-permute-start | bytes 589832 | tf_op jit(solution)/shard_map/ppermute | solution.py:128
  142.4 1.0 collective-permute-done.2
  143.4 3.8 %collective-permute-done.3 = bf16[256,384]{1,0:T(8,128)(2,1)S(1)} collective-permute-done((bf16[256,384]{1,0:T(8,128)(2,1)S(1)}, bf16[256,384]{1,0:T(8,128)(2,1)S(1)}, u32[]{:S(2)}, u32[]{:S(2)}) %collective-permute-start.3) | collective-permute-done | bytes 196640 | tf_op jit(solution)/shard_map/ppermute | solution.py:128
  147.2 0.7 fusion.5
  (10 shorter events, 0.7 us)
Async XLA Ops:
  6.5 59.3 %all-gather.3.cloned.1.call-start = ((), (), s32[]{:S(2)}) async-start(), calls=%async_computation.2 | async-start | bytes 6684672 | tf_op jit(solution)/shard_map/all_gather | solution.py:95
  6.5 8.4 %collective-permute-start = (bf16[256,384]{1,0:T(8,128)(2,1)}, bf16[256,384]{1,0:T(8,128)(2,1)S(1)}, u32[]{:S(2)}, u32[]{:S(2)}) collective-permute-start(bf16[256,384]{1,0:T(8,128)(2,1)} %bitcast.44), channel_id=1, source_target_pairs={{0,2},{2,0},{1,3},{3,1},{4,6},{6,4},{5,7},{7,5},{8,10},{10,8},{9,1... | collective-permute-start | bytes 589832 | tf_op jit(solution)/shard_map/ppermute | solution.py:17
  16.7 119.9 %reduce-scatter.2.cloned.1.call-start = ((), (), s32[]{:S(2)}) async-start(), calls=%async_computation.1 | async-start | bytes 3538944 | tf_op jit(solution)/shard_map/reduce_scatter | solution.py:123
  80.4 5.9 %collective-permute-start.1 = (bf16[16,256,384]{2,1,0:T(8,128)(2,1)}, bf16[16,256,384]{2,1,0:T(8,128)(2,1)S(1)}, u32[]{:S(2)}, u32[]{:S(2)}) collective-permute-start(bf16[16,256,384]{2,1,0:T(8,128)(2,1)} %shard_map.57), channel_id=1, source_target_pairs={{0,1},{1,0},{2,3},{3,2},{4,5},{5,4},{6,7},{7,6},{8,9},{9,8},{10,11... | collective-permute-start | bytes 9437192 | tf_op jit(solution)/shard_map/ppermute | solution.py:17
  90.8 45.9 %copy-start = (bf16[1,256,384]{2,1,0:T(8,128)(2,1)S(1)}, bf16[1,256,384]{2,1,0:T(8,128)(2,1)}, u32[]{:S(2)}) copy-start(bf16[1,256,384]{2,1,0:T(8,128)(2,1)} %param.5) | copy-start | bytes 589828
  137.6 5.8 %collective-permute-start.2 = (bf16[256,384]{1,0:T(8,128)(2,1)S(1)}, bf16[256,384]{1,0:T(8,128)(2,1)S(1)}, u32[]{:S(2)}, u32[]{:S(2)}) collective-permute-start(bf16[256,384]{1,0:T(8,128)(2,1)S(1)} %fusion.4), channel_id=1, source_target_pairs={{0,128},{128,0},{1,129},{129,1},{2,130},{130,2},{3,131},{131,3},{4... | collective-permute-start | bytes 589832 | tf_op jit(solution)/shard_map/ppermute | solution.py:17
  140.2 7.0 %collective-permute-start.3 = (bf16[256,384]{1,0:T(8,128)(2,1)S(1)}, bf16[256,384]{1,0:T(8,128)(2,1)S(1)}, u32[]{:S(2)}, u32[]{:S(2)}) collective-permute-start(bf16[256,384]{1,0:T(8,128)(2,1)S(1)} %dynamic-slice_bitcast_fusion), channel_id=1, source_target_pairs={{0,130},{2,128},{128,2},{130,0},{1,131},{3,129},{129,3},{131,1},{4... | collective-permute-start | bytes 589832 | tf_op jit(solution)/shard_map/ppermute | solution.py:128
Sparse Core Ops, SparseCore 0:
  16.8 48.9 all-gather.2
  90.9 45.6 reduce-scatter.1

commit v8 on v7

--- a/solution.py
+++ b/solution.py
@@ -17,7 +17,7 @@
     return lax.ppermute(value, axis, [(0, 1), (1, 0)])
 
 
-def out_proj_kernel(core_ref, ctx_ref, *refs):
+def out_proj_kernel(sel_ref, ctx_ref, *refs):
     w_refs, o_ref = refs[:-1], refs[-1]
     ctx = ctx_ref[...]
     for k, w_ref in enumerate(w_refs):
@@ -25,14 +25,16 @@
         o_ref[k] = d.astype(jnp.bfloat16)
 
 
-def out_proj(core, context, weight_o, width):
+def out_proj(sel, context, weight_o, width):
     tokens, inner = context.shape
     n_groups = weight_o.shape[1] // (N_C * width)
     step = GROUPS_PER_STEP
-    w_specs = [
-        pl.BlockSpec((inner, width), lambda i, c, k=k: (0, N_C * (i * step + k) + c[0]))
-        for k in range(step)
-    ]
+
+    def w_index(i, c, k):
+        z = i * (step // N_Y) + k // N_Y
+        return (0, N_C * (z * N_Y + (k % N_Y + c[1]) % N_Y) + c[0])
+
+    w_specs = [pl.BlockSpec((inner, width), lambda i, c, k=k: w_index(i, c, k)) for k in range(step)]
     return pl.pallas_call(
         out_proj_kernel,
         out_shape=jax.ShapeDtypeStruct((n_groups, tokens, width), jnp.bfloat16),
@@ -42,10 +44,10 @@
             in_specs=[pl.BlockSpec((tokens, inner), lambda i, c: (0, 0))] + w_specs,
             out_specs=pl.BlockSpec((step, tokens, width), lambda i, c: (i, 0, 0)),
         ),
-    )(core, context, *([weight_o] * step))
+    )(sel, context, *([weight_o] * step))
 
 
-def gathered_proj_kernel(f_ref, *refs):
+def gathered_proj_kernel(y_ref, f_ref, *refs):
     w_refs, o_ref = refs[:-1], refs[-1]
 
     @pl.when(pl.program_id(0) == 0)
@@ -58,7 +60,7 @@
     o_ref[...] = acc
 
 
-def gathered_proj(feats, weight_v):
+def gathered_proj(y_index, feats, weight_v):
     tokens, width = feats.shape[-2:]
     feats = feats.reshape(-1, tokens, width)
     per_z = N_C * N_Y
@@ -66,7 +68,9 @@
     w_specs = [
         pl.BlockSpec(
             (width, weight_v.shape[1]),
-            lambda i, z=z, c=c, y=y: ((i * Z_PER_STEP + z) * per_z + y * N_C + c, 0),
+            lambda i, yi, z=z, c=c, y=y: (
+                (i * Z_PER_STEP + z) * per_z + ((y + yi[0]) % N_Y) * N_C + c, 0
+            ),
         )
         for z in range(Z_PER_STEP)
         for c in range(N_C)
@@ -75,10 +79,13 @@
     return pl.pallas_call(
         gathered_proj_kernel,
         out_shape=jax.ShapeDtypeStruct((tokens, weight_v.shape[1]), jnp.float32),
-        grid=(N_Z // Z_PER_STEP,),
-        in_specs=[pl.BlockSpec((step, tokens, width), lambda i: (i, 0, 0))] + w_specs,
-        out_specs=pl.BlockSpec((tokens, weight_v.shape[1]), lambda i: (0, 0)),
-    )(feats, *([weight_v] * step))
+        grid_spec=pltpu.PrefetchScalarGridSpec(
+            num_scalar_prefetch=1,
+            grid=(N_Z // Z_PER_STEP,),
+            in_specs=[pl.BlockSpec((step, tokens, width), lambda i, yi: (i, 0, 0))] + w_specs,
+            out_specs=pl.BlockSpec((tokens, weight_v.shape[1]), lambda i, yi: (0, 0)),
+        ),
+    )(y_index, feats, *([weight_v] * step))
 
 
 def on_device(inputs, queries, keys, w_value, w_out):
@@ -89,11 +96,10 @@
     col_width = activ.shape[1]
     n_feat = weight_v.shape[0]
 
-    y_first = lax.axis_index("ty") == 0
-    other = swap(activ, "ty")
-    gathered = jnp.stack([jnp.where(y_first, activ, other), jnp.where(y_first, other, activ)])
+    y_index = lax.axis_index("ty").astype(jnp.int32)
+    gathered = jnp.stack([activ, swap(activ, "ty")])
     gathered = lax.all_gather(gathered, ("tz", "tc"), axis=0)
-    values = gathered_proj(gathered, weight_v)
+    values = gathered_proj(y_index.reshape(1), gathered, weight_v)
     values = values.astype(jnp.bfloat16)
 
     heads_here = weight_v.shape[1] // HEAD_SIZE
@@ -114,16 +120,14 @@
     ).astype(jnp.bfloat16)
     context = context.reshape(length, heads_here * HEAD_SIZE)
 
-    core = lax.axis_index("tc").astype(jnp.int32).reshape(1)
-    sib = out_proj(1 - core, context, weight_o, col_width)
+    core = lax.axis_index("tc").astype(jnp.int32)
+    sib = out_proj(jnp.stack([1 - core, y_index]), context, weight_o, col_width)
     from_sib = swap(sib, "tc")
-    mine = out_proj(core, context, weight_o, col_width)
+    mine = out_proj(jnp.stack([core, y_index]), context, weight_o, col_width)
     part = mine.astype(jnp.float32) + from_sib.astype(jnp.float32)
     part = part.astype(jnp.bfloat16).reshape(N_Z, N_Y, length, col_width)
     part = lax.psum_scatter(part, "tz", scatter_dimension=0, tiled=False)
-    y_index = lax.axis_index("ty")
-    keep = lax.dynamic_index_in_dim(part, y_index, 0, keepdims=False)
-    send = lax.dynamic_index_in_dim(part, 1 - y_index, 0, keepdims=False)
+    keep, send = part[0], part[1]
     keep = (keep.astype(jnp.float32) + activ.astype(jnp.float32)).astype(jnp.bfloat16)
     across = lax.ppermute(send, ("section", "ty"), [(i, 3 - i) for i in range(4)])
     result = swap(keep, "section").astype(jnp.float32) + across.astype(jnp.float32)

time: 155 us -> 157 us (1.013)
  transfers between devices with their start and end apart: 6 -> 6, of which waited for: 6 -> 5; matrix products, arithmetic and copies ran while one was open for 2% -> 3% of each run, Pallas kernels for 3% -> 4%
where the time goes in v8:
time: 157 us
  waiting for transfers between devices  102 us (65%)
  Pallas kernels  19.3 us (12%)
  between operations  13.5 us (9%)
  other arithmetic  10.2 us (6%)
  starting transfers between devices  7.33 us (5%)
  local copies, waits for them, and re-layouts  3.69 us (2%)
    all_gather x1, waiting for transfers between devices, on_device(): gathered = lax.all_gather(gathered, ('tz', 'tc'), axis=0)  45.9 us
    reduce_scatter x1, waiting for transfers between devices, on_device(): part = lax.psum_scatter(part, 'tz', scatter_dimension=0, tiled=False)  45.8 us
    pallas_call x2, Pallas kernels, out_proj(): pl.pallas_call(out_proj_kernel, out_shape=jax.ShapeDtypeStruct((n_groups,...  12.2 us
    pallas_call x1, Pallas kernels, gathered_proj(): pl.pallas_call(gathered_proj_kernel, out_shape=jax.ShapeDtypeStruct((toke...  7.08 us
    ppermute x3, waiting for transfers between devices, swap(): return lax.ppermute(value, axis, [(0, 1), (1, 0)])  6.11 us
    ppermute x3, starting transfers between devices, swap(): return lax.ppermute(value, axis, [(0, 1), (1, 0)])  5.11 us
    convert_element_type x1, other arithmetic, on_device(): part = part.astype(jnp.bfloat16).reshape(N_Z, N_Y, length, col_width)  4.53 us
    ppermute x1, waiting for transfers between devices, on_device(): lax.ppermute(send, ('section', 'ty'), [(i, 3 - i) for i in range(4)])  3.84 us
  transfers between devices with their start and end apart: 6, of which 5 were waited for; matrix products, arithmetic and copies ran while one was open for 3% of the time, Pallas kernels for 4%

profile of v8, /device:TPU:2, one launch (start us, length us, event | category | flops | bytes accessed | tf_op | source)
XLA Modules:
  0.0 156.6 jit_solution(9345478105604535387)
XLA Ops:
  6.5 3.2 %collective-permute-start = (bf16[256,384]{1,0:T(8,128)(2,1)}, bf16[256,384]{1,0:T(8,128)(2,1)S(1)}, u32[]{:S(2)}, u32[]{:S(2)}) collective-permute-start(bf16[256,384]{1,0:T(8,128)(2,1)} %bitcast.43), channel_id=1, source_target_pairs={{0,2},{2,0},{1,3},{3,1},{4,6},{6,4},{5,7},{7,5},{8,10},{10,8},{9,1... | collective-permute-start | bytes 589832 | tf_op jit(solution)/shard_map/ppermute | solution.py:17
  9.7 5.2 %collective-permute-done = bf16[256,384]{1,0:T(8,128)(2,1)S(1)} collective-permute-done((bf16[256,384]{1,0:T(8,128)(2,1)}, bf16[256,384]{1,0:T(8,128)(2,1)S(1)}, u32[]{:S(2)}, u32[]{:S(2)}) %collective-permute-start) | collective-permute-done | bytes 196640 | tf_op jit(solution)/shard_map/ppermute | solution.py:17
  14.9 1.7 %pad_maximum_fusion = bf16[2,256,384]{2,1,0:T(8,128)(2,1)} fusion(bf16[1,256,384]{2,1,0:T(8,128)(2,1)S(1)} %bitcast.44, bf16[1,256,384]{2,1,0:T(8,128)(2,1)} %param.5), kind=kLoop, calls=%fused_computation.8 | loop fusion | flops 196608 | bytes 786432 | tf_op jit(solution)/shard_map/stack | solution.py:100
  16.7 0.9 reshape.61
  17.7 0.9 reshape.62
  18.6 0.6 pad_add_fusion.1.sel_ref
  19.3 0.3 fusion.15
  19.9 45.9 %all-gather.3.cloned.1.call-done.f_ref = bf16[32,256,384]{2,1,0:T(8,128)(2,1)} async-done(((bf16[2,256,384]{2,1,0:T(8,128)(2,1)}), bf16[32,256,384]{2,1,0:T(8,128)(2,1)}) %all-gather.3.cloned.1.call-update) | async-done | bytes 6291472 | tf_op jit(solution)/shard_map/all_gather | solution.py:101
  65.8 7.1 %shard_map.55 = f32[256,256]{1,0:T(8,128)} custom-call(s32[1]{0:T(128)} %bitcast.1.y_ref, bf16[32,256,384]{2,1,0:T(8,128)(2,1)} %all-gather.3.cloned.1.call-done.f_ref, bf16[12288,256]{1,0:T(8,128)(2,1)} %bitcast.26, bf16[12288,256]{1,0:T(8,128)(2,1)} %bitcast.27, bf16[12288,256]{1,0:T(8,128)(2,1)} %bitcast.28, bf16[12288,256]{1,0:T(8,128)(2,1)} %bitcast.29, ...), custom_call_target="tpu_custom_call" | custom-call | tf_op jit(solution)/shard_map/pallas_call | solution.py:79
  72.9 1.0 convert_element_type.46
  74.0 0.3 convolution_convert_fusion
  74.3 0.8 copy.18.ctx_ref
  75.0 6.1 %shard_map.57 = bf16[16,256,384]{2,1,0:T(8,128)(2,1)} custom-call(s32[2]{0:T(128)} %pad_add_fusion.1.sel_ref, bf16[256,256]{1,0:T(8,128)(2,1)} %copy.18.ctx_ref, bf16[256,12288]{1,0:T(8,128)(2,1)} %bitcast.34, bf16[256,12288]{1,0:T(8,128)(2,1)} %bitcast.35, bf16[256,12288]{1,0:T(8,128)(2,1)} %bitcast.36, bf16[256,12288]{1,0:T(8,128)(2,1)} %bitcast.37), custom_call_target="tpu_custom_call" | custom-call | tf_op jit(solution)/shard_map/pallas_call | solution.py:38
  81.3 0.6 pad_add_fusion.sel_ref
  81.9 6.1 %shard_map.56 = bf16[16,256,384]{2,1,0:T(8,128)(2,1)} custom-call(s32[2]{0:T(128)} %pad_add_fusion.sel_ref, bf16[256,256]{1,0:T(8,128)(2,1)} %copy.18.ctx_ref, bf16[256,12288]{1,0:T(8,128)(2,1)} %bitcast.38, bf16[256,12288]{1,0:T(8,128)(2,1)} %bitcast.39, bf16[256,12288]{1,0:T(8,128)(2,1)} %bitcast.40, bf16[256,12288]{1,0:T(8,128)(2,1)} %bitcast.41), custom_call_target="tpu_custom_call" | custom-call | tf_op jit(solution)/shard_map/pallas_call | solution.py:38
  88.0 4.5 %add_convert_fusion = bf16[16,256,384]{2,1,0:T(8,128)(2,1)} fusion(bf16[16,256,384]{2,1,0:T(8,128)(2,1)S(1)} %collective-permute-done.1, bf16[16,256,384]{2,1,0:T(8,128)(2,1)} %shard_map.56), kind=kLoop, calls=%fused_computation.1 | loop fusion | flops 6291456 | bytes 9437184 | tf_op jit(solution)/shard_map/convert_element_type | solution.py:128
  92.6 45.8 %reduce-scatter.2.cloned.1.call-done = bf16[1,2,256,384]{3,2,1,0:T(8,128)(2,1)} async-done(((bf16[8,2,256,384]{3,2,1,0:T(8,128)(2,1)}), bf16[1,2,256,384]{3,2,1,0:T(8,128)(2,1)}) %reduce-scatter.2.cloned.1.call-update) | async-done | bytes 393232 | tf_op jit(solution)/shard_map/reduce_scatter | solution.py:129
  138.4 1.0 fusion.4
  139.4 1.7 %collective-permute-start.2 = (bf16[256,384]{1,0:T(8,128)(2,1)S(1)}, bf16[256,384]{1,0:T(8,128)(2,1)S(1)}, u32[]{:S(2)}, u32[]{:S(2)}) collective-permute-start(bf16[256,384]{1,0:T(8,128)(2,1)S(1)} %fusion.4), channel_id=1, source_target_pairs={{0,128},{128,0},{1,129},{129,1},{2,130},{130,2},{3,131},{131,3},{4... | collective-permute-start | bytes 589832 | tf_op jit(solution)/shard_map/ppermute | solution.py:17
  141.1 0.9 slice_bitcast_fusion
  142.0 2.2 %collective-permute-start.3 = (bf16[256,384]{1,0:T(8,128)(2,1)S(1)}, bf16[256,384]{1,0:T(8,128)(2,1)S(1)}, u32[]{:S(2)}, u32[]{:S(2)}) collective-permute-start(bf16[256,384]{1,0:T(8,128)(2,1)S(1)} %slice_bitcast_fusion), channel_id=1, source_target_pairs={{0,130},{2,128},{128,2},{130,0},{1,131},{3,129},{129,3},{131,1},{4... | collective-permute-start | bytes 589832 | tf_op jit(solution)/shard_map/ppermute | solution.py:132
  144.2 0.9 collective-permute-done.2
  145.1 3.8 %collective-permute-done.3 = bf16[256,384]{1,0:T(8,128)(2,1)S(1)} collective-permute-done((bf16[256,384]{1,0:T(8,128)(2,1)S(1)}, bf16[256,384]{1,0:T(8,128)(2,1)S(1)}, u32[]{:S(2)}, u32[]{:S(2)}) %collective-permute-start.3) | collective-permute-done | bytes 196640 | tf_op jit(solution)/shard_map/ppermute | solution.py:132
  149.0 0.7 fusion.5
  (11 shorter events, 0.7 us)
Async XLA Ops:
  6.5 59.3 %all-gather.3.cloned.1.call-start = ((), (), s32[]{:S(2)}) async-start(), calls=%async_computation.2 | async-start | bytes 6684672 | tf_op jit(solution)/shard_map/all_gather | solution.py:101
  6.5 8.4 %collective-permute-start = (bf16[256,384]{1,0:T(8,128)(2,1)}, bf16[256,384]{1,0:T(8,128)(2,1)S(1)}, u32[]{:S(2)}, u32[]{:S(2)}) collective-permute-start(bf16[256,384]{1,0:T(8,128)(2,1)} %bitcast.43), channel_id=1, source_target_pairs={{0,2},{2,0},{1,3},{3,1},{4,6},{6,4},{5,7},{7,5},{8,10},{10,8},{9,1... | collective-permute-start | bytes 589832 | tf_op jit(solution)/shard_map/ppermute | solution.py:17
  16.7 121.7 %reduce-scatter.2.cloned.1.call-start = ((), (), s32[]{:S(2)}) async-start(), calls=%async_computation.1 | async-start | bytes 3538944 | tf_op jit(solution)/shard_map/reduce_scatter | solution.py:129
  81.1 6.9 %collective-permute-start.1 = (bf16[16,256,384]{2,1,0:T(8,128)(2,1)}, bf16[16,256,384]{2,1,0:T(8,128)(2,1)S(1)}, u32[]{:S(2)}, u32[]{:S(2)}) collective-permute-start(bf16[16,256,384]{2,1,0:T(8,128)(2,1)} %shard_map.57), channel_id=1, source_target_pairs={{0,1},{1,0},{2,3},{3,2},{4,5},{5,4},{6,7},{7,6},{8,9},{9,8},{10,11... | collective-permute-start | bytes 9437192 | tf_op jit(solution)/shard_map/ppermute | solution.py:17
  92.6 45.8 %copy-start = (bf16[1,256,384]{2,1,0:T(8,128)(2,1)S(1)}, bf16[1,256,384]{2,1,0:T(8,128)(2,1)}, u32[]{:S(2)}) copy-start(bf16[1,256,384]{2,1,0:T(8,128)(2,1)} %param.5) | copy-start | bytes 589828
  139.4 5.8 %collective-permute-start.2 = (bf16[256,384]{1,0:T(8,128)(2,1)S(1)}, bf16[256,384]{1,0:T(8,128)(2,1)S(1)}, u32[]{:S(2)}, u32[]{:S(2)}) collective-permute-start(bf16[256,384]{1,0:T(8,128)(2,1)S(1)} %fusion.4), channel_id=1, source_target_pairs={{0,128},{128,0},{1,129},{129,1},{2,130},{130,2},{3,131},{131,3},{4... | collective-permute-start | bytes 589832 | tf_op jit(solution)/shard_map/ppermute | solution.py:17
  142.0 7.0 %collective-permute-start.3 = (bf16[256,384]{1,0:T(8,128)(2,1)S(1)}, bf16[256,384]{1,0:T(8,128)(2,1)S(1)}, u32[]{:S(2)}, u32[]{:S(2)}) collective-permute-start(bf16[256,384]{1,0:T(8,128)(2,1)S(1)} %slice_bitcast_fusion), channel_id=1, source_target_pairs={{0,130},{2,128},{128,2},{130,0},{1,131},{3,129},{129,3},{131,1},{4... | collective-permute-start | bytes 589832 | tf_op jit(solution)/shard_map/ppermute | solution.py:132
Sparse Core Ops, SparseCore 0:
  16.8 48.9 all-gather.2
  92.7 45.6 reduce-scatter.1

commit v9 on v7

--- a/solution.py
+++ b/solution.py
@@ -17,32 +17,61 @@
     return lax.ppermute(value, axis, [(0, 1), (1, 0)])
 
 
-def out_proj_kernel(core_ref, ctx_ref, *refs):
+def column_spec(inner, width, step, k):
+    return pl.BlockSpec((inner, width), lambda i, c: (0, N_C * (i * step + k) + c[0]))
+
+
+def pick_kernel(sel_ref, *refs):
+    w_refs, o_ref = refs[:-1], refs[-1]
+    for k, w_ref in enumerate(w_refs):
+        o_ref[k] = w_ref[...]
+
+
+def pick_columns(sel, weight_o, width):
+    inner = weight_o.shape[0]
+    n_groups = weight_o.shape[1] // (N_C * width)
+    step = GROUPS_PER_STEP
+    return pl.pallas_call(
+        pick_kernel,
+        out_shape=jax.ShapeDtypeStruct((n_groups, inner, width), weight_o.dtype),
+        grid_spec=pltpu.PrefetchScalarGridSpec(
+            num_scalar_prefetch=1,
+            grid=(n_groups // step,),
+            in_specs=[column_spec(inner, width, step, k) for k in range(step)],
+            out_specs=pl.BlockSpec((step, inner, width), lambda i, c: (i, 0, 0)),
+        ),
+    )(sel, *([weight_o] * step))
+
+
+def out_proj_kernel(core_ref, ctx_ref, ctx_sib_ref, w_sib_ref, *refs):
     w_refs, o_ref = refs[:-1], refs[-1]
     ctx = ctx_ref[...]
+    ctx_sib = ctx_sib_ref[...]
     for k, w_ref in enumerate(w_refs):
         d = jnp.dot(ctx, w_ref[...], preferred_element_type=jnp.float32)
+        d = d + jnp.dot(ctx_sib, w_sib_ref[k], preferred_element_type=jnp.float32)
         o_ref[k] = d.astype(jnp.bfloat16)
 
 
-def out_proj(core, context, weight_o, width):
+def out_proj(core, context, context_sib, weight_sib, weight_o, width):
     tokens, inner = context.shape
     n_groups = weight_o.shape[1] // (N_C * width)
     step = GROUPS_PER_STEP
-    w_specs = [
-        pl.BlockSpec((inner, width), lambda i, c, k=k: (0, N_C * (i * step + k) + c[0]))
-        for k in range(step)
-    ]
     return pl.pallas_call(
         out_proj_kernel,
         out_shape=jax.ShapeDtypeStruct((n_groups, tokens, width), jnp.bfloat16),
         grid_spec=pltpu.PrefetchScalarGridSpec(
             num_scalar_prefetch=1,
             grid=(n_groups // step,),
-            in_specs=[pl.BlockSpec((tokens, inner), lambda i, c: (0, 0))] + w_specs,
+            in_specs=[
+                pl.BlockSpec((tokens, inner), lambda i, c: (0, 0)),
+                pl.BlockSpec((tokens, inner), lambda i, c: (0, 0)),
+                pl.BlockSpec((step, inner, width), lambda i, c: (i, 0, 0)),
+            ]
+            + [column_spec(inner, width, step, k) for k in range(step)],
             out_specs=pl.BlockSpec((step, tokens, width), lambda i, c: (i, 0, 0)),
         ),
-    )(core, context, *([weight_o] * step))
+    )(core, context, context_sib, weight_sib, *([weight_o] * step))
 
 
 def gathered_proj_kernel(f_ref, *refs):
@@ -89,6 +118,8 @@
     col_width = activ.shape[1]
     n_feat = weight_v.shape[0]
 
+    core = lax.axis_index("tc").astype(jnp.int32).reshape(1)
+    weight_from_sib = swap(pick_columns(1 - core, weight_o, col_width), "tc")
     y_first = lax.axis_index("ty") == 0
     other = swap(activ, "ty")
     gathered = jnp.stack([jnp.where(y_first, activ, other), jnp.where(y_first, other, activ)])
@@ -114,12 +145,8 @@
     ).astype(jnp.bfloat16)
     context = context.reshape(length, heads_here * HEAD_SIZE)
 
-    core = lax.axis_index("tc").astype(jnp.int32).reshape(1)
-    sib = out_proj(1 - core, context, weight_o, col_width)
-    from_sib = swap(sib, "tc")
-    mine = out_proj(core, context, weight_o, col_width)
-    part = mine.astype(jnp.float32) + from_sib.astype(jnp.float32)
-    part = part.astype(jnp.bfloat16).reshape(N_Z, N_Y, length, col_width)
+    part = out_proj(core, context, swap(context, "tc"), weight_from_sib, weight_o, col_width)
+    part = part.reshape(N_Z, N_Y, length, col_width)
     part = lax.psum_scatter(part, "tz", scatter_dimension=0, tiled=False)
     y_index = lax.axis_index("ty")
     keep = lax.dynamic_index_in_dim(part, y_index, 0, keepdims=False)

time: 155 us -> 149 us (0.961)
  other arithmetic: 9 us -> 4.45 us
  waiting for transfers between devices: 103 us -> 99.3 us
  matrix products: 0.86 us -> 2.85 us
    convert_element_type x1 -> x0, other arithmetic: 4.53 us -> none  [on_device(): part = part.astype(jnp.bfloat16).reshape(N_Z, N_Y, length, col_width)]
    pallas_call x0 -> x1, Pallas kernels: none -> 4.43 us  [pick_columns(): pl.pallas_call(pick_kernel, out_shape=jax.ShapeDtypeStruct((n_groups, inn...]
    all_gather x1, waiting for transfers between devices: 46.6 us -> 42.2 us  [on_device(): gathered = lax.all_gather(gathered, ('tz', 'tc'), axis=0)]
    pallas_call x2 -> x1, Pallas kernels: 10.8 us -> 6.57 us  [out_proj(): pl.pallas_call(out_proj_kernel, out_shape=jax.ShapeDtypeStruct((n_groups,...]
    ppermute x3 -> x4, waiting for transfers between devices: 6.36 us -> 7.35 us  [swap(): return lax.ppermute(value, axis, [(0, 1), (1, 0)])]
    ppermute x3 -> x4, starting transfers between devices: 5.09 us -> 5.23 us  [swap(): return lax.ppermute(value, axis, [(0, 1), (1, 0)])]
  transfers between devices with their start and end apart: 6 -> 7, of which waited for: 6 -> 6; matrix products, arithmetic and copies ran while one was open for 2% -> 4% of each run, Pallas kernels for 3% -> 8%
where the time goes in v9:
time: 149 us; the launch traced here: 148 us
  waiting for transfers between devices  99.3 us (67%)
  Pallas kernels  18 us (12%)
  between operations  13.5 us (9%)
  starting transfers between devices  7.43 us (5%)
  other arithmetic  4.45 us (3%)
  matrix products  2.85 us (2%)
  local copies, waits for them, and re-layouts  2.57 us (2%)
    reduce_scatter x1, waiting for transfers between devices, on_device(): part = lax.psum_scatter(part, 'tz', scatter_dimension=0, tiled=False)  45.8 us
    all_gather x1, waiting for transfers between devices, on_device(): gathered = lax.all_gather(gathered, ('tz', 'tc'), axis=0)  42.2 us
    ppermute x4, waiting for transfers between devices, swap(): return lax.ppermute(value, axis, [(0, 1), (1, 0)])  7.35 us
    pallas_call x1, Pallas kernels, gathered_proj(): pl.pallas_call(gathered_proj_kernel, out_shape=jax.ShapeDtypeStruct((toke...  7.03 us
    pallas_call x1, Pallas kernels, out_proj(): pl.pallas_call(out_proj_kernel, out_shape=jax.ShapeDtypeStruct((n_groups,...  6.57 us
    ppermute x4, starting transfers between devices, swap(): return lax.ppermute(value, axis, [(0, 1), (1, 0)])  5.23 us
    pallas_call x1, Pallas kernels, pick_columns(): pl.pallas_call(pick_kernel, out_shape=jax.ShapeDtypeStruct((n_groups, inn...  4.43 us
    ppermute x1, waiting for transfers between devices, on_device(): lax.ppermute(send, ('section', 'ty'), [(i, 3 - i) for i in range(4)])  3.87 us
  transfers between devices with their start and end apart: 7, of which 6 were waited for; matrix products, arithmetic and copies ran while one was open for 4% of the time, Pallas kernels for 8%

profile of v9, /device:TPU:2, one launch (start us, length us, event | category | flops | bytes accessed | tf_op | source)
XLA Modules:
  0.0 148.1 jit_solution(15396940851206349594)
XLA Ops:
  6.5 3.2 %collective-permute-start = (bf16[256,384]{1,0:T(8,128)(2,1)}, bf16[256,384]{1,0:T(8,128)(2,1)S(1)}, u32[]{:S(2)}, u32[]{:S(2)}) collective-permute-start(bf16[256,384]{1,0:T(8,128)(2,1)} %bitcast.44), channel_id=1, source_target_pairs={{0,2},{2,0},{1,3},{3,1},{4,6},{6,4},{5,7},{7,5},{8,10},{10,8},{9,1... | collective-permute-start | bytes 589832 | tf_op jit(solution)/shard_map/ppermute | solution.py:17
  9.7 5.2 %collective-permute-done = bf16[256,384]{1,0:T(8,128)(2,1)S(1)} collective-permute-done((bf16[256,384]{1,0:T(8,128)(2,1)}, bf16[256,384]{1,0:T(8,128)(2,1)S(1)}, u32[]{:S(2)}, u32[]{:S(2)}) %collective-permute-start) | collective-permute-done | bytes 196640 | tf_op jit(solution)/shard_map/ppermute | solution.py:17
  14.9 1.0 select_bitcast_fusion.1
  15.9 0.8 pad_maximum_fusion
  16.7 4.4 %shard_map.56 = bf16[16,256,384]{2,1,0:T(8,128)(2,1)} custom-call(s32[1]{0:T(128)S(6)} %sub.17.sel_ref, bf16[256,12288]{1,0:T(8,128)(2,1)} %bitcast.35, bf16[256,12288]{1,0:T(8,128)(2,1)} %bitcast.36, bf16[256,12288]{1,0:T(8,128)(2,1)} %bitcast.37, bf16[256,12288]{1,0:T(8,128)(2,1)} %bitcast.38), custom_call_target="tpu_custom_call" | custom-call | tf_op jit(solution)/shard_map/pallas_call | solution.py:34
  21.2 0.9 reshape.65
  22.2 0.3 fusion.15
  22.5 1.0 fusion.3
  23.6 42.2 %all-gather.3.cloned.1.call-done.f_ref = bf16[32,256,384]{2,1,0:T(8,128)(2,1)} async-done(((bf16[2,256,384]{2,1,0:T(8,128)(2,1)}), bf16[32,256,384]{2,1,0:T(8,128)(2,1)}) %all-gather.3.cloned.1.call-update) | async-done | bytes 6291472 | tf_op jit(solution)/shard_map/all_gather | solution.py:126
  65.8 7.0 %shard_map.55 = f32[256,256]{1,0:T(8,128)} custom-call(bf16[32,256,384]{2,1,0:T(8,128)(2,1)} %all-gather.3.cloned.1.call-done.f_ref, bf16[12288,256]{1,0:T(8,128)(2,1)} %bitcast.27, bf16[12288,256]{1,0:T(8,128)(2,1)} %bitcast.28, bf16[12288,256]{1,0:T(8,128)(2,1)} %bitcast.29, bf16[12288,256]{1,0:T(8,128)(2,1)} %bitcast.30, bf16[12288,256]{1,0:T(8,128)(2,1)} %bitcast.31, ...), custom_call_target="tpu_custom_call" | custom-call | tf_op jit(solution)/shard_map/pallas_call | solution.py:104
  72.9 1.0 convert_element_type.37
  73.9 1.5 convolution_convert_fusion
  75.5 0.3 collective-permute-start.1
  75.9 1.2 collective-permute-done.1.ctx_sib_ref
  77.1 0.4 copy-done
  77.5 6.6 %shard_map.57 = bf16[16,256,384]{2,1,0:T(8,128)(2,1)} custom-call(s32[1]{0:T(128)} %bitcast.core_ref, bf16[256,256]{1,0:T(8,128)(2,1)} %copy-done.2, bf16[256,256]{1,0:T(8,128)(2,1)} %collective-permute-done.1.ctx_sib_ref, bf16[16,256,384]{2,1,0:T(8,128)(2,1)} %copy-done, bf16[256,12288]{1,0:T(8,128)(2,1)} %bitcast.39, bf16[256,12288]{1,0:T(8,128)(2,1)} %bitcast.40, ...), custom_call_target="tpu_custom_call" | custom-call | tf_op jit(solution)/shard_map/pallas_call | solution.py:60
  84.1 45.8 %reduce-scatter.2.cloned.1.call-done = bf16[1,2,256,384]{3,2,1,0:T(8,128)(2,1)} async-done(((bf16[8,2,256,384]{3,2,1,0:T(8,128)(2,1)}), bf16[1,2,256,384]{3,2,1,0:T(8,128)(2,1)}) %reduce-scatter.2.cloned.1.call-update) | async-done | bytes 393232 | tf_op jit(solution)/shard_map/reduce_scatter | solution.py:150
  130.0 1.0 fusion.4
  130.9 1.7 %collective-permute-start.3 = (bf16[256,384]{1,0:T(8,128)(2,1)S(1)}, bf16[256,384]{1,0:T(8,128)(2,1)S(1)}, u32[]{:S(2)}, u32[]{:S(2)}) collective-permute-start(bf16[256,384]{1,0:T(8,128)(2,1)S(1)} %fusion.4), channel_id=1, source_target_pairs={{0,128},{128,0},{1,129},{129,1},{2,130},{130,2},{3,131},{131,3},{4... | collective-permute-start | bytes 589832 | tf_op jit(solution)/shard_map/ppermute | solution.py:17
  132.6 0.9 dynamic-slice_bitcast_fusion
  133.6 2.2 %collective-permute-start.4 = (bf16[256,384]{1,0:T(8,128)(2,1)S(1)}, bf16[256,384]{1,0:T(8,128)(2,1)S(1)}, u32[]{:S(2)}, u32[]{:S(2)}) collective-permute-start(bf16[256,384]{1,0:T(8,128)(2,1)S(1)} %dynamic-slice_bitcast_fusion), channel_id=1, source_target_pairs={{0,130},{2,128},{128,2},{130,0},{1,131},{3,129},{129,3},{131,1},{4... | collective-permute-start | bytes 589832 | tf_op jit(solution)/shard_map/ppermute | solution.py:155
  135.7 0.9 collective-permute-done.3
  136.7 3.9 %collective-permute-done.4 = bf16[256,384]{1,0:T(8,128)(2,1)S(1)} collective-permute-done((bf16[256,384]{1,0:T(8,128)(2,1)S(1)}, bf16[256,384]{1,0:T(8,128)(2,1)S(1)}, u32[]{:S(2)}, u32[]{:S(2)}) %collective-permute-start.4) | collective-permute-done | bytes 196640 | tf_op jit(solution)/shard_map/ppermute | solution.py:155
  140.6 0.7 fusion.5
  (17 shorter events, 0.4 us)
Async XLA Ops:
  6.5 59.3 %all-gather.3.cloned.1.call-start = ((), (), s32[]{:S(2)}) async-start(), calls=%async_computation.2 | async-start | bytes 6684672 | tf_op jit(solution)/shard_map/all_gather | solution.py:126
  6.5 8.4 %collective-permute-start = (bf16[256,384]{1,0:T(8,128)(2,1)}, bf16[256,384]{1,0:T(8,128)(2,1)S(1)}, u32[]{:S(2)}, u32[]{:S(2)}) collective-permute-start(bf16[256,384]{1,0:T(8,128)(2,1)} %bitcast.44), channel_id=1, source_target_pairs={{0,2},{2,0},{1,3},{3,1},{4,6},{6,4},{5,7},{7,5},{8,10},{10,8},{9,1... | collective-permute-start | bytes 589832 | tf_op jit(solution)/shard_map/ppermute | solution.py:17
  16.7 113.3 %reduce-scatter.2.cloned.1.call-start = ((), (), s32[]{:S(2)}) async-start(), calls=%async_computation.1 | async-start | bytes 3538944 | tf_op jit(solution)/shard_map/reduce_scatter | solution.py:150
  16.7 4.5 %copy-start.3 = (bf16[1,256,256]{2,1,0:T(8,128)(2,1)S(1)}, bf16[1,256,256]{2,1,0:T(8,128)(2,1)}, u32[]{:S(2)}) copy-start(bf16[1,256,256]{2,1,0:T(8,128)(2,1)} %param.6) | copy-start | bytes 393220
  21.2 54.7 %collective-permute-start.2 = (bf16[16,256,384]{2,1,0:T(8,128)(2,1)}, bf16[16,256,384]{2,1,0:T(8,128)(2,1)S(1)}, u32[]{:S(2)}, u32[]{:S(2)}) collective-permute-start(bf16[16,256,384]{2,1,0:T(8,128)(2,1)} %shard_map.56), channel_id=1, source_target_pairs={{0,1},{1,0},{2,3},{3,2},{4,5},{5,4},{6,7},{7,6},{8,9},{9,8},{10,11... | collective-permute-start | bytes 9437192 | tf_op jit(solution)/shard_map/ppermute | solution.py:17
  75.5 1.6 %copy-start.2 = (bf16[256,256]{1,0:T(8,128)(2,1)}, bf16[256,256]{1,0:T(8,128)(2,1)S(1)}, u32[]{:S(2)}) copy-start(bf16[256,256]{1,0:T(8,128)(2,1)S(1)} %copy.18.ctx_ref) | copy-start | bytes 393220
  75.5 54.4 %copy-start.1 = (bf16[1,256,384]{2,1,0:T(8,128)(2,1)S(1)}, bf16[1,256,384]{2,1,0:T(8,128)(2,1)}, u32[]{:S(2)}) copy-start(bf16[1,256,384]{2,1,0:T(8,128)(2,1)} %param.5) | copy-start | bytes 589828
  75.5 1.6 %collective-permute-start.1 = (bf16[256,256]{1,0:T(8,128)(2,1)S(1)}, bf16[256,256]{1,0:T(8,128)(2,1)}, u32[]{:S(2)}, u32[]{:S(2)}) collective-permute-start(bf16[256,256]{1,0:T(8,128)(2,1)S(1)} %copy.18.ctx_ref), channel_id=1, source_target_pairs={{0,1},{1,0},{2,3},{3,2},{4,5},{5,4},{6,7},{7,6},{8,9},{9,8},{10,11... | collective-permute-start | bytes 393224 | tf_op jit(solution)/shard_map/ppermute | solution.py:17
  75.9 1.7 %copy-start = (bf16[16,256,384]{2,1,0:T(8,128)(2,1)}, bf16[16,256,384]{2,1,0:T(8,128)(2,1)S(1)}, u32[]{:S(2)}) copy-start(bf16[16,256,384]{2,1,0:T(8,128)(2,1)S(1)} %collective-permute-done.2.w_sib_ref) | copy-start | bytes 9437188
  130.9 5.8 %collective-permute-start.3 = (bf16[256,384]{1,0:T(8,128)(2,1)S(1)}, bf16[256,384]{1,0:T(8,128)(2,1)S(1)}, u32[]{:S(2)}, u32[]{:S(2)}) collective-permute-start(bf16[256,384]{1,0:T(8,128)(2,1)S(1)} %fusion.4), channel_id=1, source_target_pairs={{0,128},{128,0},{1,129},{129,1},{2,130},{130,2},{3,131},{131,3},{4... | collective-permute-start | bytes 589832 | tf_op jit(solution)/shard_map/ppermute | solution.py:17
  133.6 7.0 %collective-permute-start.4 = (bf16[256,384]{1,0:T(8,128)(2,1)S(1)}, bf16[256,384]{1,0:T(8,128)(2,1)S(1)}, u32[]{:S(2)}, u32[]{:S(2)}) collective-permute-start(bf16[256,384]{1,0:T(8,128)(2,1)S(1)} %dynamic-slice_bitcast_fusion), channel_id=1, source_target_pairs={{0,130},{2,128},{128,2},{130,0},{1,131},{3,129},{129,3},{131,1},{4... | collective-permute-start | bytes 589832 | tf_op jit(solution)/shard_map/ppermute | solution.py:155
Sparse Core Ops, SparseCore 0:
  16.8 48.9 all-gather.2
  84.3 45.6 reduce-scatter.1

commit v10 on v9

--- a/solution.py
+++ b/solution.py
@@ -9,8 +9,8 @@
 HEAD_SIZE = 128
 LEN = 256
 N_Z, N_Y, N_C = 8, 2, 2
-GROUPS_PER_STEP = 4
-Z_PER_STEP = 2
+GROUPS_PER_STEP = 8
+Z_PER_STEP = 4
 
 
 def swap(value, axis):

time: 149 us -> 148 us (level)
  waiting for transfers between devices: 99.3 us -> 101 us
  Pallas kernels: 18 us -> 16.3 us
  transfers between devices with their start and end apart: 7 -> 7, of which waited for: 6 -> 6; matrix products, arithmetic and copies ran while one was open for 4% -> 4% of each run, Pallas kernels for 8% -> 7%
where the time goes in v10:
time: 148 us; the launch traced here: 147 us
  waiting for transfers between devices  101 us (68%)
  Pallas kernels  16.3 us (11%)
  between operations  13.5 us (9%)
  starting transfers between devices  7.2 us (5%)
  other arithmetic  4.45 us (3%)
  matrix products  2.85 us (2%)
  local copies, waits for them, and re-layouts  2.58 us (2%)
    reduce_scatter x1, waiting for transfers between devices, on_device(): part = lax.psum_scatter(part, 'tz', scatter_dimension=0, tiled=False)  45.9 us
    all_gather x1, waiting for transfers between devices, on_device(): gathered = lax.all_gather(gathered, ('tz', 'tc'), axis=0)  43.3 us
    ppermute x4, waiting for transfers between devices, swap(): return lax.ppermute(value, axis, [(0, 1), (1, 0)])  7.57 us
    pallas_call x1, Pallas kernels, gathered_proj(): pl.pallas_call(gathered_proj_kernel, out_shape=jax.ShapeDtypeStruct((toke...  6.8 us
    pallas_call x1, Pallas kernels, out_proj(): pl.pallas_call(out_proj_kernel, out_shape=jax.ShapeDtypeStruct((n_groups,...  6.12 us
    ppermute x4, starting transfers between devices, swap(): return lax.ppermute(value, axis, [(0, 1), (1, 0)])  5.09 us
    ppermute x1, waiting for transfers between devices, on_device(): lax.ppermute(send, ('section', 'ty'), [(i, 3 - i) for i in range(4)])  3.73 us
    pallas_call x1, Pallas kernels, pick_columns(): pl.pallas_call(pick_kernel, out_shape=jax.ShapeDtypeStruct((n_groups, inn...  3.43 us
  transfers between devices with their start and end apart: 7, of which 6 were waited for; matrix products, arithmetic and copies ran while one was open for 4% of the time, Pallas kernels for 7%

profile of v10, /device:TPU:2, one launch (start us, length us, event | category | flops | bytes accessed | tf_op | source)
XLA Modules:
  0.0 147.4 jit_solution(14468147928923030305)
XLA Ops:
  6.5 3.2 %collective-permute-start = (bf16[256,384]{1,0:T(8,128)(2,1)}, bf16[256,384]{1,0:T(8,128)(2,1)S(1)}, u32[]{:S(2)}, u32[]{:S(2)}) collective-permute-start(bf16[256,384]{1,0:T(8,128)(2,1)} %bitcast.60), channel_id=1, source_target_pairs={{0,2},{2,0},{1,3},{3,1},{4,6},{6,4},{5,7},{7,5},{8,10},{10,8},{9,1... | collective-permute-start | bytes 589832 | tf_op jit(solution)/shard_map/ppermute | solution.py:17
  9.7 5.2 %collective-permute-done = bf16[256,384]{1,0:T(8,128)(2,1)S(1)} collective-permute-done((bf16[256,384]{1,0:T(8,128)(2,1)}, bf16[256,384]{1,0:T(8,128)(2,1)S(1)}, u32[]{:S(2)}, u32[]{:S(2)}) %collective-permute-start) | collective-permute-done | bytes 196640 | tf_op jit(solution)/shard_map/ppermute | solution.py:17
  14.9 1.0 select_bitcast_fusion.1
  15.9 0.8 pad_maximum_fusion
  16.7 3.4 %shard_map.56 = bf16[16,256,384]{2,1,0:T(8,128)(2,1)} custom-call(s32[1]{0:T(128)S(6)} %sub.17.sel_ref, bf16[256,12288]{1,0:T(8,128)(2,1)} %bitcast.43, bf16[256,12288]{1,0:T(8,128)(2,1)} %bitcast.44, bf16[256,12288]{1,0:T(8,128)(2,1)} %bitcast.45, bf16[256,12288]{1,0:T(8,128)(2,1)} %bitcast.46, bf16[256,12288]{1,0:T(8,128)(2,1)} %bitcast.47, ...), custom_call_target="tpu_custom_call" | custom-call | tf_op jit(solution)/shard_map/pallas_call | solution.py:34
  20.2 0.9 reshape.65
  21.2 0.3 fusion.15
  21.5 1.0 fusion.3
  22.6 43.3 %all-gather.3.cloned.1.call-done.f_ref = bf16[32,256,384]{2,1,0:T(8,128)(2,1)} async-done(((bf16[2,256,384]{2,1,0:T(8,128)(2,1)}), bf16[32,256,384]{2,1,0:T(8,128)(2,1)}) %all-gather.3.cloned.1.call-update) | async-done | bytes 6291472 | tf_op jit(solution)/shard_map/all_gather | solution.py:126
  65.8 6.8 %shard_map.55 = f32[256,256]{1,0:T(8,128)} custom-call(bf16[32,256,384]{2,1,0:T(8,128)(2,1)} %all-gather.3.cloned.1.call-done.f_ref, bf16[12288,256]{1,0:T(8,128)(2,1)} %bitcast.27, bf16[12288,256]{1,0:T(8,128)(2,1)} %bitcast.28, bf16[12288,256]{1,0:T(8,128)(2,1)} %bitcast.29, bf16[12288,256]{1,0:T(8,128)(2,1)} %bitcast.30, bf16[12288,256]{1,0:T(8,128)(2,1)} %bitcast.31, ...), custom_call_target="tpu_custom_call" | custom-call | tf_op jit(solution)/shard_map/pallas_call | solution.py:104
  72.6 1.0 convert_element_type.37
  73.7 1.5 %convolution_convert_fusion = bf16[2,128,256]{2,1,0:T(8,128)(2,1)S(1)} fusion(bf16[256,2,128]{0,2,1:T(8,128)(2,1)S(1)} %bitcast.61, f32[2,256]{1,0:T(2,128)S(1)} %fusion.15, f32[2,256,256]{1,2,0:T(8,128)} %fusion.3), kind=kOutput, calls=%fused_computation.5 | convolution fusion | flops 34013952 | bytes 788480 | tf_op jit(solution)/shard_map/bhqk,bkhd->bqhd/dot_general | solution.py:143
  75.3 0.3 collective-permute-start.1
  75.6 1.2 collective-permute-done.1.ctx_sib_ref
  76.9 0.4 copy-done
  77.3 6.1 %shard_map.57 = bf16[16,256,384]{2,1,0:T(8,128)(2,1)} custom-call(s32[1]{0:T(128)} %bitcast.core_ref, bf16[256,256]{1,0:T(8,128)(2,1)} %copy-done.2, bf16[256,256]{1,0:T(8,128)(2,1)} %collective-permute-done.1.ctx_sib_ref, bf16[16,256,384]{2,1,0:T(8,128)(2,1)} %copy-done, bf16[256,12288]{1,0:T(8,128)(2,1)} %bitcast.51, bf16[256,12288]{1,0:T(8,128)(2,1)} %bitcast.52, ...), custom_call_target="tpu_custom_call" | custom-call | tf_op jit(solution)/shard_map/pallas_call | solution.py:60
  83.5 45.9 %reduce-scatter.2.cloned.1.call-done = bf16[1,2,256,384]{3,2,1,0:T(8,128)(2,1)} async-done(((bf16[8,2,256,384]{3,2,1,0:T(8,128)(2,1)}), bf16[1,2,256,384]{3,2,1,0:T(8,128)(2,1)}) %reduce-scatter.2.cloned.1.call-update) | async-done | bytes 393232 | tf_op jit(solution)/shard_map/reduce_scatter | solution.py:150
  129.4 1.0 fusion.4
  130.4 1.6 %collective-permute-start.3 = (bf16[256,384]{1,0:T(8,128)(2,1)S(1)}, bf16[256,384]{1,0:T(8,128)(2,1)S(1)}, u32[]{:S(2)}, u32[]{:S(2)}) collective-permute-start(bf16[256,384]{1,0:T(8,128)(2,1)S(1)} %fusion.4), channel_id=1, source_target_pairs={{0,128},{128,0},{1,129},{129,1},{2,130},{130,2},{3,131},{131,3},{4... | collective-permute-start | bytes 589832 | tf_op jit(solution)/shard_map/ppermute | solution.py:17
  131.9 0.9 dynamic-slice_bitcast_fusion
  132.9 2.1 %collective-permute-start.4 = (bf16[256,384]{1,0:T(8,128)(2,1)S(1)}, bf16[256,384]{1,0:T(8,128)(2,1)S(1)}, u32[]{:S(2)}, u32[]{:S(2)}) collective-permute-start(bf16[256,384]{1,0:T(8,128)(2,1)S(1)} %dynamic-slice_bitcast_fusion), channel_id=1, source_target_pairs={{0,130},{2,128},{128,2},{130,0},{1,131},{3,129},{129,3},{131,1},{4... | collective-permute-start | bytes 589832 | tf_op jit(solution)/shard_map/ppermute | solution.py:155
  135.0 1.2 collective-permute-done.3
  136.1 3.7 %collective-permute-done.4 = bf16[256,384]{1,0:T(8,128)(2,1)S(1)} collective-permute-done((bf16[256,384]{1,0:T(8,128)(2,1)S(1)}, bf16[256,384]{1,0:T(8,128)(2,1)S(1)}, u32[]{:S(2)}, u32[]{:S(2)}) %collective-permute-start.4) | collective-permute-done | bytes 196640 | tf_op jit(solution)/shard_map/ppermute | solution.py:155
  139.9 0.7 fusion.5
  (17 shorter events, 0.4 us)
Async XLA Ops:
  6.5 59.3 %all-gather.3.cloned.1.call-start = ((), (), s32[]{:S(2)}) async-start(), calls=%async_computation.2 | async-start | bytes 6684672 | tf_op jit(solution)/shard_map/all_gather | solution.py:126
  6.5 8.4 %collective-permute-start = (bf16[256,384]{1,0:T(8,128)(2,1)}, bf16[256,384]{1,0:T(8,128)(2,1)S(1)}, u32[]{:S(2)}, u32[]{:S(2)}) collective-permute-start(bf16[256,384]{1,0:T(8,128)(2,1)} %bitcast.60), channel_id=1, source_target_pairs={{0,2},{2,0},{1,3},{3,1},{4,6},{6,4},{5,7},{7,5},{8,10},{10,8},{9,1... | collective-permute-start | bytes 589832 | tf_op jit(solution)/shard_map/ppermute | solution.py:17
  16.7 112.7 %reduce-scatter.2.cloned.1.call-start = ((), (), s32[]{:S(2)}) async-start(), calls=%async_computation.1 | async-start | bytes 3538944 | tf_op jit(solution)/shard_map/reduce_scatter | solution.py:150
  16.7 3.4 %copy-start.3 = (bf16[1,256,256]{2,1,0:T(8,128)(2,1)S(1)}, bf16[1,256,256]{2,1,0:T(8,128)(2,1)}, u32[]{:S(2)}) copy-start(bf16[1,256,256]{2,1,0:T(8,128)(2,1)} %param.6) | copy-start | bytes 393220
  20.2 55.5 %collective-permute-start.2 = (bf16[16,256,384]{2,1,0:T(8,128)(2,1)}, bf16[16,256,384]{2,1,0:T(8,128)(2,1)S(1)}, u32[]{:S(2)}, u32[]{:S(2)}) collective-permute-start(bf16[16,256,384]{2,1,0:T(8,128)(2,1)} %shard_map.56), channel_id=1, source_target_pairs={{0,1},{1,0},{2,3},{3,2},{4,5},{5,4},{6,7},{7,6},{8,9},{9,8},{10,11... | collective-permute-start | bytes 9437192 | tf_op jit(solution)/shard_map/ppermute | solution.py:17
  75.3 1.6 %copy-start.2 = (bf16[256,256]{1,0:T(8,128)(2,1)}, bf16[256,256]{1,0:T(8,128)(2,1)S(1)}, u32[]{:S(2)}) copy-start(bf16[256,256]{1,0:T(8,128)(2,1)S(1)} %copy.18.ctx_ref) | copy-start | bytes 393220
  75.3 54.1 %copy-start.1 = (bf16[1,256,384]{2,1,0:T(8,128)(2,1)S(1)}, bf16[1,256,384]{2,1,0:T(8,128)(2,1)}, u32[]{:S(2)}) copy-start(bf16[1,256,384]{2,1,0:T(8,128)(2,1)} %param.5) | copy-start | bytes 589828
  75.3 1.6 %collective-permute-start.1 = (bf16[256,256]{1,0:T(8,128)(2,1)S(1)}, bf16[256,256]{1,0:T(8,128)(2,1)}, u32[]{:S(2)}, u32[]{:S(2)}) collective-permute-start(bf16[256,256]{1,0:T(8,128)(2,1)S(1)} %copy.18.ctx_ref), channel_id=1, source_target_pairs={{0,1},{1,0},{2,3},{3,2},{4,5},{5,4},{6,7},{7,6},{8,9},{9,8},{10,11... | collective-permute-start | bytes 393224 | tf_op jit(solution)/shard_map/ppermute | solution.py:17
  75.6 1.7 %copy-start = (bf16[16,256,384]{2,1,0:T(8,128)(2,1)}, bf16[16,256,384]{2,1,0:T(8,128)(2,1)S(1)}, u32[]{:S(2)}) copy-start(bf16[16,256,384]{2,1,0:T(8,128)(2,1)S(1)} %collective-permute-done.2.w_sib_ref) | copy-start | bytes 9437188
  130.4 5.8 %collective-permute-start.3 = (bf16[256,384]{1,0:T(8,128)(2,1)S(1)}, bf16[256,384]{1,0:T(8,128)(2,1)S(1)}, u32[]{:S(2)}, u32[]{:S(2)}) collective-permute-start(bf16[256,384]{1,0:T(8,128)(2,1)S(1)} %fusion.4), channel_id=1, source_target_pairs={{0,128},{128,0},{1,129},{129,1},{2,130},{130,2},{3,131},{131,3},{4... | collective-permute-start | bytes 589832 | tf_op jit(solution)/shard_map/ppermute | solution.py:17
  132.9 7.0 %collective-permute-start.4 = (bf16[256,384]{1,0:T(8,128)(2,1)S(1)}, bf16[256,384]{1,0:T(8,128)(2,1)S(1)}, u32[]{:S(2)}, u32[]{:S(2)}) collective-permute-start(bf16[256,384]{1,0:T(8,128)(2,1)S(1)} %dynamic-slice_bitcast_fusion), channel_id=1, source_target_pairs={{0,130},{2,128},{128,2},{130,0},{1,131},{3,129},{129,3},{131,1},{4... | collective-permute-start | bytes 589832 | tf_op jit(solution)/shard_map/ppermute | solution.py:155
Sparse Core Ops, SparseCore 0:
  16.8 48.9 all-gather.2
  83.6 45.7 reduce-scatter.1

commit v11 on v10

--- a/solution.py
+++ b/solution.py
@@ -43,17 +43,20 @@
     )(sel, *([weight_o] * step))
 
 
-def out_proj_kernel(core_ref, ctx_ref, ctx_sib_ref, w_sib_ref, *refs):
+def out_proj_kernel(sel_ref, ctx_ref, ctx_sib_ref, w_sib_ref, activ_ref, *refs):
     w_refs, o_ref = refs[:-1], refs[-1]
     ctx = ctx_ref[...]
     ctx_sib = ctx_sib_ref[...]
+    activ = activ_ref[...].astype(jnp.float32)
+    first = pl.program_id(0) * len(w_refs)
     for k, w_ref in enumerate(w_refs):
         d = jnp.dot(ctx, w_ref[...], preferred_element_type=jnp.float32)
         d = d + jnp.dot(ctx_sib, w_sib_ref[k], preferred_element_type=jnp.float32)
+        d = d + jnp.where(first + k == sel_ref[1], activ, jnp.zeros_like(activ))
         o_ref[k] = d.astype(jnp.bfloat16)
 
 
-def out_proj(core, context, context_sib, weight_sib, weight_o, width):
+def out_proj(sel, context, context_sib, weight_sib, activ, weight_o, width):
     tokens, inner = context.shape
     n_groups = weight_o.shape[1] // (N_C * width)
     step = GROUPS_PER_STEP
@@ -67,24 +70,29 @@
                 pl.BlockSpec((tokens, inner), lambda i, c: (0, 0)),
                 pl.BlockSpec((tokens, inner), lambda i, c: (0, 0)),
                 pl.BlockSpec((step, inner, width), lambda i, c: (i, 0, 0)),
+                pl.BlockSpec((tokens, width), lambda i, c: (0, 0)),
             ]
             + [column_spec(inner, width, step, k) for k in range(step)],
             out_specs=pl.BlockSpec((step, tokens, width), lambda i, c: (i, 0, 0)),
         ),
-    )(core, context, context_sib, weight_sib, *([weight_o] * step))
+    )(sel, context, context_sib, weight_sib, activ, *([weight_o] * step))
 
 
 def gathered_proj_kernel(f_ref, *refs):
-    w_refs, o_ref = refs[:-1], refs[-1]
+    w_refs, o_ref, acc_ref = refs[:-2], refs[-2], refs[-1]
 
     @pl.when(pl.program_id(0) == 0)
     def _():
-        o_ref[...] = jnp.zeros(o_ref.shape, o_ref.dtype)
+        acc_ref[...] = jnp.zeros(acc_ref.shape, acc_ref.dtype)
 
-    acc = o_ref[...]
+    acc = acc_ref[...]
     for k, w_ref in enumerate(w_refs):
         acc = acc + jnp.dot(f_ref[k], w_ref[...], preferred_element_type=jnp.float32)
-    o_ref[...] = acc
+    acc_ref[...] = acc
+
+    @pl.when(pl.program_id(0) == pl.num_programs(0) - 1)
+    def _():
+        o_ref[...] = acc.astype(o_ref.dtype)
 
 
 def gathered_proj(feats, weight_v):
@@ -103,8 +111,9 @@
     ]
     return pl.pallas_call(
         gathered_proj_kernel,
-        out_shape=jax.ShapeDtypeStruct((tokens, weight_v.shape[1]), jnp.float32),
+        out_shape=jax.ShapeDtypeStruct((tokens, weight_v.shape[1]), jnp.bfloat16),
         grid=(N_Z // Z_PER_STEP,),
+        scratch_shapes=[pltpu.VMEM((tokens, weight_v.shape[1]), jnp.float32)],
         in_specs=[pl.BlockSpec((step, tokens, width), lambda i: (i, 0, 0))] + w_specs,
         out_specs=pl.BlockSpec((tokens, weight_v.shape[1]), lambda i: (0, 0)),
     )(feats, *([weight_v] * step))
@@ -125,7 +134,6 @@
     gathered = jnp.stack([jnp.where(y_first, activ, other), jnp.where(y_first, other, activ)])
     gathered = lax.all_gather(gathered, ("tz", "tc"), axis=0)
     values = gathered_proj(gathered, weight_v)
-    values = values.astype(jnp.bfloat16)
 
     heads_here = weight_v.shape[1] // HEAD_SIZE
     query_rows = queries[0].reshape(length // LEN, LEN, heads_here, HEAD_SIZE)
@@ -145,13 +153,14 @@
     ).astype(jnp.bfloat16)
     context = context.reshape(length, heads_here * HEAD_SIZE)
 
-    part = out_proj(core, context, swap(context, "tc"), weight_from_sib, weight_o, col_width)
+    y_index = lax.axis_index("ty")
+    own_group = (lax.axis_index("tz") * N_Y + y_index).astype(jnp.int32)
+    sel = jnp.concatenate([core, own_group.reshape(1)])
+    part = out_proj(sel, context, swap(context, "tc"), weight_from_sib, activ, weight_o, col_width)
     part = part.reshape(N_Z, N_Y, length, col_width)
     part = lax.psum_scatter(part, "tz", scatter_dimension=0, tiled=False)
-    y_index = lax.axis_index("ty")
     keep = lax.dynamic_index_in_dim(part, y_index, 0, keepdims=False)
     send = lax.dynamic_index_in_dim(part, 1 - y_index, 0, keepdims=False)
-    keep = (keep.astype(jnp.float32) + activ.astype(jnp.float32)).astype(jnp.bfloat16)
     across = lax.ppermute(send, ("section", "ty"), [(i, 3 - i) for i in range(4)])
     result = swap(keep, "section").astype(jnp.float32) + across.astype(jnp.float32)
     return result.astype(jnp.bfloat16)[None]

time: 148 us -> 149 us (level)
  local copies, waits for them, and re-layouts: 2.58 us -> 4.15 us
    convert_element_type x2 -> x0, other arithmetic: 1.94 us -> none  [the longest x1 0.98 us: on_device(): (keep.astype(jnp.float32) + activ.astype(jnp.float32)).astype(jnp.bfloat16)]
  transfers between devices with their start and end apart: 7 -> 7, of which waited for: 6 -> 6; matrix products, arithmetic and copies ran while one was open for 4% -> 3% of each run, Pallas kernels for 7% -> 7%
where the time goes in v11:
time: 149 us; the launch traced here: 148 us
  waiting for transfers between devices  100 us (67%)
  Pallas kernels  17.1 us (11%)
  between operations  13.5 us (9%)
  starting transfers between devices  7.42 us (5%)
  local copies, waits for them, and re-layouts  4.15 us (3%)
  other arithmetic  3.18 us (2%)
  matrix products  2.86 us (2%)
    reduce_scatter x1, waiting for transfers between devices, on_device(): part = lax.psum_scatter(part, 'tz', scatter_dimension=0, tiled=False)  45.7 us
    all_gather x1, waiting for transfers between devices, on_device(): gathered = lax.all_gather(gathered, ('tz', 'tc'), axis=0)  44.1 us
    ppermute x4, waiting for transfers between devices, swap(): return lax.ppermute(value, axis, [(0, 1), (1, 0)])  7.51 us
    pallas_call x1, Pallas kernels, out_proj(): pl.pallas_call(out_proj_kernel, out_shape=jax.ShapeDtypeStruct((n_groups,...  6.89 us
    pallas_call x1, Pallas kernels, gathered_proj(): pl.pallas_call(gathered_proj_kernel, out_shape=jax.ShapeDtypeStruct((toke...  6.75 us
    ppermute x4, starting transfers between devices, swap(): return lax.ppermute(value, axis, [(0, 1), (1, 0)])  5.23 us
    pallas_call x1, Pallas kernels, pick_columns(): pl.pallas_call(pick_kernel, out_shape=jax.ShapeDtypeStruct((n_groups, inn...  3.46 us
  transfers between devices with their start and end apart: 7, of which 6 were waited for; matrix products, arithmetic and copies ran while one was open for 3% of the time, Pallas kernels for 7%

profile of v11, /device:TPU:2, one launch (start us, length us, event | category | flops | bytes accessed | tf_op | source)
XLA Modules:
  0.0 148.4 jit_solution(17831104363455644731)
XLA Ops:
  6.5 3.2 %collective-permute-start = (bf16[256,384]{1,0:T(8,128)(2,1)}, bf16[256,384]{1,0:T(8,128)(2,1)S(1)}, u32[]{:S(2)}, u32[]{:S(2)}) collective-permute-start(bf16[256,384]{1,0:T(8,128)(2,1)} %bitcast.59), channel_id=1, source_target_pairs={{0,2},{2,0},{1,3},{3,1},{4,6},{6,4},{5,7},{7,5},{8,10},{10,8},{9,1... | collective-permute-start | bytes 589832 | tf_op jit(solution)/shard_map/ppermute | solution.py:17
  9.7 5.2 %collective-permute-done = bf16[256,384]{1,0:T(8,128)(2,1)S(1)} collective-permute-done((bf16[256,384]{1,0:T(8,128)(2,1)}, bf16[256,384]{1,0:T(8,128)(2,1)S(1)}, u32[]{:S(2)}, u32[]{:S(2)}) %collective-permute-start) | collective-permute-done | bytes 196640 | tf_op jit(solution)/shard_map/ppermute | solution.py:17
  14.9 1.0 select_bitcast_fusion.1
  15.9 0.8 pad_maximum_fusion
  16.8 3.5 %shard_map.56 = bf16[16,256,384]{2,1,0:T(8,128)(2,1)} custom-call(s32[1]{0:T(128)S(6)} %sub.17.sel_ref, bf16[256,12288]{1,0:T(8,128)(2,1)} %bitcast.42, bf16[256,12288]{1,0:T(8,128)(2,1)} %bitcast.43, bf16[256,12288]{1,0:T(8,128)(2,1)} %bitcast.44, bf16[256,12288]{1,0:T(8,128)(2,1)} %bitcast.45, bf16[256,12288]{1,0:T(8,128)(2,1)} %bitcast.46, ...), custom_call_target="tpu_custom_call" | custom-call | tf_op jit(solution)/shard_map/pallas_call | solution.py:34
  20.4 0.3 fusion.14
  20.7 1.0 fusion.3
  21.8 44.1 %all-gather.3.cloned.1.call-done.f_ref = bf16[32,256,384]{2,1,0:T(8,128)(2,1)} async-done(((bf16[2,256,384]{2,1,0:T(8,128)(2,1)}), bf16[32,256,384]{2,1,0:T(8,128)(2,1)}) %all-gather.3.cloned.1.call-update) | async-done | bytes 6291472 | tf_op jit(solution)/shard_map/all_gather | solution.py:135
  65.8 6.8 %shard_map.55 = bf16[256,256]{1,0:T(8,128)(2,1)} custom-call(bf16[32,256,384]{2,1,0:T(8,128)(2,1)} %all-gather.3.cloned.1.call-done.f_ref, bf16[12288,256]{1,0:T(8,128)(2,1)} %bitcast.26, bf16[12288,256]{1,0:T(8,128)(2,1)} %bitcast.27, bf16[12288,256]{1,0:T(8,128)(2,1)} %bitcast.28, bf16[12288,256]{1,0:T(8,128)(2,1)} %bitcast.29, ...), custom_call_target="tpu_custom_call" | custom-call | tf_op jit(solution)/shard_map/pallas_call | solution.py:112
  72.6 1.0 copy.17
  73.6 1.5 convolution_convert_fusion
  75.2 0.3 collective-permute-start.1
  75.5 0.7 pad_add_fusion.sel_ref
  76.2 0.4 collective-permute-done.1.ctx_sib_ref
  76.7 1.2 copy-done
  77.9 0.7 copy-done.2
  78.5 6.9 %shard_map.57 = bf16[16,256,384]{2,1,0:T(8,128)(2,1)} custom-call(s32[2]{0:T(128)} %pad_add_fusion.sel_ref, bf16[256,256]{1,0:T(8,128)(2,1)} %copy-done.1, bf16[256,256]{1,0:T(8,128)(2,1)} %copy-done.2, bf16[16,256,384]{2,1,0:T(8,128)(2,1)} %copy-done, bf16[256,384]{1,0:T(8,128)(2,1)} %bitcast.60, bf16[256,12288]{1,0:T(8,128)(2,1)} %bitcast.50, ...), custom_call_target="tpu_custom_call" | custom-call | tf_op jit(solution)/shard_map/pallas_call | solution.py:63
  85.5 45.7 %reduce-scatter.2.cloned.1.call-done = bf16[1,2,256,384]{3,2,1,0:T(8,128)(2,1)} async-done(((bf16[8,2,256,384]{3,2,1,0:T(8,128)(2,1)}), bf16[1,2,256,384]{3,2,1,0:T(8,128)(2,1)}) %reduce-scatter.2.cloned.1.call-update) | async-done | bytes 393232 | tf_op jit(solution)/shard_map/reduce_scatter | solution.py:161
  131.1 1.1 dynamic-slice_bitcast_fusion.1
  132.2 1.7 %collective-permute-start.3 = (bf16[256,384]{1,0:T(8,128)(2,1)S(1)}, bf16[256,384]{1,0:T(8,128)(2,1)S(1)}, u32[]{:S(2)}, u32[]{:S(2)}) collective-permute-start(bf16[256,384]{1,0:T(8,128)(2,1)S(1)} %get-tuple-element.5), channel_id=1, source_target_pairs={{0,128},{128,0},{1,129},{129,1},{2,130},{130,2},{3,131},{131,3},{4... | collective-permute-start | bytes 589832 | tf_op jit(solution)/shard_map/ppermute | solution.py:17
  133.9 2.1 %collective-permute-start.4 = (bf16[256,384]{1,0:T(8,128)(2,1)S(1)}, bf16[256,384]{1,0:T(8,128)(2,1)S(1)}, u32[]{:S(2)}, u32[]{:S(2)}) collective-permute-start(bf16[256,384]{1,0:T(8,128)(2,1)S(1)} %get-tuple-element.6), channel_id=1, source_target_pairs={{0,130},{2,128},{128,2},{130,0},{1,131},{3,129},{129,3},{131,1},{4... | collective-permute-start | bytes 589832 | tf_op jit(solution)/shard_map/ppermute | solution.py:164
  136.1 1.9 %collective-permute-done.3 = bf16[256,384]{1,0:T(8,128)(2,1)S(1)} collective-permute-done((bf16[256,384]{1,0:T(8,128)(2,1)S(1)}, bf16[256,384]{1,0:T(8,128)(2,1)S(1)}, u32[]{:S(2)}, u32[]{:S(2)}) %collective-permute-start.3) | collective-permute-done | bytes 196640 | tf_op jit(solution)/shard_map/ppermute | solution.py:17
  138.0 2.8 %collective-permute-done.4 = bf16[256,384]{1,0:T(8,128)(2,1)S(1)} collective-permute-done((bf16[256,384]{1,0:T(8,128)(2,1)S(1)}, bf16[256,384]{1,0:T(8,128)(2,1)S(1)}, u32[]{:S(2)}, u32[]{:S(2)}) %collective-permute-start.4) | collective-permute-done | bytes 196640 | tf_op jit(solution)/shard_map/ppermute | solution.py:164
  140.8 0.7 fusion.4
  (18 shorter events, 0.3 us)
Async XLA Ops:
  6.5 59.3 %all-gather.3.cloned.1.call-start = ((), (), s32[]{:S(2)}) async-start(), calls=%async_computation.2 | async-start | bytes 6684672 | tf_op jit(solution)/shard_map/all_gather | solution.py:135
  6.5 8.4 %collective-permute-start = (bf16[256,384]{1,0:T(8,128)(2,1)}, bf16[256,384]{1,0:T(8,128)(2,1)S(1)}, u32[]{:S(2)}, u32[]{:S(2)}) collective-permute-start(bf16[256,384]{1,0:T(8,128)(2,1)} %bitcast.59), channel_id=1, source_target_pairs={{0,2},{2,0},{1,3},{3,1},{4,6},{6,4},{5,7},{7,5},{8,10},{10,8},{9,1... | collective-permute-start | bytes 589832 | tf_op jit(solution)/shard_map/ppermute | solution.py:17
  16.7 114.4 %reduce-scatter.2.cloned.1.call-start = ((), (), s32[]{:S(2)}) async-start(), calls=%async_computation.1 | async-start | bytes 3538944 | tf_op jit(solution)/shard_map/reduce_scatter | solution.py:161
  16.7 3.5 %copy-start.3 = (bf16[1,256,256]{2,1,0:T(8,128)(2,1)S(1)}, bf16[1,256,256]{2,1,0:T(8,128)(2,1)}, u32[]{:S(2)}) copy-start(bf16[1,256,256]{2,1,0:T(8,128)(2,1)} %param.6) | copy-start | bytes 393220
  16.8 3.5 %copy-start.4 = (bf16[1,256,256]{2,1,0:T(8,128)(2,1)S(1)}, bf16[1,256,256]{2,1,0:T(8,128)(2,1)}, u32[]{:S(2)}) copy-start(bf16[1,256,256]{2,1,0:T(8,128)(2,1)} %param.7) | copy-start | bytes 393220
  20.2 56.0 %collective-permute-start.2 = (bf16[16,256,384]{2,1,0:T(8,128)(2,1)}, bf16[16,256,384]{2,1,0:T(8,128)(2,1)S(1)}, u32[]{:S(2)}, u32[]{:S(2)}) collective-permute-start(bf16[16,256,384]{2,1,0:T(8,128)(2,1)} %shard_map.56), channel_id=1, source_target_pairs={{0,1},{1,0},{2,3},{3,2},{4,5},{5,4},{6,7},{7,6},{8,9},{9,8},{10,11... | collective-permute-start | bytes 9437192 | tf_op jit(solution)/shard_map/ppermute | solution.py:17
  75.2 1.4 copy-start.1
  75.2 1.4 collective-permute-start.1
  76.2 1.7 %copy-start = (bf16[16,256,384]{2,1,0:T(8,128)(2,1)}, bf16[16,256,384]{2,1,0:T(8,128)(2,1)S(1)}, u32[]{:S(2)}) copy-start(bf16[16,256,384]{2,1,0:T(8,128)(2,1)S(1)} %collective-permute-done.2.w_sib_ref) | copy-start | bytes 9437188
  77.9 0.7 copy-start.2
  132.2 5.8 %collective-permute-start.3 = (bf16[256,384]{1,0:T(8,128)(2,1)S(1)}, bf16[256,384]{1,0:T(8,128)(2,1)S(1)}, u32[]{:S(2)}, u32[]{:S(2)}) collective-permute-start(bf16[256,384]{1,0:T(8,128)(2,1)S(1)} %get-tuple-element.5), channel_id=1, source_target_pairs={{0,128},{128,0},{1,129},{129,1},{2,130},{130,2},{3,131},{131,3},{4... | collective-permute-start | bytes 589832 | tf_op jit(solution)/shard_map/ppermute | solution.py:17
  133.9 6.9 %collective-permute-start.4 = (bf16[256,384]{1,0:T(8,128)(2,1)S(1)}, bf16[256,384]{1,0:T(8,128)(2,1)S(1)}, u32[]{:S(2)}, u32[]{:S(2)}) collective-permute-start(bf16[256,384]{1,0:T(8,128)(2,1)S(1)} %get-tuple-element.6), channel_id=1, source_target_pairs={{0,130},{2,128},{128,2},{130,0},{1,131},{3,129},{129,3},{131,1},{4... | collective-permute-start | bytes 589832 | tf_op jit(solution)/shard_map/ppermute | solution.py:164
Sparse Core Ops, SparseCore 0:
  16.8 48.9 all-gather.2
  85.6 45.5 reduce-scatter.1

commit v12 on v10

--- a/solution.py
+++ b/solution.py
@@ -146,14 +146,9 @@
     context = context.reshape(length, heads_here * HEAD_SIZE)
 
     part = out_proj(core, context, swap(context, "tc"), weight_from_sib, weight_o, col_width)
-    part = part.reshape(N_Z, N_Y, length, col_width)
-    part = lax.psum_scatter(part, "tz", scatter_dimension=0, tiled=False)
-    y_index = lax.axis_index("ty")
-    keep = lax.dynamic_index_in_dim(part, y_index, 0, keepdims=False)
-    send = lax.dynamic_index_in_dim(part, 1 - y_index, 0, keepdims=False)
-    keep = (keep.astype(jnp.float32) + activ.astype(jnp.float32)).astype(jnp.bfloat16)
-    across = lax.ppermute(send, ("section", "ty"), [(i, 3 - i) for i in range(4)])
-    result = swap(keep, "section").astype(jnp.float32) + across.astype(jnp.float32)
+    part = lax.psum_scatter(part, ("tz", "ty"), scatter_dimension=0, tiled=False)
+    result = part.astype(jnp.float32) + activ.astype(jnp.float32)
+    result = swap(result.astype(jnp.bfloat16), "section")
     return result.astype(jnp.bfloat16)[None]
 
 

time: 148 us -> 308 us (2.08)
  waiting for transfers between devices: 101 us -> 266 us
    reduce_scatter x1, waiting for transfers between devices: 45.9 us -> 210 us  [on_device(): lax.psum_scatter(part, ('tz', 'ty'), scatter_dimension=0, tiled=False)]
    ppermute x4, waiting for transfers between devices: 7.57 us -> 11.4 us  [swap(): return lax.ppermute(value, axis, [(0, 1), (1, 0)])]
    ppermute x1 -> x0, waiting for transfers between devices: 3.73 us -> none  [on_device(): lax.ppermute(send, ('section', 'ty'), [(i, 3 - i) for i in range(4)])]
  transfers between devices with their start and end apart: 7 -> 6, of which waited for: 6 -> 5; matrix products, arithmetic and copies ran while one was open for 4% -> 1% of each run, Pallas kernels for 7% -> 3%
where the time goes in v12:
time: 308 us
  waiting for transfers between devices  266 us (86%)
  Pallas kernels  16.4 us (5%)
  between operations  13.5 us (4%)
  starting transfers between devices  4.29 us (1%)
  other arithmetic  3.73 us (1%)
    reduce_scatter x1, waiting for transfers between devices, on_device(): lax.psum_scatter(part, ('tz', 'ty'), scatter_dimension=0, tiled=False)  210 us
    all_gather x1, waiting for transfers between devices, on_device(): gathered = lax.all_gather(gathered, ('tz', 'tc'), axis=0)  44.1 us
    ppermute x4, waiting for transfers between devices, swap(): return lax.ppermute(value, axis, [(0, 1), (1, 0)])  11.4 us
    pallas_call x1, Pallas kernels, gathered_proj(): pl.pallas_call(gathered_proj_kernel, out_shape=jax.ShapeDtypeStruct((toke...  6.8 us
  transfers between devices with their start and end apart: 6, of which 5 were waited for; matrix products, arithmetic and copies ran while one was open for 1% of the time, Pallas kernels for 3%

profile of v12, /device:TPU:2, one launch (start us, length us, event | category | flops | bytes accessed | tf_op | source)
XLA Modules:
  0.0 308.0 jit_solution(460127476712287112)
XLA Ops:
  6.5 3.2 %collective-permute-start = (bf16[256,384]{1,0:T(8,128)(2,1)}, bf16[256,384]{1,0:T(8,128)(2,1)S(1)}, u32[]{:S(2)}, u32[]{:S(2)}) collective-permute-start(bf16[256,384]{1,0:T(8,128)(2,1)} %bitcast.55), channel_id=1, source_target_pairs={{0,2},{2,0},{1,3},{3,1},{4,6},{6,4},{5,7},{7,5},{8,10},{10,8},{9,1... | collective-permute-start | bytes 589832 | tf_op jit(solution)/shard_map/ppermute | solution.py:17
  9.7 5.2 %collective-permute-done = bf16[256,384]{1,0:T(8,128)(2,1)S(1)} collective-permute-done((bf16[256,384]{1,0:T(8,128)(2,1)}, bf16[256,384]{1,0:T(8,128)(2,1)S(1)}, u32[]{:S(2)}, u32[]{:S(2)}) %collective-permute-start) | collective-permute-done | bytes 196640 | tf_op jit(solution)/shard_map/ppermute | solution.py:17
  14.9 1.0 select_bitcast_fusion.1
  15.9 0.8 pad_maximum_fusion
  16.7 0.0 all-gather.3.cloned.1.call-update
  16.7 0.0 reduce-scatter.2.cloned.1.call-start
  16.8 3.4 %shard_map.56 = bf16[16,256,384]{2,1,0:T(8,128)(2,1)} custom-call(s32[1]{0:T(128)S(6)} %sub.14.sel_ref, bf16[256,12288]{1,0:T(8,128)(2,1)} %bitcast.39, bf16[256,12288]{1,0:T(8,128)(2,1)} %bitcast.40, bf16[256,12288]{1,0:T(8,128)(2,1)} %bitcast.41, bf16[256,12288]{1,0:T(8,128)(2,1)} %bitcast.42, bf16[256,12288]{1,0:T(8,128)(2,1)} %bitcast.43, ...), custom_call_target="tpu_custom_call" | custom-call | tf_op jit(solution)/shard_map/pallas_call | solution.py:34
  20.3 0.3 fusion.14
  20.7 1.0 fusion.3
  21.7 44.1 %all-gather.3.cloned.1.call-done.f_ref = bf16[32,256,384]{2,1,0:T(8,128)(2,1)} async-done(((bf16[2,256,384]{2,1,0:T(8,128)(2,1)}), bf16[32,256,384]{2,1,0:T(8,128)(2,1)}) %all-gather.3.cloned.1.call-update) | async-done | bytes 6291472 | tf_op jit(solution)/shard_map/all_gather | solution.py:126
  65.8 6.8 %shard_map.55 = f32[256,256]{1,0:T(8,128)} custom-call(bf16[32,256,384]{2,1,0:T(8,128)(2,1)} %all-gather.3.cloned.1.call-done.f_ref, bf16[12288,256]{1,0:T(8,128)(2,1)} %bitcast.23, bf16[12288,256]{1,0:T(8,128)(2,1)} %bitcast.24, bf16[12288,256]{1,0:T(8,128)(2,1)} %bitcast.25, bf16[12288,256]{1,0:T(8,128)(2,1)} %bitcast.26, bf16[12288,256]{1,0:T(8,128)(2,1)} %bitcast.27, ...), custom_call_target="tpu_custom_call" | custom-call | tf_op jit(solution)/shard_map/pallas_call | solution.py:104
  72.6 1.0 convert_element_type.28
  73.6 0.1 copy.17
  73.7 1.5 convolution_convert_fusion
  75.2 0.1 copy.18.ctx_ref
  75.3 0.3 collective-permute-start.1
  75.6 1.2 collective-permute-done.1.ctx_sib_ref
  76.9 0.4 copy-done
  77.3 6.1 %shard_map.57 = bf16[16,256,384]{2,1,0:T(8,128)(2,1)} custom-call(s32[1]{0:T(128)} %bitcast.core_ref, bf16[256,256]{1,0:T(8,128)(2,1)} %copy-done.2, bf16[256,256]{1,0:T(8,128)(2,1)} %collective-permute-done.1.ctx_sib_ref, bf16[16,256,384]{2,1,0:T(8,128)(2,1)} %copy-done, bf16[256,12288]{1,0:T(8,128)(2,1)} %bitcast.47, bf16[256,12288]{1,0:T(8,128)(2,1)} %bitcast.48, ...), custom_call_target="tpu_custom_call" | custom-call | tf_op jit(solution)/shard_map/pallas_call | solution.py:60
  83.5 210.3 %reduce-scatter.2.cloned.1.call-done = bf16[1,256,384]{2,1,0:T(8,128)(2,1)} async-done(((bf16[16,256,384]{2,1,0:T(8,128)(2,1)}), bf16[1,256,384]{2,1,0:T(8,128)(2,1)}) %reduce-scatter.2.cloned.1.call-update) | async-done | bytes 196624 | tf_op jit(solution)/shard_map/reduce_scatter | solution.py:149
  293.8 1.0 fusion.4
  294.7 0.7 collective-permute-start.3
  295.5 5.0 %collective-permute-done.3 = bf16[256,384]{1,0:T(8,128)(2,1)S(1)} collective-permute-done((bf16[256,384]{1,0:T(8,128)(2,1)S(1)}, bf16[256,384]{1,0:T(8,128)(2,1)S(1)}, u32[]{:S(2)}, u32[]{:S(2)}) %collective-permute-start.3) | collective-permute-done | bytes 196640 | tf_op jit(solution)/shard_map/ppermute | solution.py:17
  300.5 0.7 copy.32
  (16 shorter events, 0.2 us)
Async XLA Ops:
  6.5 59.3 %all-gather.3.cloned.1.call-start = ((), (), s32[]{:S(2)}) async-start(), calls=%async_computation.2 | async-start | bytes 6684672 | tf_op jit(solution)/shard_map/all_gather | solution.py:126
  6.5 8.4 %collective-permute-start = (bf16[256,384]{1,0:T(8,128)(2,1)}, bf16[256,384]{1,0:T(8,128)(2,1)S(1)}, u32[]{:S(2)}, u32[]{:S(2)}) collective-permute-start(bf16[256,384]{1,0:T(8,128)(2,1)} %bitcast.55), channel_id=1, source_target_pairs={{0,2},{2,0},{1,3},{3,1},{4,6},{6,4},{5,7},{7,5},{8,10},{10,8},{9,1... | collective-permute-start | bytes 589832 | tf_op jit(solution)/shard_map/ppermute | solution.py:17
  16.7 277.1 %reduce-scatter.2.cloned.1.call-start = ((), (), s32[]{:S(2)}) async-start(), calls=%async_computation.1 | async-start | bytes 3342336 | tf_op jit(solution)/shard_map/reduce_scatter | solution.py:149
  16.7 3.5 %copy-start.3 = (bf16[1,256,256]{2,1,0:T(8,128)(2,1)S(1)}, bf16[1,256,256]{2,1,0:T(8,128)(2,1)}, u32[]{:S(2)}) copy-start(bf16[1,256,256]{2,1,0:T(8,128)(2,1)} %param.6) | copy-start | bytes 393220
  16.7 3.5 %copy-start.4 = (bf16[1,256,256]{2,1,0:T(8,128)(2,1)S(1)}, bf16[1,256,256]{2,1,0:T(8,128)(2,1)}, u32[]{:S(2)}) copy-start(bf16[1,256,256]{2,1,0:T(8,128)(2,1)} %param.7) | copy-start | bytes 393220
  20.2 55.4 %collective-permute-start.2 = (bf16[16,256,384]{2,1,0:T(8,128)(2,1)}, bf16[16,256,384]{2,1,0:T(8,128)(2,1)S(1)}, u32[]{:S(2)}, u32[]{:S(2)}) collective-permute-start(bf16[16,256,384]{2,1,0:T(8,128)(2,1)} %shard_map.56), channel_id=1, source_target_pairs={{0,1},{1,0},{2,3},{3,2},{4,5},{5,4},{6,7},{7,6},{8,9},{9,8},{10,11... | collective-permute-start | bytes 9437192 | tf_op jit(solution)/shard_map/ppermute | solution.py:17
  75.3 1.6 copy-start.2
  75.3 218.4 %copy-start.1 = (bf16[1,256,384]{2,1,0:T(8,128)(2,1)S(1)}, bf16[1,256,384]{2,1,0:T(8,128)(2,1)}, u32[]{:S(2)}) copy-start(bf16[1,256,384]{2,1,0:T(8,128)(2,1)} %param.5) | copy-start | bytes 589828
  75.3 1.6 collective-permute-start.1
  75.6 1.7 copy-start
  294.7 5.8 %collective-permute-start.3 = (bf16[256,384]{1,0:T(8,128)(2,1)S(1)}, bf16[256,384]{1,0:T(8,128)(2,1)S(1)}, u32[]{:S(2)}, u32[]{:S(2)}) collective-permute-start(bf16[256,384]{1,0:T(8,128)(2,1)S(1)} %fusion.4), channel_id=1, source_target_pairs={{0,128},{128,0},{1,129},{129,1},{2,130},{130,2},{3,131},{131,3},{4... | collective-permute-start | bytes 589832 | tf_op jit(solution)/shard_map/ppermute | solution.py:17
Sparse Core Ops, SparseCore 0:
  16.8 48.9 all-gather.2
  83.6 210.1 reduce-scatter.1

commit v13 on v10

--- a/solution.py
+++ b/solution.py
@@ -74,40 +74,39 @@
     )(core, context, context_sib, weight_sib, *([weight_o] * step))
 
 
-def gathered_proj_kernel(f_ref, *refs):
-    w_refs, o_ref = refs[:-1], refs[-1]
+def gathered_proj_kernel(f_ref, w_ref, o_ref):
+    width = f_ref.shape[-1]
 
     @pl.when(pl.program_id(0) == 0)
     def _():
         o_ref[...] = jnp.zeros(o_ref.shape, o_ref.dtype)
 
     acc = o_ref[...]
-    for k, w_ref in enumerate(w_refs):
-        acc = acc + jnp.dot(f_ref[k], w_ref[...], preferred_element_type=jnp.float32)
+    for z in range(Z_PER_STEP):
+        for c in range(N_C):
+            for y in range(N_Y):
+                slot = (z * N_C + c) * N_Y + y
+                row = ((z * N_Y + y) * N_C + c) * width
+                acc = acc + jnp.dot(
+                    f_ref[slot], w_ref[row:row + width, :], preferred_element_type=jnp.float32
+                )
     o_ref[...] = acc
 
 
 def gathered_proj(feats, weight_v):
     tokens, width = feats.shape[-2:]
     feats = feats.reshape(-1, tokens, width)
-    per_z = N_C * N_Y
-    step = Z_PER_STEP * per_z
-    w_specs = [
-        pl.BlockSpec(
-            (width, weight_v.shape[1]),
-            lambda i, z=z, c=c, y=y: ((i * Z_PER_STEP + z) * per_z + y * N_C + c, 0),
-        )
-        for z in range(Z_PER_STEP)
-        for c in range(N_C)
-        for y in range(N_Y)
-    ]
+    step = Z_PER_STEP * N_C * N_Y
     return pl.pallas_call(
         gathered_proj_kernel,
         out_shape=jax.ShapeDtypeStruct((tokens, weight_v.shape[1]), jnp.float32),
         grid=(N_Z // Z_PER_STEP,),
-        in_specs=[pl.BlockSpec((step, tokens, width), lambda i: (i, 0, 0))] + w_specs,
+        in_specs=[
+            pl.BlockSpec((step, tokens, width), lambda i: (i, 0, 0)),
+            pl.BlockSpec((step * width, weight_v.shape[1]), lambda i: (i, 0)),
+        ],
         out_specs=pl.BlockSpec((tokens, weight_v.shape[1]), lambda i: (0, 0)),
-    )(feats, *([weight_v] * step))
+    )(feats, weight_v)
 
 
 def on_device(inputs, queries, keys, w_value, w_out):

time: 148 us -> 147 us (level)
  no operation moved by 1% of the time
where the time goes in v13:
time: 147 us
  waiting for transfers between devices  101 us (69%)
  Pallas kernels  16.1 us (11%)
  between operations  13.5 us (9%)
  starting transfers between devices  7.06 us (5%)
  other arithmetic  4.45 us (3%)
  matrix products  2.85 us (2%)
  local copies, waits for them, and re-layouts  2.58 us (2%)
    reduce_scatter x1, waiting for transfers between devices, on_device(): part = lax.psum_scatter(part, 'tz', scatter_dimension=0, tiled=False)  46 us
    all_gather x1, waiting for transfers between devices, on_device(): gathered = lax.all_gather(gathered, ('tz', 'tc'), axis=0)  43.3 us
    ppermute x4, waiting for transfers between devices, swap(): return lax.ppermute(value, axis, [(0, 1), (1, 0)])  7.71 us
    pallas_call x1, Pallas kernels, gathered_proj(): pl.pallas_call(gathered_proj_kernel, out_shape=jax.ShapeDtypeStruct((toke...  6.59 us
    pallas_call x1, Pallas kernels, out_proj(): pl.pallas_call(out_proj_kernel, out_shape=jax.ShapeDtypeStruct((n_groups,...  6.11 us
    ppermute x4, starting transfers between devices, swap(): return lax.ppermute(value, axis, [(0, 1), (1, 0)])  5.06 us
    ppermute x1, waiting for transfers between devices, on_device(): lax.ppermute(send, ('section', 'ty'), [(i, 3 - i) for i in range(4)])  3.7 us
    pallas_call x1, Pallas kernels, pick_columns(): pl.pallas_call(pick_kernel, out_shape=jax.ShapeDtypeStruct((n_groups, inn...  3.43 us
  transfers between devices with their start and end apart: 7, of which 6 were waited for; matrix products, arithmetic and copies ran while one was open for 4% of the time, Pallas kernels for 7%

profile of v13, /device:TPU:2, one launch (start us, length us, event | category | flops | bytes accessed | tf_op | source)
XLA Modules:
  0.0 147.2 jit_solution(16036700008063066612)
XLA Ops:
  6.5 3.2 %collective-permute-start = (bf16[256,384]{1,0:T(8,128)(2,1)}, bf16[256,384]{1,0:T(8,128)(2,1)S(1)}, u32[]{:S(2)}, u32[]{:S(2)}) collective-permute-start(bf16[256,384]{1,0:T(8,128)(2,1)} %bitcast.45), channel_id=1, source_target_pairs={{0,2},{2,0},{1,3},{3,1},{4,6},{6,4},{5,7},{7,5},{8,10},{10,8},{9,1... | collective-permute-start | bytes 589832 | tf_op jit(solution)/shard_map/ppermute | solution.py:17
  9.7 5.2 %collective-permute-done = bf16[256,384]{1,0:T(8,128)(2,1)S(1)} collective-permute-done((bf16[256,384]{1,0:T(8,128)(2,1)}, bf16[256,384]{1,0:T(8,128)(2,1)S(1)}, u32[]{:S(2)}, u32[]{:S(2)}) %collective-permute-start) | collective-permute-done | bytes 196640 | tf_op jit(solution)/shard_map/ppermute | solution.py:17
  14.9 1.0 select_bitcast_fusion.1
  15.9 0.8 pad_maximum_fusion
  16.7 3.4 %shard_map.56 = bf16[16,256,384]{2,1,0:T(8,128)(2,1)} custom-call(s32[1]{0:T(128)S(6)} %sub.17.sel_ref, bf16[256,12288]{1,0:T(8,128)(2,1)} %bitcast.27, bf16[256,12288]{1,0:T(8,128)(2,1)} %bitcast.28, bf16[256,12288]{1,0:T(8,128)(2,1)} %bitcast.29, bf16[256,12288]{1,0:T(8,128)(2,1)} %bitcast.30, bf16[256,12288]{1,0:T(8,128)(2,1)} %bitcast.31, ...), custom_call_target="tpu_custom_call" | custom-call | tf_op jit(solution)/shard_map/pallas_call | solution.py:34
  20.2 0.9 reshape.65
  21.2 0.3 fusion.15
  21.5 1.0 fusion.3
  22.6 43.3 %all-gather.3.cloned.1.call-done.f_ref = bf16[32,256,384]{2,1,0:T(8,128)(2,1)} async-done(((bf16[2,256,384]{2,1,0:T(8,128)(2,1)}), bf16[32,256,384]{2,1,0:T(8,128)(2,1)}) %all-gather.3.cloned.1.call-update) | async-done | bytes 6291472 | tf_op jit(solution)/shard_map/all_gather | solution.py:125
  65.8 6.6 %shard_map.55 = f32[256,256]{1,0:T(8,128)} custom-call(bf16[32,256,384]{2,1,0:T(8,128)(2,1)} %all-gather.3.cloned.1.call-done.f_ref, bf16[12288,256]{1,0:T(8,128)(2,1)} %bitcast.44), custom_call_target="tpu_custom_call" | custom-call | tf_op jit(solution)/shard_map/pallas_call | solution.py:100
  72.4 1.0 convert_element_type.37
  73.5 1.5 %convolution_convert_fusion = bf16[2,128,256]{2,1,0:T(8,128)(2,1)S(1)} fusion(bf16[256,2,128]{0,2,1:T(8,128)(2,1)S(1)} %bitcast.46, f32[2,256]{1,0:T(2,128)S(1)} %fusion.15, f32[2,256,256]{1,2,0:T(8,128)} %fusion.3), kind=kOutput, calls=%fused_computation.5 | convolution fusion | flops 34013952 | bytes 788480 | tf_op jit(solution)/shard_map/bhqk,bkhd->bqhd/dot_general | solution.py:142
  75.1 0.3 collective-permute-start.1
  75.4 1.2 collective-permute-done.1.ctx_sib_ref
  76.7 0.4 copy-done
  77.1 6.1 %shard_map.57 = bf16[16,256,384]{2,1,0:T(8,128)(2,1)} custom-call(s32[1]{0:T(128)} %bitcast.core_ref, bf16[256,256]{1,0:T(8,128)(2,1)} %copy-done.2, bf16[256,256]{1,0:T(8,128)(2,1)} %collective-permute-done.1.ctx_sib_ref, bf16[16,256,384]{2,1,0:T(8,128)(2,1)} %copy-done, bf16[256,12288]{1,0:T(8,128)(2,1)} %bitcast.35, bf16[256,12288]{1,0:T(8,128)(2,1)} %bitcast.36, ...), custom_call_target="tpu_custom_call" | custom-call | tf_op jit(solution)/shard_map/pallas_call | solution.py:60
  83.2 46.0 %reduce-scatter.2.cloned.1.call-done = bf16[1,2,256,384]{3,2,1,0:T(8,128)(2,1)} async-done(((bf16[8,2,256,384]{3,2,1,0:T(8,128)(2,1)}), bf16[1,2,256,384]{3,2,1,0:T(8,128)(2,1)}) %reduce-scatter.2.cloned.1.call-update) | async-done | bytes 393232 | tf_op jit(solution)/shard_map/reduce_scatter | solution.py:149
  129.2 1.0 fusion.4
  130.2 1.5 %collective-permute-start.3 = (bf16[256,384]{1,0:T(8,128)(2,1)S(1)}, bf16[256,384]{1,0:T(8,128)(2,1)S(1)}, u32[]{:S(2)}, u32[]{:S(2)}) collective-permute-start(bf16[256,384]{1,0:T(8,128)(2,1)S(1)} %fusion.4), channel_id=1, source_target_pairs={{0,128},{128,0},{1,129},{129,1},{2,130},{130,2},{3,131},{131,3},{4... | collective-permute-start | bytes 589832 | tf_op jit(solution)/shard_map/ppermute | solution.py:17
  131.8 0.9 dynamic-slice_bitcast_fusion
  132.7 2.0 %collective-permute-start.4 = (bf16[256,384]{1,0:T(8,128)(2,1)S(1)}, bf16[256,384]{1,0:T(8,128)(2,1)S(1)}, u32[]{:S(2)}, u32[]{:S(2)}) collective-permute-start(bf16[256,384]{1,0:T(8,128)(2,1)S(1)} %dynamic-slice_bitcast_fusion), channel_id=1, source_target_pairs={{0,130},{2,128},{128,2},{130,0},{1,131},{3,129},{129,3},{131,1},{4... | collective-permute-start | bytes 589832 | tf_op jit(solution)/shard_map/ppermute | solution.py:154
  134.7 1.3 collective-permute-done.3
  136.0 3.7 %collective-permute-done.4 = bf16[256,384]{1,0:T(8,128)(2,1)S(1)} collective-permute-done((bf16[256,384]{1,0:T(8,128)(2,1)S(1)}, bf16[256,384]{1,0:T(8,128)(2,1)S(1)}, u32[]{:S(2)}, u32[]{:S(2)}) %collective-permute-start.4) | collective-permute-done | bytes 196640 | tf_op jit(solution)/shard_map/ppermute | solution.py:154
  139.7 0.7 fusion.5
  (17 shorter events, 0.4 us)
Async XLA Ops:
  6.5 59.3 %all-gather.3.cloned.1.call-start = ((), (), s32[]{:S(2)}) async-start(), calls=%async_computation.2 | async-start | bytes 6684672 | tf_op jit(solution)/shard_map/all_gather | solution.py:125
  6.5 8.4 %collective-permute-start = (bf16[256,384]{1,0:T(8,128)(2,1)}, bf16[256,384]{1,0:T(8,128)(2,1)S(1)}, u32[]{:S(2)}, u32[]{:S(2)}) collective-permute-start(bf16[256,384]{1,0:T(8,128)(2,1)} %bitcast.45), channel_id=1, source_target_pairs={{0,2},{2,0},{1,3},{3,1},{4,6},{6,4},{5,7},{7,5},{8,10},{10,8},{9,1... | collective-permute-start | bytes 589832 | tf_op jit(solution)/shard_map/ppermute | solution.py:17
  16.7 112.5 %reduce-scatter.2.cloned.1.call-start = ((), (), s32[]{:S(2)}) async-start(), calls=%async_computation.1 | async-start | bytes 3538944 | tf_op jit(solution)/shard_map/reduce_scatter | solution.py:149
  16.7 3.4 %copy-start.3 = (bf16[1,256,256]{2,1,0:T(8,128)(2,1)S(1)}, bf16[1,256,256]{2,1,0:T(8,128)(2,1)}, u32[]{:S(2)}) copy-start(bf16[1,256,256]{2,1,0:T(8,128)(2,1)} %param.6) | copy-start | bytes 393220
  20.2 55.3 %collective-permute-start.2 = (bf16[16,256,384]{2,1,0:T(8,128)(2,1)}, bf16[16,256,384]{2,1,0:T(8,128)(2,1)S(1)}, u32[]{:S(2)}, u32[]{:S(2)}) collective-permute-start(bf16[16,256,384]{2,1,0:T(8,128)(2,1)} %shard_map.56), channel_id=1, source_target_pairs={{0,1},{1,0},{2,3},{3,2},{4,5},{5,4},{6,7},{7,6},{8,9},{9,8},{10,11... | collective-permute-start | bytes 9437192 | tf_op jit(solution)/shard_map/ppermute | solution.py:17
  75.1 1.6 %copy-start.2 = (bf16[256,256]{1,0:T(8,128)(2,1)}, bf16[256,256]{1,0:T(8,128)(2,1)S(1)}, u32[]{:S(2)}) copy-start(bf16[256,256]{1,0:T(8,128)(2,1)S(1)} %copy.18.ctx_ref) | copy-start | bytes 393220
  75.1 54.1 %copy-start.1 = (bf16[1,256,384]{2,1,0:T(8,128)(2,1)S(1)}, bf16[1,256,384]{2,1,0:T(8,128)(2,1)}, u32[]{:S(2)}) copy-start(bf16[1,256,384]{2,1,0:T(8,128)(2,1)} %param.5) | copy-start | bytes 589828
  75.1 1.6 %collective-permute-start.1 = (bf16[256,256]{1,0:T(8,128)(2,1)S(1)}, bf16[256,256]{1,0:T(8,128)(2,1)}, u32[]{:S(2)}, u32[]{:S(2)}) collective-permute-start(bf16[256,256]{1,0:T(8,128)(2,1)S(1)} %copy.18.ctx_ref), channel_id=1, source_target_pairs={{0,1},{1,0},{2,3},{3,2},{4,5},{5,4},{6,7},{7,6},{8,9},{9,8},{10,11... | collective-permute-start | bytes 393224 | tf_op jit(solution)/shard_map/ppermute | solution.py:17
  75.4 1.7 %copy-start = (bf16[16,256,384]{2,1,0:T(8,128)(2,1)}, bf16[16,256,384]{2,1,0:T(8,128)(2,1)S(1)}, u32[]{:S(2)}) copy-start(bf16[16,256,384]{2,1,0:T(8,128)(2,1)S(1)} %collective-permute-done.2.w_sib_ref) | copy-start | bytes 9437188
  130.2 5.8 %collective-permute-start.3 = (bf16[256,384]{1,0:T(8,128)(2,1)S(1)}, bf16[256,384]{1,0:T(8,128)(2,1)S(1)}, u32[]{:S(2)}, u32[]{:S(2)}) collective-permute-start(bf16[256,384]{1,0:T(8,128)(2,1)S(1)} %fusion.4), channel_id=1, source_target_pairs={{0,128},{128,0},{1,129},{129,1},{2,130},{130,2},{3,131},{131,3},{4... | collective-permute-start | bytes 589832 | tf_op jit(solution)/shard_map/ppermute | solution.py:17
  132.7 7.0 %collective-permute-start.4 = (bf16[256,384]{1,0:T(8,128)(2,1)S(1)}, bf16[256,384]{1,0:T(8,128)(2,1)S(1)}, u32[]{:S(2)}, u32[]{:S(2)}) collective-permute-start(bf16[256,384]{1,0:T(8,128)(2,1)S(1)} %dynamic-slice_bitcast_fusion), channel_id=1, source_target_pairs={{0,130},{2,128},{128,2},{130,0},{1,131},{3,129},{129,3},{131,1},{4... | collective-permute-start | bytes 589832 | tf_op jit(solution)/shard_map/ppermute | solution.py:154
Sparse Core Ops, SparseCore 0:
  16.8 48.9 all-gather.2
  83.4 45.8 reduce-scatter.1

commit v14 on v13

--- a/solution.py
+++ b/solution.py
@@ -74,23 +74,30 @@
     )(core, context, context_sib, weight_sib, *([weight_o] * step))
 
 
-def gathered_proj_kernel(f_ref, w_ref, o_ref):
+def gathered_proj_kernel(f_ref, w_ref, o_ref, acc_ref):
     width = f_ref.shape[-1]
 
     @pl.when(pl.program_id(0) == 0)
     def _():
-        o_ref[...] = jnp.zeros(o_ref.shape, o_ref.dtype)
+        acc_ref[...] = jnp.zeros(acc_ref.shape, acc_ref.dtype)
 
-    acc = o_ref[...]
+    acc = acc_ref[...]
     for z in range(Z_PER_STEP):
         for c in range(N_C):
             for y in range(N_Y):
                 slot = (z * N_C + c) * N_Y + y
                 row = ((z * N_Y + y) * N_C + c) * width
-                acc = acc + jnp.dot(
-                    f_ref[slot], w_ref[row:row + width, :], preferred_element_type=jnp.float32
+                acc = acc + lax.dot_general(
+                    w_ref[row:row + width, :],
+                    f_ref[slot],
+                    (((0,), (1,)), ((), ())),
+                    preferred_element_type=jnp.float32,
                 )
-    o_ref[...] = acc
+    acc_ref[...] = acc
+
+    @pl.when(pl.program_id(0) == pl.num_programs(0) - 1)
+    def _():
+        o_ref[...] = acc.astype(o_ref.dtype)
 
 
 def gathered_proj(feats, weight_v):
@@ -99,13 +106,14 @@
     step = Z_PER_STEP * N_C * N_Y
     return pl.pallas_call(
         gathered_proj_kernel,
-        out_shape=jax.ShapeDtypeStruct((tokens, weight_v.shape[1]), jnp.float32),
+        out_shape=jax.ShapeDtypeStruct((weight_v.shape[1], tokens), jnp.bfloat16),
         grid=(N_Z // Z_PER_STEP,),
         in_specs=[
             pl.BlockSpec((step, tokens, width), lambda i: (i, 0, 0)),
             pl.BlockSpec((step * width, weight_v.shape[1]), lambda i: (i, 0)),
         ],
-        out_specs=pl.BlockSpec((tokens, weight_v.shape[1]), lambda i: (0, 0)),
+        out_specs=pl.BlockSpec((weight_v.shape[1], tokens), lambda i: (0, 0)),
+        scratch_shapes=[pltpu.VMEM((weight_v.shape[1], tokens), jnp.float32)],
     )(feats, weight_v)
 
 
@@ -123,8 +131,7 @@
     other = swap(activ, "ty")
     gathered = jnp.stack([jnp.where(y_first, activ, other), jnp.where(y_first, other, activ)])
     gathered = lax.all_gather(gathered, ("tz", "tc"), axis=0)
-    values = gathered_proj(gathered, weight_v)
-    values = values.astype(jnp.bfloat16)
+    values = gathered_proj(gathered, weight_v).T
 
     heads_here = weight_v.shape[1] // HEAD_SIZE
     query_rows = queries[0].reshape(length // LEN, LEN, heads_here, HEAD_SIZE)

time: 147 us -> 146 us (level)
  transfers between devices with their start and end apart: 7 -> 7, of which waited for: 6 -> 6; matrix products, arithmetic and copies ran while one was open for 4% -> 3% of each run, Pallas kernels for 7% -> 7%
where the time goes in v14:
time: 146 us
  waiting for transfers between devices  101 us (69%)
  Pallas kernels  16.1 us (11%)
  between operations  13.5 us (9%)
  starting transfers between devices  7.17 us (5%)
  other arithmetic  3.49 us (2%)
  matrix products  2.88 us (2%)
  local copies, waits for them, and re-layouts  2.48 us (2%)
    reduce_scatter x1, waiting for transfers between devices, on_device(): part = lax.psum_scatter(part, 'tz', scatter_dimension=0, tiled=False)  46 us
    all_gather x1, waiting for transfers between devices, on_device(): gathered = lax.all_gather(gathered, ('tz', 'tc'), axis=0)  43.3 us
    ppermute x4, waiting for transfers between devices, swap(): return lax.ppermute(value, axis, [(0, 1), (1, 0)])  7.6 us
    pallas_call x1, Pallas kernels, gathered_proj(): pl.pallas_call(gathered_proj_kernel, out_shape=jax.ShapeDtypeStruct((weig...  6.6 us
    pallas_call x1, Pallas kernels, out_proj(): pl.pallas_call(out_proj_kernel, out_shape=jax.ShapeDtypeStruct((n_groups,...  6.11 us
    ppermute x4, starting transfers between devices, swap(): return lax.ppermute(value, axis, [(0, 1), (1, 0)])  5.04 us
    ppermute x1, waiting for transfers between devices, on_device(): lax.ppermute(send, ('section', 'ty'), [(i, 3 - i) for i in range(4)])  3.67 us
    pallas_call x1, Pallas kernels, pick_columns(): pl.pallas_call(pick_kernel, out_shape=jax.ShapeDtypeStruct((n_groups, inn...  3.43 us
  transfers between devices with their start and end apart: 7, of which 6 were waited for; matrix products, arithmetic and copies ran while one was open for 3% of the time, Pallas kernels for 7%

profile of v14, /device:TPU:2, one launch (start us, length us, event | category | flops | bytes accessed | tf_op | source)
XLA Modules:
  0.0 146.2 jit_solution(1184719230677276257)
XLA Ops:
  6.5 3.2 %collective-permute-start = (bf16[256,384]{1,0:T(8,128)(2,1)}, bf16[256,384]{1,0:T(8,128)(2,1)S(1)}, u32[]{:S(2)}, u32[]{:S(2)}) collective-permute-start(bf16[256,384]{1,0:T(8,128)(2,1)} %bitcast.47), channel_id=1, source_target_pairs={{0,2},{2,0},{1,3},{3,1},{4,6},{6,4},{5,7},{7,5},{8,10},{10,8},{9,1... | collective-permute-start | bytes 589832 | tf_op jit(solution)/shard_map/ppermute | solution.py:17
  9.7 5.2 %collective-permute-done = bf16[256,384]{1,0:T(8,128)(2,1)S(1)} collective-permute-done((bf16[256,384]{1,0:T(8,128)(2,1)}, bf16[256,384]{1,0:T(8,128)(2,1)S(1)}, u32[]{:S(2)}, u32[]{:S(2)}) %collective-permute-start) | collective-permute-done | bytes 196640 | tf_op jit(solution)/shard_map/ppermute | solution.py:17
  14.9 1.0 select_bitcast_fusion.1
  15.9 0.8 pad_maximum_fusion
  16.7 3.4 %shard_map.56 = bf16[16,256,384]{2,1,0:T(8,128)(2,1)} custom-call(s32[1]{0:T(128)S(6)} %sub.17.sel_ref, bf16[256,12288]{1,0:T(8,128)(2,1)} %bitcast.29, bf16[256,12288]{1,0:T(8,128)(2,1)} %bitcast.30, bf16[256,12288]{1,0:T(8,128)(2,1)} %bitcast.31, bf16[256,12288]{1,0:T(8,128)(2,1)} %bitcast.32, bf16[256,12288]{1,0:T(8,128)(2,1)} %bitcast.33, ...), custom_call_target="tpu_custom_call" | custom-call | tf_op jit(solution)/shard_map/pallas_call | solution.py:34
  20.2 0.9 reshape.65
  21.2 0.3 fusion.15
  21.5 1.0 fusion.3
  22.6 43.3 %all-gather.3.cloned.1.call-done.f_ref = bf16[32,256,384]{2,1,0:T(8,128)(2,1)} async-done(((bf16[2,256,384]{2,1,0:T(8,128)(2,1)}), bf16[32,256,384]{2,1,0:T(8,128)(2,1)}) %all-gather.3.cloned.1.call-update) | async-done | bytes 6291472 | tf_op jit(solution)/shard_map/all_gather | solution.py:133
  65.8 6.6 %shard_map.55 = bf16[256,256]{1,0:T(8,128)(2,1)} custom-call(bf16[32,256,384]{2,1,0:T(8,128)(2,1)} %all-gather.3.cloned.1.call-done.f_ref, bf16[12288,256]{1,0:T(8,128)(2,1)} %bitcast.46), custom_call_target="tpu_custom_call" | custom-call | tf_op jit(solution)/shard_map/pallas_call | solution.py:107
  72.4 1.5 %convolution_convert_fusion = bf16[2,128,256]{2,1,0:T(8,128)(2,1)S(1)} fusion(bf16[256,2,128]{0,2,1:T(8,128)(2,1)} %bitcast.48, f32[2,256]{1,0:T(2,128)S(1)} %fusion.15, f32[2,256,256]{1,2,0:T(8,128)} %fusion.3), kind=kOutput, calls=%fused_computation.5 | convolution fusion | flops 34013952 | bytes 788480 | tf_op jit(solution)/shard_map/bhqk,bkhd->bqhd/dot_general | solution.py:149
  73.9 0.1 copy.15.ctx_ref
  74.1 0.3 collective-permute-start.1
  74.4 1.2 collective-permute-done.1.ctx_sib_ref
  75.6 0.4 copy-done
  76.1 6.1 %shard_map.57 = bf16[16,256,384]{2,1,0:T(8,128)(2,1)} custom-call(s32[1]{0:T(128)} %bitcast.core_ref, bf16[256,256]{1,0:T(8,128)(2,1)} %copy-done.2, bf16[256,256]{1,0:T(8,128)(2,1)} %collective-permute-done.1.ctx_sib_ref, bf16[16,256,384]{2,1,0:T(8,128)(2,1)} %copy-done, bf16[256,12288]{1,0:T(8,128)(2,1)} %bitcast.37, bf16[256,12288]{1,0:T(8,128)(2,1)} %bitcast.38, ...), custom_call_target="tpu_custom_call" | custom-call | tf_op jit(solution)/shard_map/pallas_call | solution.py:60
  82.2 46.0 %reduce-scatter.2.cloned.1.call-done = bf16[1,2,256,384]{3,2,1,0:T(8,128)(2,1)} async-done(((bf16[8,2,256,384]{3,2,1,0:T(8,128)(2,1)}), bf16[1,2,256,384]{3,2,1,0:T(8,128)(2,1)}) %reduce-scatter.2.cloned.1.call-update) | async-done | bytes 393232 | tf_op jit(solution)/shard_map/reduce_scatter | solution.py:156
  128.2 1.0 fusion.4
  129.2 1.5 %collective-permute-start.3 = (bf16[256,384]{1,0:T(8,128)(2,1)S(1)}, bf16[256,384]{1,0:T(8,128)(2,1)S(1)}, u32[]{:S(2)}, u32[]{:S(2)}) collective-permute-start(bf16[256,384]{1,0:T(8,128)(2,1)S(1)} %fusion.4), channel_id=1, source_target_pairs={{0,128},{128,0},{1,129},{129,1},{2,130},{130,2},{3,131},{131,3},{4... | collective-permute-start | bytes 589832 | tf_op jit(solution)/shard_map/ppermute | solution.py:17
  130.7 0.9 dynamic-slice_bitcast_fusion
  131.6 2.1 %collective-permute-start.4 = (bf16[256,384]{1,0:T(8,128)(2,1)S(1)}, bf16[256,384]{1,0:T(8,128)(2,1)S(1)}, u32[]{:S(2)}, u32[]{:S(2)}) collective-permute-start(bf16[256,384]{1,0:T(8,128)(2,1)S(1)} %dynamic-slice_bitcast_fusion), channel_id=1, source_target_pairs={{0,130},{2,128},{128,2},{130,0},{1,131},{3,129},{129,3},{131,1},{4... | collective-permute-start | bytes 589832 | tf_op jit(solution)/shard_map/ppermute | solution.py:161
  133.7 1.2 collective-permute-done.3
  134.9 3.7 %collective-permute-done.4 = bf16[256,384]{1,0:T(8,128)(2,1)S(1)} collective-permute-done((bf16[256,384]{1,0:T(8,128)(2,1)S(1)}, bf16[256,384]{1,0:T(8,128)(2,1)S(1)}, u32[]{:S(2)}, u32[]{:S(2)}) %collective-permute-start.4) | collective-permute-done | bytes 196640 | tf_op jit(solution)/shard_map/ppermute | solution.py:161
  138.6 0.7 fusion.5
  (15 shorter events, 0.2 us)
Async XLA Ops:
  6.5 59.3 %all-gather.3.cloned.1.call-start = ((), (), s32[]{:S(2)}) async-start(), calls=%async_computation.2 | async-start | bytes 6684672 | tf_op jit(solution)/shard_map/all_gather | solution.py:133
  6.5 8.4 %collective-permute-start = (bf16[256,384]{1,0:T(8,128)(2,1)}, bf16[256,384]{1,0:T(8,128)(2,1)S(1)}, u32[]{:S(2)}, u32[]{:S(2)}) collective-permute-start(bf16[256,384]{1,0:T(8,128)(2,1)} %bitcast.47), channel_id=1, source_target_pairs={{0,2},{2,0},{1,3},{3,1},{4,6},{6,4},{5,7},{7,5},{8,10},{10,8},{9,1... | collective-permute-start | bytes 589832 | tf_op jit(solution)/shard_map/ppermute | solution.py:17
  16.7 111.5 %reduce-scatter.2.cloned.1.call-start = ((), (), s32[]{:S(2)}) async-start(), calls=%async_computation.1 | async-start | bytes 3538944 | tf_op jit(solution)/shard_map/reduce_scatter | solution.py:156
  16.7 3.4 %copy-start.3 = (bf16[1,256,256]{2,1,0:T(8,128)(2,1)S(1)}, bf16[1,256,256]{2,1,0:T(8,128)(2,1)}, u32[]{:S(2)}) copy-start(bf16[1,256,256]{2,1,0:T(8,128)(2,1)} %param.6) | copy-start | bytes 393220
  20.2 54.2 %collective-permute-start.2 = (bf16[16,256,384]{2,1,0:T(8,128)(2,1)}, bf16[16,256,384]{2,1,0:T(8,128)(2,1)S(1)}, u32[]{:S(2)}, u32[]{:S(2)}) collective-permute-start(bf16[16,256,384]{2,1,0:T(8,128)(2,1)} %shard_map.56), channel_id=1, source_target_pairs={{0,1},{1,0},{2,3},{3,2},{4,5},{5,4},{6,7},{7,6},{8,9},{9,8},{10,11... | collective-permute-start | bytes 9437192 | tf_op jit(solution)/shard_map/ppermute | solution.py:17
  74.1 1.6 %copy-start.2 = (bf16[256,256]{1,0:T(8,128)(2,1)}, bf16[256,256]{1,0:T(8,128)(2,1)S(1)}, u32[]{:S(2)}) copy-start(bf16[256,256]{1,0:T(8,128)(2,1)S(1)} %copy.15.ctx_ref) | copy-start | bytes 393220
  74.1 54.1 %copy-start.1 = (bf16[1,256,384]{2,1,0:T(8,128)(2,1)S(1)}, bf16[1,256,384]{2,1,0:T(8,128)(2,1)}, u32[]{:S(2)}) copy-start(bf16[1,256,384]{2,1,0:T(8,128)(2,1)} %param.5) | copy-start | bytes 589828
  74.1 1.6 %collective-permute-start.1 = (bf16[256,256]{1,0:T(8,128)(2,1)S(1)}, bf16[256,256]{1,0:T(8,128)(2,1)}, u32[]{:S(2)}, u32[]{:S(2)}) collective-permute-start(bf16[256,256]{1,0:T(8,128)(2,1)S(1)} %copy.15.ctx_ref), channel_id=1, source_target_pairs={{0,1},{1,0},{2,3},{3,2},{4,5},{5,4},{6,7},{7,6},{8,9},{9,8},{10,11... | collective-permute-start | bytes 393224 | tf_op jit(solution)/shard_map/ppermute | solution.py:17
  74.4 1.7 %copy-start = (bf16[16,256,384]{2,1,0:T(8,128)(2,1)}, bf16[16,256,384]{2,1,0:T(8,128)(2,1)S(1)}, u32[]{:S(2)}) copy-start(bf16[16,256,384]{2,1,0:T(8,128)(2,1)S(1)} %collective-permute-done.2.w_sib_ref) | copy-start | bytes 9437188
  129.2 5.8 %collective-permute-start.3 = (bf16[256,384]{1,0:T(8,128)(2,1)S(1)}, bf16[256,384]{1,0:T(8,128)(2,1)S(1)}, u32[]{:S(2)}, u32[]{:S(2)}) collective-permute-start(bf16[256,384]{1,0:T(8,128)(2,1)S(1)} %fusion.4), channel_id=1, source_target_pairs={{0,128},{128,0},{1,129},{129,1},{2,130},{130,2},{3,131},{131,3},{4... | collective-permute-start | bytes 589832 | tf_op jit(solution)/shard_map/ppermute | solution.py:17
  131.6 7.0 %collective-permute-start.4 = (bf16[256,384]{1,0:T(8,128)(2,1)S(1)}, bf16[256,384]{1,0:T(8,128)(2,1)S(1)}, u32[]{:S(2)}, u32[]{:S(2)}) collective-permute-start(bf16[256,384]{1,0:T(8,128)(2,1)S(1)} %dynamic-slice_bitcast_fusion), channel_id=1, source_target_pairs={{0,130},{2,128},{128,2},{130,0},{1,131},{3,129},{129,3},{131,1},{4... | collective-permute-start | bytes 589832 | tf_op jit(solution)/shard_map/ppermute | solution.py:161
Sparse Core Ops, SparseCore 0:
  16.8 48.9 all-gather.2
  82.3 45.7 reduce-scatter.1

commit v15 on v14

--- a/solution.py
+++ b/solution.py
@@ -47,14 +47,15 @@
     w_refs, o_ref = refs[:-1], refs[-1]
     ctx = ctx_ref[...]
     ctx_sib = ctx_sib_ref[...]
+    dims = (((0,), (0,)), ((), ()))
     for k, w_ref in enumerate(w_refs):
-        d = jnp.dot(ctx, w_ref[...], preferred_element_type=jnp.float32)
-        d = d + jnp.dot(ctx_sib, w_sib_ref[k], preferred_element_type=jnp.float32)
+        d = lax.dot_general(ctx, w_ref[...], dims, preferred_element_type=jnp.float32)
+        d = d + lax.dot_general(ctx_sib, w_sib_ref[k], dims, preferred_element_type=jnp.float32)
         o_ref[k] = d.astype(jnp.bfloat16)
 
 
 def out_proj(core, context, context_sib, weight_sib, weight_o, width):
-    tokens, inner = context.shape
+    inner, tokens = context.shape
     n_groups = weight_o.shape[1] // (N_C * width)
     step = GROUPS_PER_STEP
     return pl.pallas_call(
@@ -64,8 +65,8 @@
             num_scalar_prefetch=1,
             grid=(n_groups // step,),
             in_specs=[
-                pl.BlockSpec((tokens, inner), lambda i, c: (0, 0)),
-                pl.BlockSpec((tokens, inner), lambda i, c: (0, 0)),
+                pl.BlockSpec((inner, tokens), lambda i, c: (0, 0)),
+                pl.BlockSpec((inner, tokens), lambda i, c: (0, 0)),
                 pl.BlockSpec((step, inner, width), lambda i, c: (i, 0, 0)),
             ]
             + [column_spec(inner, width, step, k) for k in range(step)],
@@ -147,9 +148,9 @@
     expo = jnp.exp(scores - top)
     probs = (expo / jnp.sum(expo, axis=-1, keepdims=True)).astype(jnp.bfloat16)
     context = jnp.einsum(
-        "bhqk,bkhd->bqhd", probs, value_rows, preferred_element_type=jnp.float32
+        "bhqk,bkhd->bhdq", probs, value_rows, preferred_element_type=jnp.float32
     ).astype(jnp.bfloat16)
-    context = context.reshape(length, heads_here * HEAD_SIZE)
+    context = context.reshape(heads_here * HEAD_SIZE, length)
 
     part = out_proj(core, context, swap(context, "tc"), weight_from_sib, weight_o, col_width)
     part = part.reshape(N_Z, N_Y, length, col_width)

time: 146 us -> 146 us (level)
  no operation moved by 1% of the time
where the time goes in v15:
time: 146 us
  waiting for transfers between devices  101 us (69%)
  Pallas kernels  16.2 us (11%)
  between operations  13.5 us (9%)
  starting transfers between devices  7.17 us (5%)
  other arithmetic  3.49 us (2%)
  matrix products  2.88 us (2%)
  local copies, waits for them, and re-layouts  2.38 us (2%)
    reduce_scatter x1, waiting for transfers between devices, on_device(): part = lax.psum_scatter(part, 'tz', scatter_dimension=0, tiled=False)  46 us
    all_gather x1, waiting for transfers between devices, on_device(): gathered = lax.all_gather(gathered, ('tz', 'tc'), axis=0)  43.3 us
    ppermute x4, waiting for transfers between devices, swap(): return lax.ppermute(value, axis, [(0, 1), (1, 0)])  7.6 us
    pallas_call x1, Pallas kernels, gathered_proj(): pl.pallas_call(gathered_proj_kernel, out_shape=jax.ShapeDtypeStruct((weig...  6.6 us
    pallas_call x1, Pallas kernels, out_proj(): pl.pallas_call(out_proj_kernel, out_shape=jax.ShapeDtypeStruct((n_groups,...  6.19 us
    ppermute x4, starting transfers between devices, swap(): return lax.ppermute(value, axis, [(0, 1), (1, 0)])  5.04 us
    ppermute x1, waiting for transfers between devices, on_device(): lax.ppermute(send, ('section', 'ty'), [(i, 3 - i) for i in range(4)])  3.67 us
    pallas_call x1, Pallas kernels, pick_columns(): pl.pallas_call(pick_kernel, out_shape=jax.ShapeDtypeStruct((n_groups, inn...  3.43 us
  transfers between devices with their start and end apart: 7, of which 6 were waited for; matrix products, arithmetic and copies ran while one was open for 3% of the time, Pallas kernels for 7%

profile of v15, /device:TPU:2, one launch (start us, length us, event | category | flops | bytes accessed | tf_op | source)
XLA Modules:
  0.0 146.1 jit_solution(12003586572570030601)
XLA Ops:
  6.5 3.2 %collective-permute-start = (bf16[256,384]{1,0:T(8,128)(2,1)}, bf16[256,384]{1,0:T(8,128)(2,1)S(1)}, u32[]{:S(2)}, u32[]{:S(2)}) collective-permute-start(bf16[256,384]{1,0:T(8,128)(2,1)} %bitcast.43), channel_id=1, source_target_pairs={{0,2},{2,0},{1,3},{3,1},{4,6},{6,4},{5,7},{7,5},{8,10},{10,8},{9,1... | collective-permute-start | bytes 589832 | tf_op jit(solution)/shard_map/ppermute | solution.py:17
  9.7 5.2 %collective-permute-done = bf16[256,384]{1,0:T(8,128)(2,1)S(1)} collective-permute-done((bf16[256,384]{1,0:T(8,128)(2,1)}, bf16[256,384]{1,0:T(8,128)(2,1)S(1)}, u32[]{:S(2)}, u32[]{:S(2)}) %collective-permute-start) | collective-permute-done | bytes 196640 | tf_op jit(solution)/shard_map/ppermute | solution.py:17
  14.9 1.0 select_bitcast_fusion.1
  15.9 0.8 pad_maximum_fusion
  16.7 0.0 reduce-scatter.2.cloned.1.call-start
  16.7 3.4 %shard_map.56 = bf16[16,256,384]{2,1,0:T(8,128)(2,1)} custom-call(s32[1]{0:T(128)S(6)} %sub.17.sel_ref, bf16[256,12288]{1,0:T(8,128)(2,1)} %bitcast.25, bf16[256,12288]{1,0:T(8,128)(2,1)} %bitcast.26, bf16[256,12288]{1,0:T(8,128)(2,1)} %bitcast.27, bf16[256,12288]{1,0:T(8,128)(2,1)} %bitcast.28, bf16[256,12288]{1,0:T(8,128)(2,1)} %bitcast.29, ...), custom_call_target="tpu_custom_call" | custom-call | tf_op jit(solution)/shard_map/pallas_call | solution.py:34
  20.2 0.9 reshape.66
  21.2 0.3 fusion.15
  21.5 1.0 fusion.3
  22.6 43.3 %all-gather.3.cloned.1.call-done.f_ref = bf16[32,256,384]{2,1,0:T(8,128)(2,1)} async-done(((bf16[2,256,384]{2,1,0:T(8,128)(2,1)}), bf16[32,256,384]{2,1,0:T(8,128)(2,1)}) %all-gather.3.cloned.1.call-update) | async-done | bytes 6291472 | tf_op jit(solution)/shard_map/all_gather | solution.py:134
  65.8 6.6 %shard_map.55 = bf16[256,256]{1,0:T(8,128)(2,1)} custom-call(bf16[32,256,384]{2,1,0:T(8,128)(2,1)} %all-gather.3.cloned.1.call-done.f_ref, bf16[12288,256]{1,0:T(8,128)(2,1)} %bitcast.42), custom_call_target="tpu_custom_call" | custom-call | tf_op jit(solution)/shard_map/pallas_call | solution.py:108
  72.4 1.5 %convolution_convert_fusion = bf16[2,128,256]{2,1,0:T(8,128)(2,1)S(1)} fusion(bf16[256,2,128]{0,2,1:T(8,128)(2,1)} %bitcast.46, f32[2,256]{1,0:T(2,128)S(1)} %fusion.15, f32[2,256,256]{1,2,0:T(8,128)} %fusion.3), kind=kOutput, calls=%fused_computation.5 | convolution fusion | flops 34013952 | bytes 788480 | tf_op jit(solution)/shard_map/bhqk,bkhd->bhdq/dot_general | solution.py:150
  74.0 0.3 collective-permute-start.1
  74.3 1.2 collective-permute-done.1.ctx_sib_ref
  75.5 0.4 copy-done
  76.0 6.2 %shard_map.57 = bf16[16,256,384]{2,1,0:T(8,128)(2,1)} custom-call(s32[1]{0:T(128)} %bitcast.core_ref, bf16[256,256]{1,0:T(8,128)(2,1)} %bitcast.45, bf16[256,256]{1,0:T(8,128)(2,1)} %collective-permute-done.1.ctx_sib_ref, bf16[16,256,384]{2,1,0:T(8,128)(2,1)} %copy-done, bf16[256,12288]{1,0:T(8,128)(2,1)} %bitcast.33, bf16[256,12288]{1,0:T(8,128)(2,1)} %bitcast.34, ...), custom_call_target="tpu_custom_call" | custom-call | tf_op jit(solution)/shard_map/pallas_call | solution.py:61
  82.2 46.0 %reduce-scatter.2.cloned.1.call-done = bf16[1,2,256,384]{3,2,1,0:T(8,128)(2,1)} async-done(((bf16[8,2,256,384]{3,2,1,0:T(8,128)(2,1)}), bf16[1,2,256,384]{3,2,1,0:T(8,128)(2,1)}) %reduce-scatter.2.cloned.1.call-update) | async-done | bytes 393232 | tf_op jit(solution)/shard_map/reduce_scatter | solution.py:157
  128.2 1.0 fusion.4
  129.1 1.5 %collective-permute-start.3 = (bf16[256,384]{1,0:T(8,128)(2,1)S(1)}, bf16[256,384]{1,0:T(8,128)(2,1)S(1)}, u32[]{:S(2)}, u32[]{:S(2)}) collective-permute-start(bf16[256,384]{1,0:T(8,128)(2,1)S(1)} %fusion.4), channel_id=1, source_target_pairs={{0,128},{128,0},{1,129},{129,1},{2,130},{130,2},{3,131},{131,3},{4... | collective-permute-start | bytes 589832 | tf_op jit(solution)/shard_map/ppermute | solution.py:17
  130.7 0.9 dynamic-slice_bitcast_fusion
  131.6 2.1 %collective-permute-start.4 = (bf16[256,384]{1,0:T(8,128)(2,1)S(1)}, bf16[256,384]{1,0:T(8,128)(2,1)S(1)}, u32[]{:S(2)}, u32[]{:S(2)}) collective-permute-start(bf16[256,384]{1,0:T(8,128)(2,1)S(1)} %dynamic-slice_bitcast_fusion), channel_id=1, source_target_pairs={{0,130},{2,128},{128,2},{130,0},{1,131},{3,129},{129,3},{131,1},{4... | collective-permute-start | bytes 589832 | tf_op jit(solution)/shard_map/ppermute | solution.py:162
  133.7 1.2 collective-permute-done.3
  134.9 3.7 %collective-permute-done.4 = bf16[256,384]{1,0:T(8,128)(2,1)S(1)} collective-permute-done((bf16[256,384]{1,0:T(8,128)(2,1)S(1)}, bf16[256,384]{1,0:T(8,128)(2,1)S(1)}, u32[]{:S(2)}, u32[]{:S(2)}) %collective-permute-start.4) | collective-permute-done | bytes 196640 | tf_op jit(solution)/shard_map/ppermute | solution.py:162
  138.6 0.7 fusion.5
  (14 shorter events, 0.1 us)
Async XLA Ops:
  6.5 59.3 %all-gather.3.cloned.1.call-start = ((), (), s32[]{:S(2)}) async-start(), calls=%async_computation.2 | async-start | bytes 6684672 | tf_op jit(solution)/shard_map/all_gather | solution.py:134
  6.5 8.4 %collective-permute-start = (bf16[256,384]{1,0:T(8,128)(2,1)}, bf16[256,384]{1,0:T(8,128)(2,1)S(1)}, u32[]{:S(2)}, u32[]{:S(2)}) collective-permute-start(bf16[256,384]{1,0:T(8,128)(2,1)} %bitcast.43), channel_id=1, source_target_pairs={{0,2},{2,0},{1,3},{3,1},{4,6},{6,4},{5,7},{7,5},{8,10},{10,8},{9,1... | collective-permute-start | bytes 589832 | tf_op jit(solution)/shard_map/ppermute | solution.py:17
  16.7 111.5 %reduce-scatter.2.cloned.1.call-start = ((), (), s32[]{:S(2)}) async-start(), calls=%async_computation.1 | async-start | bytes 3538944 | tf_op jit(solution)/shard_map/reduce_scatter | solution.py:157
  16.7 3.4 %copy-start.3 = (bf16[1,256,256]{2,1,0:T(8,128)(2,1)S(1)}, bf16[1,256,256]{2,1,0:T(8,128)(2,1)}, u32[]{:S(2)}) copy-start(bf16[1,256,256]{2,1,0:T(8,128)(2,1)} %param.6) | copy-start | bytes 393220
  20.2 54.1 %collective-permute-start.2 = (bf16[16,256,384]{2,1,0:T(8,128)(2,1)}, bf16[16,256,384]{2,1,0:T(8,128)(2,1)S(1)}, u32[]{:S(2)}, u32[]{:S(2)}) collective-permute-start(bf16[16,256,384]{2,1,0:T(8,128)(2,1)} %shard_map.56), channel_id=1, source_target_pairs={{0,1},{1,0},{2,3},{3,2},{4,5},{5,4},{6,7},{7,6},{8,9},{9,8},{10,11... | collective-permute-start | bytes 9437192 | tf_op jit(solution)/shard_map/ppermute | solution.py:17
  73.9 1.6 %copy-start.2 = (bf16[2,128,256]{2,1,0:T(8,128)(2,1)}, bf16[2,128,256]{2,1,0:T(8,128)(2,1)S(1)}, u32[]{:S(2)}) copy-start(bf16[2,128,256]{2,1,0:T(8,128)(2,1)S(1)} %convolution_convert_fusion) | copy-start | bytes 393220
  74.0 54.2 %copy-start.1 = (bf16[1,256,384]{2,1,0:T(8,128)(2,1)S(1)}, bf16[1,256,384]{2,1,0:T(8,128)(2,1)}, u32[]{:S(2)}) copy-start(bf16[1,256,384]{2,1,0:T(8,128)(2,1)} %param.5) | copy-start | bytes 589828
  74.0 1.6 %collective-permute-start.1 = (bf16[256,256]{1,0:T(8,128)(2,1)S(1)}, bf16[256,256]{1,0:T(8,128)(2,1)}, u32[]{:S(2)}, u32[]{:S(2)}) collective-permute-start(bf16[256,256]{1,0:T(8,128)(2,1)S(1)} %bitcast.44), channel_id=1, source_target_pairs={{0,1},{1,0},{2,3},{3,2},{4,5},{5,4},{6,7},{7,6},{8,9},{9,8},{10,11... | collective-permute-start | bytes 393224 | tf_op jit(solution)/shard_map/ppermute | solution.py:17
  74.3 1.7 %copy-start = (bf16[16,256,384]{2,1,0:T(8,128)(2,1)}, bf16[16,256,384]{2,1,0:T(8,128)(2,1)S(1)}, u32[]{:S(2)}) copy-start(bf16[16,256,384]{2,1,0:T(8,128)(2,1)S(1)} %collective-permute-done.2.w_sib_ref) | copy-start | bytes 9437188
  129.1 5.8 %collective-permute-start.3 = (bf16[256,384]{1,0:T(8,128)(2,1)S(1)}, bf16[256,384]{1,0:T(8,128)(2,1)S(1)}, u32[]{:S(2)}, u32[]{:S(2)}) collective-permute-start(bf16[256,384]{1,0:T(8,128)(2,1)S(1)} %fusion.4), channel_id=1, source_target_pairs={{0,128},{128,0},{1,129},{129,1},{2,130},{130,2},{3,131},{131,3},{4... | collective-permute-start | bytes 589832 | tf_op jit(solution)/shard_map/ppermute | solution.py:17
  131.6 7.0 %collective-permute-start.4 = (bf16[256,384]{1,0:T(8,128)(2,1)S(1)}, bf16[256,384]{1,0:T(8,128)(2,1)S(1)}, u32[]{:S(2)}, u32[]{:S(2)}) collective-permute-start(bf16[256,384]{1,0:T(8,128)(2,1)S(1)} %dynamic-slice_bitcast_fusion), channel_id=1, source_target_pairs={{0,130},{2,128},{128,2},{130,0},{1,131},{3,129},{129,3},{131,1},{4... | collective-permute-start | bytes 589832 | tf_op jit(solution)/shard_map/ppermute | solution.py:162
Sparse Core Ops, SparseCore 0:
  16.8 48.9 all-gather.2
  82.3 45.7 reduce-scatter.1

commit v16 on v14

--- a/solution.py
+++ b/solution.py
@@ -152,12 +152,15 @@
     context = context.reshape(length, heads_here * HEAD_SIZE)
 
     part = out_proj(core, context, swap(context, "tc"), weight_from_sib, weight_o, col_width)
+    y_index = lax.axis_index("ty")
+    own = lax.axis_index("tz") * N_Y + y_index
+    own_sum = lax.dynamic_index_in_dim(part, own, 0, keepdims=False).astype(jnp.float32)
+    own_sum = (own_sum + activ.astype(jnp.float32)).astype(jnp.bfloat16)
+    part = lax.dynamic_update_index_in_dim(part, own_sum, own, 0)
     part = part.reshape(N_Z, N_Y, length, col_width)
     part = lax.psum_scatter(part, "tz", scatter_dimension=0, tiled=False)
-    y_index = lax.axis_index("ty")
     keep = lax.dynamic_index_in_dim(part, y_index, 0, keepdims=False)
     send = lax.dynamic_index_in_dim(part, 1 - y_index, 0, keepdims=False)
-    keep = (keep.astype(jnp.float32) + activ.astype(jnp.float32)).astype(jnp.bfloat16)
     across = lax.ppermute(send, ("section", "ty"), [(i, 3 - i) for i in range(4)])
     result = swap(keep, "section").astype(jnp.float32) + across.astype(jnp.float32)
     return result.astype(jnp.bfloat16)[None]

time: 146 us -> 147 us (level)
    dynamic_update_slice x0 -> x1, other arithmetic: none -> 1.65 us  [on_device(): part = lax.dynamic_update_index_in_dim(part, own_sum, own, 0)]
  transfers between devices with their start and end apart: 7 -> 7, of which waited for: 6 -> 6; matrix products, arithmetic and copies ran while one was open for 3% -> 2% of each run, Pallas kernels for 7% -> 7%
where the time goes in v16:
time: 147 us
  waiting for transfers between devices  101 us (69%)
  Pallas kernels  16.2 us (11%)
  between operations  13.5 us (9%)
  starting transfers between devices  7.27 us (5%)
  other arithmetic  4.18 us (3%)
  matrix products  2.9 us (2%)
  local copies, waits for them, and re-layouts  1.7 us (1%)
    reduce_scatter x1, waiting for transfers between devices, on_device(): part = lax.psum_scatter(part, 'tz', scatter_dimension=0, tiled=False)  45.8 us
    all_gather x1, waiting for transfers between devices, on_device(): gathered = lax.all_gather(gathered, ('tz', 'tc'), axis=0)  44.1 us
    ppermute x4, waiting for transfers between devices, swap(): return lax.ppermute(value, axis, [(0, 1), (1, 0)])  8.45 us
    pallas_call x1, Pallas kernels, gathered_proj(): pl.pallas_call(gathered_proj_kernel, out_shape=jax.ShapeDtypeStruct((weig...  6.6 us
    pallas_call x1, Pallas kernels, out_proj(): pl.pallas_call(out_proj_kernel, out_shape=jax.ShapeDtypeStruct((n_groups,...  6.12 us
    ppermute x4, starting transfers between devices, swap(): return lax.ppermute(value, axis, [(0, 1), (1, 0)])  5.06 us
    pallas_call x1, Pallas kernels, pick_columns(): pl.pallas_call(pick_kernel, out_shape=jax.ShapeDtypeStruct((n_groups, inn...  3.46 us
  transfers between devices with their start and end apart: 7, of which 6 were waited for; matrix products, arithmetic and copies ran while one was open for 2% of the time, Pallas kernels for 7%

profile of v16, /device:TPU:2, one launch (start us, length us, event | category | flops | bytes accessed | tf_op | source)
XLA Modules:
  0.0 146.8 jit_solution(3961315841459834359)
XLA Ops:
  6.5 3.2 %collective-permute-start = (bf16[256,384]{1,0:T(8,128)(2,1)}, bf16[256,384]{1,0:T(8,128)(2,1)S(1)}, u32[]{:S(2)}, u32[]{:S(2)}) collective-permute-start(bf16[256,384]{1,0:T(8,128)(2,1)} %bitcast.45), channel_id=1, source_target_pairs={{0,2},{2,0},{1,3},{3,1},{4,6},{6,4},{5,7},{7,5},{8,10},{10,8},{9,1... | collective-permute-start | bytes 589832 | tf_op jit(solution)/shard_map/ppermute | solution.py:17
  9.7 5.2 %collective-permute-done = bf16[256,384]{1,0:T(8,128)(2,1)S(1)} collective-permute-done((bf16[256,384]{1,0:T(8,128)(2,1)}, bf16[256,384]{1,0:T(8,128)(2,1)S(1)}, u32[]{:S(2)}, u32[]{:S(2)}) %collective-permute-start) | collective-permute-done | bytes 196640 | tf_op jit(solution)/shard_map/ppermute | solution.py:17
  14.9 1.0 select_bitcast_fusion.1
  15.9 0.8 pad_maximum_fusion
  16.7 0.0 reduce-scatter.2.cloned.1.call-start
  16.8 3.5 %shard_map.56 = bf16[16,256,384]{2,1,0:T(8,128)(2,1)} custom-call(s32[1]{0:T(128)S(6)} %sub.17.sel_ref, bf16[256,12288]{1,0:T(8,128)(2,1)} %bitcast.27, bf16[256,12288]{1,0:T(8,128)(2,1)} %bitcast.28, bf16[256,12288]{1,0:T(8,128)(2,1)} %bitcast.29, bf16[256,12288]{1,0:T(8,128)(2,1)} %bitcast.30, bf16[256,12288]{1,0:T(8,128)(2,1)} %bitcast.31, ...), custom_call_target="tpu_custom_call" | custom-call | tf_op jit(solution)/shard_map/pallas_call | solution.py:34
  20.4 0.3 fusion.15
  20.7 1.0 fusion.3
  21.8 44.1 %all-gather.3.cloned.1.call-done.f_ref = bf16[32,256,384]{2,1,0:T(8,128)(2,1)} async-done(((bf16[2,256,384]{2,1,0:T(8,128)(2,1)}), bf16[32,256,384]{2,1,0:T(8,128)(2,1)}) %all-gather.3.cloned.1.call-update) | async-done | bytes 6291472 | tf_op jit(solution)/shard_map/all_gather | solution.py:133
  65.8 6.6 %shard_map.55 = bf16[256,256]{1,0:T(8,128)(2,1)} custom-call(bf16[32,256,384]{2,1,0:T(8,128)(2,1)} %all-gather.3.cloned.1.call-done.f_ref, bf16[12288,256]{1,0:T(8,128)(2,1)} %bitcast.44), custom_call_target="tpu_custom_call" | custom-call | tf_op jit(solution)/shard_map/pallas_call | solution.py:107
  72.4 1.5 %convolution_convert_fusion = bf16[2,128,256]{2,1,0:T(8,128)(2,1)S(1)} fusion(bf16[256,2,128]{0,2,1:T(8,128)(2,1)} %bitcast.46, f32[2,256]{1,0:T(2,128)S(1)} %fusion.15, f32[2,256,256]{1,2,0:T(8,128)} %fusion.3), kind=kOutput, calls=%fused_computation.5 | convolution fusion | flops 34013952 | bytes 788480 | tf_op jit(solution)/shard_map/bhqk,bkhd->bqhd/dot_general | solution.py:149
  74.0 0.1 copy.15.ctx_ref
  74.1 0.3 collective-permute-start.1
  74.4 1.2 collective-permute-done.1.ctx_sib_ref
  75.7 0.4 copy-done
  76.1 6.1 %shard_map.57 = bf16[16,256,384]{2,1,0:T(8,128)(2,1)} custom-call(s32[1]{0:T(128)} %bitcast.core_ref, bf16[256,256]{1,0:T(8,128)(2,1)} %copy-done.2, bf16[256,256]{1,0:T(8,128)(2,1)} %collective-permute-done.1.ctx_sib_ref, bf16[16,256,384]{2,1,0:T(8,128)(2,1)} %copy-done, bf16[256,12288]{1,0:T(8,128)(2,1)} %bitcast.35, bf16[256,12288]{1,0:T(8,128)(2,1)} %bitcast.36, ...), custom_call_target="tpu_custom_call" | custom-call | tf_op jit(solution)/shard_map/pallas_call | solution.py:60
  82.2 1.6 %fusion.4 = bf16[16,256,384]{2,1,0:T(8,128)(2,1)} fusion(bf16[16,256,384]{2,1,0:T(8,128)(2,1)} %shard_map.57, s32[]{:T(128)S(6)} %select_n.34, bf16[1,256,384]{2,1,0:T(8,128)(2,1)S(1)} %copy-done.1), kind=kLoop, calls=%fused_computation.11 | loop fusion | flops 393216 | bytes 589828 | tf_op jit(solution)/shard_map/jit(dynamic_update_index_in_dim)/dynamic_update_slice | solution.py:159
  83.9 45.8 %reduce-scatter.2.cloned.1.call-done = bf16[1,2,256,384]{3,2,1,0:T(8,128)(2,1)} async-done(((bf16[8,2,256,384]{3,2,1,0:T(8,128)(2,1)}), bf16[1,2,256,384]{3,2,1,0:T(8,128)(2,1)}) %reduce-scatter.2.cloned.1.call-update) | async-done | bytes 393232 | tf_op jit(solution)/shard_map/reduce_scatter | solution.py:161
  129.7 1.1 dynamic-slice_bitcast_fusion.1
  130.8 1.5 %collective-permute-start.3 = (bf16[256,384]{1,0:T(8,128)(2,1)S(1)}, bf16[256,384]{1,0:T(8,128)(2,1)S(1)}, u32[]{:S(2)}, u32[]{:S(2)}) collective-permute-start(bf16[256,384]{1,0:T(8,128)(2,1)S(1)} %get-tuple-element.5), channel_id=1, source_target_pairs={{0,128},{128,0},{1,129},{129,1},{2,130},{130,2},{3,131},{131,3},{4... | collective-permute-start | bytes 589832 | tf_op jit(solution)/shard_map/ppermute | solution.py:17
  132.4 2.2 %collective-permute-start.4 = (bf16[256,384]{1,0:T(8,128)(2,1)S(1)}, bf16[256,384]{1,0:T(8,128)(2,1)S(1)}, u32[]{:S(2)}, u32[]{:S(2)}) collective-permute-start(bf16[256,384]{1,0:T(8,128)(2,1)S(1)} %get-tuple-element.6), channel_id=1, source_target_pairs={{0,130},{2,128},{128,2},{130,0},{1,131},{3,129},{129,3},{131,1},{4... | collective-permute-start | bytes 589832 | tf_op jit(solution)/shard_map/ppermute | solution.py:164
  134.5 2.0 %collective-permute-done.3 = bf16[256,384]{1,0:T(8,128)(2,1)S(1)} collective-permute-done((bf16[256,384]{1,0:T(8,128)(2,1)S(1)}, bf16[256,384]{1,0:T(8,128)(2,1)S(1)}, u32[]{:S(2)}, u32[]{:S(2)}) %collective-permute-start.3) | collective-permute-done | bytes 196640 | tf_op jit(solution)/shard_map/ppermute | solution.py:17
  136.6 2.7 %collective-permute-done.4 = bf16[256,384]{1,0:T(8,128)(2,1)S(1)} collective-permute-done((bf16[256,384]{1,0:T(8,128)(2,1)S(1)}, bf16[256,384]{1,0:T(8,128)(2,1)S(1)}, u32[]{:S(2)}, u32[]{:S(2)}) %collective-permute-start.4) | collective-permute-done | bytes 196640 | tf_op jit(solution)/shard_map/ppermute | solution.py:164
  139.2 0.7 fusion.5
  (17 shorter events, 0.2 us)
Async XLA Ops:
  6.5 59.3 %all-gather.3.cloned.1.call-start = ((), (), s32[]{:S(2)}) async-start(), calls=%async_computation.2 | async-start | bytes 6684672 | tf_op jit(solution)/shard_map/all_gather | solution.py:133
  6.5 8.4 %collective-permute-start = (bf16[256,384]{1,0:T(8,128)(2,1)}, bf16[256,384]{1,0:T(8,128)(2,1)S(1)}, u32[]{:S(2)}, u32[]{:S(2)}) collective-permute-start(bf16[256,384]{1,0:T(8,128)(2,1)} %bitcast.45), channel_id=1, source_target_pairs={{0,2},{2,0},{1,3},{3,1},{4,6},{6,4},{5,7},{7,5},{8,10},{10,8},{9,1... | collective-permute-start | bytes 589832 | tf_op jit(solution)/shard_map/ppermute | solution.py:17
  16.7 113.0 %reduce-scatter.2.cloned.1.call-start = ((), (), s32[]{:S(2)}) async-start(), calls=%async_computation.1 | async-start | bytes 3538944 | tf_op jit(solution)/shard_map/reduce_scatter | solution.py:161
  16.7 3.5 %copy-start.3 = (bf16[1,256,256]{2,1,0:T(8,128)(2,1)S(1)}, bf16[1,256,256]{2,1,0:T(8,128)(2,1)}, u32[]{:S(2)}) copy-start(bf16[1,256,256]{2,1,0:T(8,128)(2,1)} %param.6) | copy-start | bytes 393220
  16.8 3.5 %copy-start.4 = (bf16[1,256,256]{2,1,0:T(8,128)(2,1)S(1)}, bf16[1,256,256]{2,1,0:T(8,128)(2,1)}, u32[]{:S(2)}) copy-start(bf16[1,256,256]{2,1,0:T(8,128)(2,1)} %param.7) | copy-start | bytes 393220
  20.2 54.2 %collective-permute-start.2 = (bf16[16,256,384]{2,1,0:T(8,128)(2,1)}, bf16[16,256,384]{2,1,0:T(8,128)(2,1)S(1)}, u32[]{:S(2)}, u32[]{:S(2)}) collective-permute-start(bf16[16,256,384]{2,1,0:T(8,128)(2,1)} %shard_map.56), channel_id=1, source_target_pairs={{0,1},{1,0},{2,3},{3,2},{4,5},{5,4},{6,7},{7,6},{8,9},{9,8},{10,11... | collective-permute-start | bytes 9437192 | tf_op jit(solution)/shard_map/ppermute | solution.py:17
  74.1 1.6 %copy-start.2 = (bf16[256,256]{1,0:T(8,128)(2,1)}, bf16[256,256]{1,0:T(8,128)(2,1)S(1)}, u32[]{:S(2)}) copy-start(bf16[256,256]{1,0:T(8,128)(2,1)S(1)} %copy.15.ctx_ref) | copy-start | bytes 393220
  74.1 1.6 %collective-permute-start.1 = (bf16[256,256]{1,0:T(8,128)(2,1)S(1)}, bf16[256,256]{1,0:T(8,128)(2,1)}, u32[]{:S(2)}, u32[]{:S(2)}) collective-permute-start(bf16[256,256]{1,0:T(8,128)(2,1)S(1)} %copy.15.ctx_ref), channel_id=1, source_target_pairs={{0,1},{1,0},{2,3},{3,2},{4,5},{5,4},{6,7},{7,6},{8,9},{9,8},{10,11... | collective-permute-start | bytes 393224 | tf_op jit(solution)/shard_map/ppermute | solution.py:17
  74.4 7.8 %copy-start.1 = (bf16[1,256,384]{2,1,0:T(8,128)(2,1)S(1)}, bf16[1,256,384]{2,1,0:T(8,128)(2,1)}, u32[]{:S(2)}) copy-start(bf16[1,256,384]{2,1,0:T(8,128)(2,1)} %param.5) | copy-start | bytes 589828
  74.4 1.7 %copy-start = (bf16[16,256,384]{2,1,0:T(8,128)(2,1)}, bf16[16,256,384]{2,1,0:T(8,128)(2,1)S(1)}, u32[]{:S(2)}) copy-start(bf16[16,256,384]{2,1,0:T(8,128)(2,1)S(1)} %collective-permute-done.2.w_sib_ref) | copy-start | bytes 9437188
  130.8 5.8 %collective-permute-start.3 = (bf16[256,384]{1,0:T(8,128)(2,1)S(1)}, bf16[256,384]{1,0:T(8,128)(2,1)S(1)}, u32[]{:S(2)}, u32[]{:S(2)}) collective-permute-start(bf16[256,384]{1,0:T(8,128)(2,1)S(1)} %get-tuple-element.5), channel_id=1, source_target_pairs={{0,128},{128,0},{1,129},{129,1},{2,130},{130,2},{3,131},{131,3},{4... | collective-permute-start | bytes 589832 | tf_op jit(solution)/shard_map/ppermute | solution.py:17
  132.4 6.9 %collective-permute-start.4 = (bf16[256,384]{1,0:T(8,128)(2,1)S(1)}, bf16[256,384]{1,0:T(8,128)(2,1)S(1)}, u32[]{:S(2)}, u32[]{:S(2)}) collective-permute-start(bf16[256,384]{1,0:T(8,128)(2,1)S(1)} %get-tuple-element.6), channel_id=1, source_target_pairs={{0,130},{2,128},{128,2},{130,0},{1,131},{3,129},{129,3},{131,1},{4... | collective-permute-start | bytes 589832 | tf_op jit(solution)/shard_map/ppermute | solution.py:164
Sparse Core Ops, SparseCore 0:
  16.8 48.9 all-gather.2
  84.0 45.6 reduce-scatter.1

commit v17 on v14

--- a/solution.py
+++ b/solution.py
@@ -9,8 +9,8 @@
 HEAD_SIZE = 128
 LEN = 256
 N_Z, N_Y, N_C = 8, 2, 2
-GROUPS_PER_STEP = 8
-Z_PER_STEP = 4
+GROUPS_PER_STEP = 16
+Z_PER_STEP = 8
 
 
 def swap(value, axis):

time: 146 us -> 148 us (1.014)
  Pallas kernels: 16.1 us -> 18.5 us
  transfers between devices with their start and end apart: 7 -> 7, of which waited for: 6 -> 6; matrix products, arithmetic and copies ran while one was open for 3% -> 3% of each run, Pallas kernels for 7% -> 8%
where the time goes in v17:
time: 148 us
  waiting for transfers between devices  99.7 us (67%)
  Pallas kernels  18.5 us (12%)
  between operations  13.5 us (9%)
  starting transfers between devices  7.28 us (5%)
  other arithmetic  3.49 us (2%)
  matrix products  2.88 us (2%)
  local copies, waits for them, and re-layouts  2.47 us (2%)
    reduce_scatter x1, waiting for transfers between devices, on_device(): part = lax.psum_scatter(part, 'tz', scatter_dimension=0, tiled=False)  45.9 us
    all_gather x1, waiting for transfers between devices, on_device(): gathered = lax.all_gather(gathered, ('tz', 'tc'), axis=0)  42.7 us
    pallas_call x1, Pallas kernels, gathered_proj(): pl.pallas_call(gathered_proj_kernel, out_shape=jax.ShapeDtypeStruct((weig...  7.63 us
    ppermute x4, waiting for transfers between devices, swap(): return lax.ppermute(value, axis, [(0, 1), (1, 0)])  7.49 us
    pallas_call x1, Pallas kernels, out_proj(): pl.pallas_call(out_proj_kernel, out_shape=jax.ShapeDtypeStruct((n_groups,...  6.94 us
    ppermute x4, starting transfers between devices, swap(): return lax.ppermute(value, axis, [(0, 1), (1, 0)])  4.93 us
    pallas_call x1, Pallas kernels, pick_columns(): pl.pallas_call(pick_kernel, out_shape=jax.ShapeDtypeStruct((n_groups, inn...  3.97 us
    ppermute x1, waiting for transfers between devices, on_device(): lax.ppermute(send, ('section', 'ty'), [(i, 3 - i) for i in range(4)])  3.57 us
  transfers between devices with their start and end apart: 7, of which 6 were waited for; matrix products, arithmetic and copies ran while one was open for 3% of the time, Pallas kernels for 8%

profile of v17, /device:TPU:2, one launch (start us, length us, event | category | flops | bytes accessed | tf_op | source)
XLA Modules:
  0.0 147.9 jit_solution(16399858482909025119)
XLA Ops:
  6.5 3.2 %collective-permute-start = (bf16[256,384]{1,0:T(8,128)(2,1)}, bf16[256,384]{1,0:T(8,128)(2,1)S(1)}, u32[]{:S(2)}, u32[]{:S(2)}) collective-permute-start(bf16[256,384]{1,0:T(8,128)(2,1)} %bitcast.63), channel_id=1, source_target_pairs={{0,2},{2,0},{1,3},{3,1},{4,6},{6,4},{5,7},{7,5},{8,10},{10,8},{9,1... | collective-permute-start | bytes 589832 | tf_op jit(solution)/shard_map/ppermute | solution.py:17
  9.7 5.2 %collective-permute-done = bf16[256,384]{1,0:T(8,128)(2,1)S(1)} collective-permute-done((bf16[256,384]{1,0:T(8,128)(2,1)}, bf16[256,384]{1,0:T(8,128)(2,1)S(1)}, u32[]{:S(2)}, u32[]{:S(2)}) %collective-permute-start) | collective-permute-done | bytes 196640 | tf_op jit(solution)/shard_map/ppermute | solution.py:17
  14.9 1.0 select_bitcast_fusion.1
  15.9 0.8 pad_maximum_fusion
  16.7 4.0 %shard_map.56 = bf16[16,256,384]{2,1,0:T(8,128)(2,1)} custom-call(s32[1]{0:T(128)S(6)} %sub.17.sel_ref, bf16[256,12288]{1,0:T(8,128)(2,1)} %bitcast.44, bf16[256,12288]{1,0:T(8,128)(2,1)} %bitcast.30, bf16[256,12288]{1,0:T(8,128)(2,1)} %bitcast.31, bf16[256,12288]{1,0:T(8,128)(2,1)} %bitcast.32, bf16[256,12288]{1,0:T(8,128)(2,1)} %bitcast.33, ...), custom_call_target="tpu_custom_call" | custom-call | tf_op jit(solution)/shard_map/pallas_call | solution.py:34
  20.8 0.9 reshape.65
  21.7 0.3 fusion.15
  22.1 1.0 fusion.3
  23.1 42.7 %all-gather.3.cloned.1.call-done.f_ref = bf16[32,256,384]{2,1,0:T(8,128)(2,1)} async-done(((bf16[2,256,384]{2,1,0:T(8,128)(2,1)}), bf16[32,256,384]{2,1,0:T(8,128)(2,1)}) %all-gather.3.cloned.1.call-update) | async-done | bytes 6291472 | tf_op jit(solution)/shard_map/all_gather | solution.py:133
  65.8 7.6 %shard_map.55 = bf16[256,256]{1,0:T(8,128)(2,1)} custom-call(bf16[32,256,384]{2,1,0:T(8,128)(2,1)} %all-gather.3.cloned.1.call-done.f_ref, bf16[12288,256]{1,0:T(8,128)(2,1)} %bitcast.62), custom_call_target="tpu_custom_call" | custom-call | tf_op jit(solution)/shard_map/pallas_call | solution.py:107
  73.5 1.5 %convolution_convert_fusion = bf16[2,128,256]{2,1,0:T(8,128)(2,1)S(1)} fusion(bf16[256,2,128]{0,2,1:T(8,128)(2,1)} %bitcast.64, f32[2,256]{1,0:T(2,128)S(1)} %fusion.15, f32[2,256,256]{1,2,0:T(8,128)} %fusion.3), kind=kOutput, calls=%fused_computation.5 | convolution fusion | flops 34013952 | bytes 788480 | tf_op jit(solution)/shard_map/bhqk,bkhd->bqhd/dot_general | solution.py:149
  75.0 0.1 copy.15.ctx_ref
  75.1 0.3 collective-permute-start.1
  75.4 1.2 collective-permute-done.1.ctx_sib_ref
  76.7 0.4 copy-done
  77.1 6.9 %shard_map.57 = bf16[16,256,384]{2,1,0:T(8,128)(2,1)} custom-call(s32[1]{0:T(128)} %bitcast.core_ref, bf16[256,256]{1,0:T(8,128)(2,1)} %copy-done.2, bf16[256,256]{1,0:T(8,128)(2,1)} %collective-permute-done.1.ctx_sib_ref, bf16[16,256,384]{2,1,0:T(8,128)(2,1)} %copy-done, bf16[256,12288]{1,0:T(8,128)(2,1)} %bitcast.45, bf16[256,12288]{1,0:T(8,128)(2,1)} %bitcast.46, ...), custom_call_target="tpu_custom_call" | custom-call | tf_op jit(solution)/shard_map/pallas_call | solution.py:60
  84.1 45.9 %reduce-scatter.2.cloned.1.call-done = bf16[1,2,256,384]{3,2,1,0:T(8,128)(2,1)} async-done(((bf16[8,2,256,384]{3,2,1,0:T(8,128)(2,1)}), bf16[1,2,256,384]{3,2,1,0:T(8,128)(2,1)}) %reduce-scatter.2.cloned.1.call-update) | async-done | bytes 393232 | tf_op jit(solution)/shard_map/reduce_scatter | solution.py:156
  130.0 1.0 fusion.4
  131.0 1.4 collective-permute-start.3
  132.4 0.9 dynamic-slice_bitcast_fusion
  133.3 2.3 %collective-permute-start.4 = (bf16[256,384]{1,0:T(8,128)(2,1)S(1)}, bf16[256,384]{1,0:T(8,128)(2,1)S(1)}, u32[]{:S(2)}, u32[]{:S(2)}) collective-permute-start(bf16[256,384]{1,0:T(8,128)(2,1)S(1)} %dynamic-slice_bitcast_fusion), channel_id=1, source_target_pairs={{0,130},{2,128},{128,2},{130,0},{1,131},{3,129},{129,3},{131,1},{4... | collective-permute-start | bytes 589832 | tf_op jit(solution)/shard_map/ppermute | solution.py:161
  135.7 1.1 collective-permute-done.3
  136.7 3.6 %collective-permute-done.4 = bf16[256,384]{1,0:T(8,128)(2,1)S(1)} collective-permute-done((bf16[256,384]{1,0:T(8,128)(2,1)S(1)}, bf16[256,384]{1,0:T(8,128)(2,1)S(1)}, u32[]{:S(2)}, u32[]{:S(2)}) %collective-permute-start.4) | collective-permute-done | bytes 196640 | tf_op jit(solution)/shard_map/ppermute | solution.py:161
  140.3 0.7 fusion.5
  (15 shorter events, 0.2 us)
Async XLA Ops:
  6.5 59.3 %all-gather.3.cloned.1.call-start = ((), (), s32[]{:S(2)}) async-start(), calls=%async_computation.2 | async-start | bytes 6684672 | tf_op jit(solution)/shard_map/all_gather | solution.py:133
  6.5 8.4 %collective-permute-start = (bf16[256,384]{1,0:T(8,128)(2,1)}, bf16[256,384]{1,0:T(8,128)(2,1)S(1)}, u32[]{:S(2)}, u32[]{:S(2)}) collective-permute-start(bf16[256,384]{1,0:T(8,128)(2,1)} %bitcast.63), channel_id=1, source_target_pairs={{0,2},{2,0},{1,3},{3,1},{4,6},{6,4},{5,7},{7,5},{8,10},{10,8},{9,1... | collective-permute-start | bytes 589832 | tf_op jit(solution)/shard_map/ppermute | solution.py:17
  16.7 113.3 %reduce-scatter.2.cloned.1.call-start = ((), (), s32[]{:S(2)}) async-start(), calls=%async_computation.1 | async-start | bytes 3538944 | tf_op jit(solution)/shard_map/reduce_scatter | solution.py:156
  16.7 4.0 %copy-start.3 = (bf16[1,256,256]{2,1,0:T(8,128)(2,1)S(1)}, bf16[1,256,256]{2,1,0:T(8,128)(2,1)}, u32[]{:S(2)}) copy-start(bf16[1,256,256]{2,1,0:T(8,128)(2,1)} %param.6) | copy-start | bytes 393220
  20.7 54.7 %collective-permute-start.2 = (bf16[16,256,384]{2,1,0:T(8,128)(2,1)}, bf16[16,256,384]{2,1,0:T(8,128)(2,1)S(1)}, u32[]{:S(2)}, u32[]{:S(2)}) collective-permute-start(bf16[16,256,384]{2,1,0:T(8,128)(2,1)} %shard_map.56), channel_id=1, source_target_pairs={{0,1},{1,0},{2,3},{3,2},{4,5},{5,4},{6,7},{7,6},{8,9},{9,8},{10,11... | collective-permute-start | bytes 9437192 | tf_op jit(solution)/shard_map/ppermute | solution.py:17
  75.1 1.6 %copy-start.2 = (bf16[256,256]{1,0:T(8,128)(2,1)}, bf16[256,256]{1,0:T(8,128)(2,1)S(1)}, u32[]{:S(2)}) copy-start(bf16[256,256]{1,0:T(8,128)(2,1)S(1)} %copy.15.ctx_ref) | copy-start | bytes 393220
  75.1 54.9 %copy-start.1 = (bf16[1,256,384]{2,1,0:T(8,128)(2,1)S(1)}, bf16[1,256,384]{2,1,0:T(8,128)(2,1)}, u32[]{:S(2)}) copy-start(bf16[1,256,384]{2,1,0:T(8,128)(2,1)} %param.5) | copy-start | bytes 589828
  75.1 1.6 %collective-permute-start.1 = (bf16[256,256]{1,0:T(8,128)(2,1)S(1)}, bf16[256,256]{1,0:T(8,128)(2,1)}, u32[]{:S(2)}, u32[]{:S(2)}) collective-permute-start(bf16[256,256]{1,0:T(8,128)(2,1)S(1)} %copy.15.ctx_ref), channel_id=1, source_target_pairs={{0,1},{1,0},{2,3},{3,2},{4,5},{5,4},{6,7},{7,6},{8,9},{9,8},{10,11... | collective-permute-start | bytes 393224 | tf_op jit(solution)/shard_map/ppermute | solution.py:17
  75.4 1.7 %copy-start = (bf16[16,256,384]{2,1,0:T(8,128)(2,1)}, bf16[16,256,384]{2,1,0:T(8,128)(2,1)S(1)}, u32[]{:S(2)}) copy-start(bf16[16,256,384]{2,1,0:T(8,128)(2,1)S(1)} %collective-permute-done.2.w_sib_ref) | copy-start | bytes 9437188
  131.0 5.8 %collective-permute-start.3 = (bf16[256,384]{1,0:T(8,128)(2,1)S(1)}, bf16[256,384]{1,0:T(8,128)(2,1)S(1)}, u32[]{:S(2)}, u32[]{:S(2)}) collective-permute-start(bf16[256,384]{1,0:T(8,128)(2,1)S(1)} %fusion.4), channel_id=1, source_target_pairs={{0,128},{128,0},{1,129},{129,1},{2,130},{130,2},{3,131},{131,3},{4... | collective-permute-start | bytes 589832 | tf_op jit(solution)/shard_map/ppermute | solution.py:17
  133.3 7.0 %collective-permute-start.4 = (bf16[256,384]{1,0:T(8,128)(2,1)S(1)}, bf16[256,384]{1,0:T(8,128)(2,1)S(1)}, u32[]{:S(2)}, u32[]{:S(2)}) collective-permute-start(bf16[256,384]{1,0:T(8,128)(2,1)S(1)} %dynamic-slice_bitcast_fusion), channel_id=1, source_target_pairs={{0,130},{2,128},{128,2},{130,0},{1,131},{3,129},{129,3},{131,1},{4... | collective-permute-start | bytes 589832 | tf_op jit(solution)/shard_map/ppermute | solution.py:161
Sparse Core Ops, SparseCore 0:
  16.8 48.9 all-gather.2
  84.2 45.7 reduce-scatter.1

commit v18 on v14

--- a/solution.py
+++ b/solution.py
@@ -127,9 +127,9 @@
 
     core = lax.axis_index("tc").astype(jnp.int32).reshape(1)
     weight_from_sib = swap(pick_columns(1 - core, weight_o, col_width), "tc")
-    y_first = lax.axis_index("ty") == 0
     other = swap(activ, "ty")
-    gathered = jnp.stack([jnp.where(y_first, activ, other), jnp.where(y_first, other, activ)])
+    slot = lax.broadcasted_iota(jnp.int32, (N_Y, 1, 1), 0)
+    gathered = jnp.where(slot == lax.axis_index("ty"), activ[None], other[None])
     gathered = lax.all_gather(gathered, ("tz", "tc"), axis=0)
     values = gathered_proj(gathered, weight_v).T
 

time: 146 us -> 146 us (level)
    select_n x0 -> x1, other arithmetic: none -> 1.79 us  [on_device(): gathered = jnp.where(slot == lax.axis_index('ty'), activ[None], other[None])]
    another operation x2 -> x0, other arithmetic: 1.76 us -> none  [on_device(): jnp.stack([jnp.where(y_first, activ, other), jnp.where(y_first, other, ac...]
where the time goes in v18:
time: 146 us
  waiting for transfers between devices  101 us (69%)
  Pallas kernels  16.2 us (11%)
  between operations  13.5 us (9%)
  starting transfers between devices  6.74 us (5%)
  other arithmetic  3.53 us (2%)
  matrix products  2.88 us (2%)
  local copies, waits for them, and re-layouts  2.46 us (2%)
    reduce_scatter x1, waiting for transfers between devices, on_device(): part = lax.psum_scatter(part, 'tz', scatter_dimension=0, tiled=False)  45.8 us
    all_gather x1, waiting for transfers between devices, on_device(): gathered = lax.all_gather(gathered, ('tz', 'tc'), axis=0)  43.3 us
    ppermute x4, waiting for transfers between devices, swap(): return lax.ppermute(value, axis, [(0, 1), (1, 0)])  9 us
    pallas_call x1, Pallas kernels, gathered_proj(): pl.pallas_call(gathered_proj_kernel, out_shape=jax.ShapeDtypeStruct((weig...  6.6 us
    pallas_call x1, Pallas kernels, out_proj(): pl.pallas_call(out_proj_kernel, out_shape=jax.ShapeDtypeStruct((n_groups,...  6.12 us
    ppermute x4, starting transfers between devices, swap(): return lax.ppermute(value, axis, [(0, 1), (1, 0)])  3.87 us
    pallas_call x1, Pallas kernels, pick_columns(): pl.pallas_call(pick_kernel, out_shape=jax.ShapeDtypeStruct((n_groups, inn...  3.43 us
  transfers between devices with their start and end apart: 7, of which 6 were waited for; matrix products, arithmetic and copies ran while one was open for 3% of the time, Pallas kernels for 7%

profile of v18, /device:TPU:2, one launch (start us, length us, event | category | flops | bytes accessed | tf_op | source)
XLA Modules:
  0.0 146.1 jit_solution(1864931416187614869)
XLA Ops:
  6.5 3.2 %collective-permute-start = (bf16[256,384]{1,0:T(8,128)(2,1)}, bf16[256,384]{1,0:T(8,128)(2,1)S(1)}, u32[]{:S(2)}, u32[]{:S(2)}) collective-permute-start(bf16[256,384]{1,0:T(8,128)(2,1)} %bitcast.43), channel_id=1, source_target_pairs={{0,2},{2,0},{1,3},{3,1},{4,6},{6,4},{5,7},{7,5},{8,10},{10,8},{9,1... | collective-permute-start | bytes 589832 | tf_op jit(solution)/shard_map/ppermute | solution.py:17
  9.7 5.2 %collective-permute-done = bf16[256,384]{1,0:T(8,128)(2,1)S(1)} collective-permute-done((bf16[256,384]{1,0:T(8,128)(2,1)}, bf16[256,384]{1,0:T(8,128)(2,1)S(1)}, u32[]{:S(2)}, u32[]{:S(2)}) %collective-permute-start) | collective-permute-done | bytes 196640 | tf_op jit(solution)/shard_map/ppermute | solution.py:17
  14.9 1.8 %broadcast_select_fusion = bf16[1,2,256,384]{3,2,1,0:T(8,128)(2,1)} fusion(pred[2]{0:T(512)(128)(4,1)S(1)} %iota_compare_fusion.1, bf16[256,384]{1,0:T(8,128)(2,1)S(1)} %collective-permute-done, bf16[256,384]{1,0:T(8,128)(2,1)} %bitcast.44), kind=kLoop, calls=%fused_computation.10 | loop fusion | flops 196608 | bytes 786434 | tf_op jit(solution)/shard_map/jit(_where)/select_n | solution.py:132
  16.7 0.0 reduce-scatter.2.cloned.1.call-start
  16.8 3.4 %shard_map.56 = bf16[16,256,384]{2,1,0:T(8,128)(2,1)} custom-call(s32[1]{0:T(128)S(6)} %sub.17.sel_ref, bf16[256,12288]{1,0:T(8,128)(2,1)} %bitcast.24, bf16[256,12288]{1,0:T(8,128)(2,1)} %bitcast.25, bf16[256,12288]{1,0:T(8,128)(2,1)} %bitcast.26, bf16[256,12288]{1,0:T(8,128)(2,1)} %bitcast.27, bf16[256,12288]{1,0:T(8,128)(2,1)} %bitcast.28, ...), custom_call_target="tpu_custom_call" | custom-call | tf_op jit(solution)/shard_map/pallas_call | solution.py:34
  20.3 0.9 reshape.74
  21.2 0.3 fusion.15
  21.6 1.0 fusion.3
  22.6 43.3 %all-gather.2.cloned.1.call-done = bf16[16,2,256,384]{3,2,1,0:T(8,128)(2,1)} async-done(((bf16[1,2,256,384]{3,2,1,0:T(8,128)(2,1)}), bf16[16,2,256,384]{3,2,1,0:T(8,128)(2,1)}) %all-gather.2.cloned.1.call-update) | async-done | bytes 6291472 | tf_op jit(solution)/shard_map/all_gather | solution.py:133
  65.9 6.6 %shard_map.55 = bf16[256,256]{1,0:T(8,128)(2,1)} custom-call(bf16[32,256,384]{2,1,0:T(8,128)(2,1)} %bitcast.42, bf16[12288,256]{1,0:T(8,128)(2,1)} %bitcast.41), custom_call_target="tpu_custom_call" | custom-call | tf_op jit(solution)/shard_map/pallas_call | solution.py:107
  72.5 1.5 %convolution_convert_fusion = bf16[2,128,256]{2,1,0:T(8,128)(2,1)S(1)} fusion(bf16[256,2,128]{0,2,1:T(8,128)(2,1)} %bitcast.45, f32[2,256]{1,0:T(2,128)S(1)} %fusion.15, f32[2,256,256]{1,2,0:T(8,128)} %fusion.3), kind=kOutput, calls=%fused_computation.5 | convolution fusion | flops 34013952 | bytes 788480 | tf_op jit(solution)/shard_map/bhqk,bkhd->bqhd/dot_general | solution.py:149
  74.0 0.1 copy.15.ctx_ref
  74.1 0.3 collective-permute-start.1
  74.4 1.2 collective-permute-done.1.ctx_sib_ref
  75.7 0.4 copy-done
  76.1 6.1 %shard_map.57 = bf16[16,256,384]{2,1,0:T(8,128)(2,1)} custom-call(s32[1]{0:T(128)} %bitcast.core_ref, bf16[256,256]{1,0:T(8,128)(2,1)} %copy-done.2, bf16[256,256]{1,0:T(8,128)(2,1)} %collective-permute-done.1.ctx_sib_ref, bf16[16,256,384]{2,1,0:T(8,128)(2,1)} %copy-done, bf16[256,12288]{1,0:T(8,128)(2,1)} %bitcast.32, bf16[256,12288]{1,0:T(8,128)(2,1)} %bitcast.33, ...), custom_call_target="tpu_custom_call" | custom-call | tf_op jit(solution)/shard_map/pallas_call | solution.py:60
  82.2 45.8 %reduce-scatter.2.cloned.1.call-done = bf16[1,2,256,384]{3,2,1,0:T(8,128)(2,1)} async-done(((bf16[8,2,256,384]{3,2,1,0:T(8,128)(2,1)}), bf16[1,2,256,384]{3,2,1,0:T(8,128)(2,1)}) %reduce-scatter.2.cloned.1.call-update) | async-done | bytes 393232 | tf_op jit(solution)/shard_map/reduce_scatter | solution.py:156
  128.1 0.9 dynamic-slice_bitcast_fusion
  129.0 2.8 %collective-permute-start.4 = (bf16[256,384]{1,0:T(8,128)(2,1)S(1)}, bf16[256,384]{1,0:T(8,128)(2,1)S(1)}, u32[]{:S(2)}, u32[]{:S(2)}) collective-permute-start(bf16[256,384]{1,0:T(8,128)(2,1)S(1)} %dynamic-slice_bitcast_fusion), channel_id=1, source_target_pairs={{0,130},{2,128},{128,2},{130,0},{1,131},{3,129},{129,3},{131,1},{4... | collective-permute-start | bytes 589832 | tf_op jit(solution)/shard_map/ppermute | solution.py:161
  131.8 1.0 fusion.4
  132.8 0.4 collective-permute-start.3
  133.2 2.8 %collective-permute-done.4 = bf16[256,384]{1,0:T(8,128)(2,1)S(1)} collective-permute-done((bf16[256,384]{1,0:T(8,128)(2,1)S(1)}, bf16[256,384]{1,0:T(8,128)(2,1)S(1)}, u32[]{:S(2)}, u32[]{:S(2)}) %collective-permute-start.4) | collective-permute-done | bytes 196640 | tf_op jit(solution)/shard_map/ppermute | solution.py:161
  136.0 2.6 %collective-permute-done.3 = bf16[256,384]{1,0:T(8,128)(2,1)S(1)} collective-permute-done((bf16[256,384]{1,0:T(8,128)(2,1)S(1)}, bf16[256,384]{1,0:T(8,128)(2,1)S(1)}, u32[]{:S(2)}, u32[]{:S(2)}) %collective-permute-start.3) | collective-permute-done | bytes 196640 | tf_op jit(solution)/shard_map/ppermute | solution.py:17
  138.6 0.7 fusion.5
  (15 shorter events, 0.1 us)
Async XLA Ops:
  6.5 59.3 %all-gather.2.cloned.1.call-start = ((), (), s32[]{:S(2)}) async-start(), calls=%async_computation.1 | async-start | bytes 6684672 | tf_op jit(solution)/shard_map/all_gather | solution.py:133
  6.5 8.4 %collective-permute-start = (bf16[256,384]{1,0:T(8,128)(2,1)}, bf16[256,384]{1,0:T(8,128)(2,1)S(1)}, u32[]{:S(2)}, u32[]{:S(2)}) collective-permute-start(bf16[256,384]{1,0:T(8,128)(2,1)} %bitcast.43), channel_id=1, source_target_pairs={{0,2},{2,0},{1,3},{3,1},{4,6},{6,4},{5,7},{7,5},{8,10},{10,8},{9,1... | collective-permute-start | bytes 589832 | tf_op jit(solution)/shard_map/ppermute | solution.py:17
  16.7 111.4 %reduce-scatter.2.cloned.1.call-start = ((), (), s32[]{:S(2)}) async-start(), calls=%async_computation.2 | async-start | bytes 3538944 | tf_op jit(solution)/shard_map/reduce_scatter | solution.py:156
  16.8 3.5 %copy-start.3 = (bf16[1,256,256]{2,1,0:T(8,128)(2,1)S(1)}, bf16[1,256,256]{2,1,0:T(8,128)(2,1)}, u32[]{:S(2)}) copy-start(bf16[1,256,256]{2,1,0:T(8,128)(2,1)} %param.6) | copy-start | bytes 393220
  20.2 54.2 %collective-permute-start.2 = (bf16[16,256,384]{2,1,0:T(8,128)(2,1)}, bf16[16,256,384]{2,1,0:T(8,128)(2,1)S(1)}, u32[]{:S(2)}, u32[]{:S(2)}) collective-permute-start(bf16[16,256,384]{2,1,0:T(8,128)(2,1)} %shard_map.56), channel_id=1, source_target_pairs={{0,1},{1,0},{2,3},{3,2},{4,5},{5,4},{6,7},{7,6},{8,9},{9,8},{10,11... | collective-permute-start | bytes 9437192 | tf_op jit(solution)/shard_map/ppermute | solution.py:17
  74.1 1.6 %copy-start.2 = (bf16[256,256]{1,0:T(8,128)(2,1)}, bf16[256,256]{1,0:T(8,128)(2,1)S(1)}, u32[]{:S(2)}) copy-start(bf16[256,256]{1,0:T(8,128)(2,1)S(1)} %copy.15.ctx_ref) | copy-start | bytes 393220
  74.1 57.7 %copy-start.1 = (bf16[1,256,384]{2,1,0:T(8,128)(2,1)S(1)}, bf16[1,256,384]{2,1,0:T(8,128)(2,1)}, u32[]{:S(2)}) copy-start(bf16[1,256,384]{2,1,0:T(8,128)(2,1)} %param.5) | copy-start | bytes 589828
  74.1 1.6 %collective-permute-start.1 = (bf16[256,256]{1,0:T(8,128)(2,1)S(1)}, bf16[256,256]{1,0:T(8,128)(2,1)}, u32[]{:S(2)}, u32[]{:S(2)}) collective-permute-start(bf16[256,256]{1,0:T(8,128)(2,1)S(1)} %copy.15.ctx_ref), channel_id=1, source_target_pairs={{0,1},{1,0},{2,3},{3,2},{4,5},{5,4},{6,7},{7,6},{8,9},{9,8},{10,11... | collective-permute-start | bytes 393224 | tf_op jit(solution)/shard_map/ppermute | solution.py:17
  74.4 1.7 %copy-start = (bf16[16,256,384]{2,1,0:T(8,128)(2,1)}, bf16[16,256,384]{2,1,0:T(8,128)(2,1)S(1)}, u32[]{:S(2)}) copy-start(bf16[16,256,384]{2,1,0:T(8,128)(2,1)S(1)} %collective-permute-done.2.w_sib_ref) | copy-start | bytes 9437188
  129.0 7.0 %collective-permute-start.4 = (bf16[256,384]{1,0:T(8,128)(2,1)S(1)}, bf16[256,384]{1,0:T(8,128)(2,1)S(1)}, u32[]{:S(2)}, u32[]{:S(2)}) collective-permute-start(bf16[256,384]{1,0:T(8,128)(2,1)S(1)} %dynamic-slice_bitcast_fusion), channel_id=1, source_target_pairs={{0,130},{2,128},{128,2},{130,0},{1,131},{3,129},{129,3},{131,1},{4... | collective-permute-start | bytes 589832 | tf_op jit(solution)/shard_map/ppermute | solution.py:161
  132.8 5.8 %collective-permute-start.3 = (bf16[256,384]{1,0:T(8,128)(2,1)S(1)}, bf16[256,384]{1,0:T(8,128)(2,1)S(1)}, u32[]{:S(2)}, u32[]{:S(2)}) collective-permute-start(bf16[256,384]{1,0:T(8,128)(2,1)S(1)} %fusion.4), channel_id=1, source_target_pairs={{0,128},{128,0},{1,129},{129,1},{2,130},{130,2},{3,131},{131,3},{4... | collective-permute-start | bytes 589832 | tf_op jit(solution)/shard_map/ppermute | solution.py:17
Sparse Core Ops, SparseCore 0:
  16.8 48.9 all-gather.1
  82.4 45.6 reduce-scatter.1

commit v19 on v14

--- a/solution.py
+++ b/solution.py
@@ -10,7 +10,7 @@
 LEN = 256
 N_Z, N_Y, N_C = 8, 2, 2
 GROUPS_PER_STEP = 8
-Z_PER_STEP = 4
+Z_PER_STEP = 2
 
 
 def swap(value, axis):

time: 146 us -> 147 us (level)
  no operation moved by 1% of the time
where the time goes in v19:
time: 147 us
  waiting for transfers between devices  100 us (68%)
  Pallas kernels  16.7 us (11%)
  between operations  13.5 us (9%)
  starting transfers between devices  7.31 us (5%)
  other arithmetic  3.49 us (2%)
  matrix products  2.88 us (2%)
  local copies, waits for them, and re-layouts  2.47 us (2%)
    reduce_scatter x1, waiting for transfers between devices, on_device(): part = lax.psum_scatter(part, 'tz', scatter_dimension=0, tiled=False)  45.8 us
    all_gather x1, waiting for transfers between devices, on_device(): gathered = lax.all_gather(gathered, ('tz', 'tc'), axis=0)  43.3 us
    ppermute x4, waiting for transfers between devices, swap(): return lax.ppermute(value, axis, [(0, 1), (1, 0)])  7.46 us
    pallas_call x1, Pallas kernels, gathered_proj(): pl.pallas_call(gathered_proj_kernel, out_shape=jax.ShapeDtypeStruct((weig...  7.12 us
    pallas_call x1, Pallas kernels, out_proj(): pl.pallas_call(out_proj_kernel, out_shape=jax.ShapeDtypeStruct((n_groups,...  6.12 us
    ppermute x4, starting transfers between devices, swap(): return lax.ppermute(value, axis, [(0, 1), (1, 0)])  5.05 us
    ppermute x1, waiting for transfers between devices, on_device(): lax.ppermute(send, ('section', 'ty'), [(i, 3 - i) for i in range(4)])  3.7 us
    pallas_call x1, Pallas kernels, pick_columns(): pl.pallas_call(pick_kernel, out_shape=jax.ShapeDtypeStruct((n_groups, inn...  3.43 us
  transfers between devices with their start and end apart: 7, of which 6 were waited for; matrix products, arithmetic and copies ran while one was open for 3% of the time, Pallas kernels for 7%

profile of v19, /device:TPU:2, one launch (start us, length us, event | category | flops | bytes accessed | tf_op | source)
XLA Modules:
  0.0 146.6 jit_solution(6764766293651050514)
XLA Ops:
  6.5 3.2 %collective-permute-start = (bf16[256,384]{1,0:T(8,128)(2,1)}, bf16[256,384]{1,0:T(8,128)(2,1)S(1)}, u32[]{:S(2)}, u32[]{:S(2)}) collective-permute-start(bf16[256,384]{1,0:T(8,128)(2,1)} %bitcast.47), channel_id=1, source_target_pairs={{0,2},{2,0},{1,3},{3,1},{4,6},{6,4},{5,7},{7,5},{8,10},{10,8},{9,1... | collective-permute-start | bytes 589832 | tf_op jit(solution)/shard_map/ppermute | solution.py:17
  9.7 5.2 %collective-permute-done = bf16[256,384]{1,0:T(8,128)(2,1)S(1)} collective-permute-done((bf16[256,384]{1,0:T(8,128)(2,1)}, bf16[256,384]{1,0:T(8,128)(2,1)S(1)}, u32[]{:S(2)}, u32[]{:S(2)}) %collective-permute-start) | collective-permute-done | bytes 196640 | tf_op jit(solution)/shard_map/ppermute | solution.py:17
  14.9 1.0 select_bitcast_fusion.1
  15.9 0.8 pad_maximum_fusion
  16.7 3.4 %shard_map.56 = bf16[16,256,384]{2,1,0:T(8,128)(2,1)} custom-call(s32[1]{0:T(128)S(6)} %sub.17.sel_ref, bf16[256,12288]{1,0:T(8,128)(2,1)} %bitcast.29, bf16[256,12288]{1,0:T(8,128)(2,1)} %bitcast.30, bf16[256,12288]{1,0:T(8,128)(2,1)} %bitcast.31, bf16[256,12288]{1,0:T(8,128)(2,1)} %bitcast.32, bf16[256,12288]{1,0:T(8,128)(2,1)} %bitcast.33, ...), custom_call_target="tpu_custom_call" | custom-call | tf_op jit(solution)/shard_map/pallas_call | solution.py:34
  20.2 0.9 reshape.65
  21.2 0.3 fusion.15
  21.5 1.0 fusion.3
  22.6 43.3 %all-gather.3.cloned.1.call-done.f_ref = bf16[32,256,384]{2,1,0:T(8,128)(2,1)} async-done(((bf16[2,256,384]{2,1,0:T(8,128)(2,1)}), bf16[32,256,384]{2,1,0:T(8,128)(2,1)}) %all-gather.3.cloned.1.call-update) | async-done | bytes 6291472 | tf_op jit(solution)/shard_map/all_gather | solution.py:133
  65.8 7.1 %shard_map.55 = bf16[256,256]{1,0:T(8,128)(2,1)} custom-call(bf16[32,256,384]{2,1,0:T(8,128)(2,1)} %all-gather.3.cloned.1.call-done.f_ref, bf16[12288,256]{1,0:T(8,128)(2,1)} %bitcast.46), custom_call_target="tpu_custom_call" | custom-call | tf_op jit(solution)/shard_map/pallas_call | solution.py:107
  73.0 1.5 %convolution_convert_fusion = bf16[2,128,256]{2,1,0:T(8,128)(2,1)S(1)} fusion(bf16[256,2,128]{0,2,1:T(8,128)(2,1)} %bitcast.48, f32[2,256]{1,0:T(2,128)S(1)} %fusion.15, f32[2,256,256]{1,2,0:T(8,128)} %fusion.3), kind=kOutput, calls=%fused_computation.5 | convolution fusion | flops 34013952 | bytes 788480 | tf_op jit(solution)/shard_map/bhqk,bkhd->bqhd/dot_general | solution.py:149
  74.5 0.1 copy.15.ctx_ref
  74.6 0.3 collective-permute-start.1
  74.9 1.2 collective-permute-done.1.ctx_sib_ref
  76.2 0.4 copy-done
  76.6 6.1 %shard_map.57 = bf16[16,256,384]{2,1,0:T(8,128)(2,1)} custom-call(s32[1]{0:T(128)} %bitcast.core_ref, bf16[256,256]{1,0:T(8,128)(2,1)} %copy-done.2, bf16[256,256]{1,0:T(8,128)(2,1)} %collective-permute-done.1.ctx_sib_ref, bf16[16,256,384]{2,1,0:T(8,128)(2,1)} %copy-done, bf16[256,12288]{1,0:T(8,128)(2,1)} %bitcast.37, bf16[256,12288]{1,0:T(8,128)(2,1)} %bitcast.38, ...), custom_call_target="tpu_custom_call" | custom-call | tf_op jit(solution)/shard_map/pallas_call | solution.py:60
  82.7 45.8 %reduce-scatter.2.cloned.1.call-done = bf16[1,2,256,384]{3,2,1,0:T(8,128)(2,1)} async-done(((bf16[8,2,256,384]{3,2,1,0:T(8,128)(2,1)}), bf16[1,2,256,384]{3,2,1,0:T(8,128)(2,1)}) %reduce-scatter.2.cloned.1.call-update) | async-done | bytes 393232 | tf_op jit(solution)/shard_map/reduce_scatter | solution.py:156
  128.6 1.0 fusion.4
  129.5 1.5 %collective-permute-start.3 = (bf16[256,384]{1,0:T(8,128)(2,1)S(1)}, bf16[256,384]{1,0:T(8,128)(2,1)S(1)}, u32[]{:S(2)}, u32[]{:S(2)}) collective-permute-start(bf16[256,384]{1,0:T(8,128)(2,1)S(1)} %fusion.4), channel_id=1, source_target_pairs={{0,128},{128,0},{1,129},{129,1},{2,130},{130,2},{3,131},{131,3},{4... | collective-permute-start | bytes 589832 | tf_op jit(solution)/shard_map/ppermute | solution.py:17
  131.1 0.9 dynamic-slice_bitcast_fusion
  132.0 2.2 %collective-permute-start.4 = (bf16[256,384]{1,0:T(8,128)(2,1)S(1)}, bf16[256,384]{1,0:T(8,128)(2,1)S(1)}, u32[]{:S(2)}, u32[]{:S(2)}) collective-permute-start(bf16[256,384]{1,0:T(8,128)(2,1)S(1)} %dynamic-slice_bitcast_fusion), channel_id=1, source_target_pairs={{0,130},{2,128},{128,2},{130,0},{1,131},{3,129},{129,3},{131,1},{4... | collective-permute-start | bytes 589832 | tf_op jit(solution)/shard_map/ppermute | solution.py:161
  134.2 1.1 collective-permute-done.3
  135.3 3.7 %collective-permute-done.4 = bf16[256,384]{1,0:T(8,128)(2,1)S(1)} collective-permute-done((bf16[256,384]{1,0:T(8,128)(2,1)S(1)}, bf16[256,384]{1,0:T(8,128)(2,1)S(1)}, u32[]{:S(2)}, u32[]{:S(2)}) %collective-permute-start.4) | collective-permute-done | bytes 196640 | tf_op jit(solution)/shard_map/ppermute | solution.py:161
  139.0 0.7 fusion.5
  (15 shorter events, 0.2 us)
Async XLA Ops:
  6.5 59.3 %all-gather.3.cloned.1.call-start = ((), (), s32[]{:S(2)}) async-start(), calls=%async_computation.2 | async-start | bytes 6684672 | tf_op jit(solution)/shard_map/all_gather | solution.py:133
  6.5 8.4 %collective-permute-start = (bf16[256,384]{1,0:T(8,128)(2,1)}, bf16[256,384]{1,0:T(8,128)(2,1)S(1)}, u32[]{:S(2)}, u32[]{:S(2)}) collective-permute-start(bf16[256,384]{1,0:T(8,128)(2,1)} %bitcast.47), channel_id=1, source_target_pairs={{0,2},{2,0},{1,3},{3,1},{4,6},{6,4},{5,7},{7,5},{8,10},{10,8},{9,1... | collective-permute-start | bytes 589832 | tf_op jit(solution)/shard_map/ppermute | solution.py:17
  16.7 111.9 %reduce-scatter.2.cloned.1.call-start = ((), (), s32[]{:S(2)}) async-start(), calls=%async_computation.1 | async-start | bytes 3538944 | tf_op jit(solution)/shard_map/reduce_scatter | solution.py:156
  16.7 3.4 %copy-start.3 = (bf16[1,256,256]{2,1,0:T(8,128)(2,1)S(1)}, bf16[1,256,256]{2,1,0:T(8,128)(2,1)}, u32[]{:S(2)}) copy-start(bf16[1,256,256]{2,1,0:T(8,128)(2,1)} %param.6) | copy-start | bytes 393220
  20.2 54.8 %collective-permute-start.2 = (bf16[16,256,384]{2,1,0:T(8,128)(2,1)}, bf16[16,256,384]{2,1,0:T(8,128)(2,1)S(1)}, u32[]{:S(2)}, u32[]{:S(2)}) collective-permute-start(bf16[16,256,384]{2,1,0:T(8,128)(2,1)} %shard_map.56), channel_id=1, source_target_pairs={{0,1},{1,0},{2,3},{3,2},{4,5},{5,4},{6,7},{7,6},{8,9},{9,8},{10,11... | collective-permute-start | bytes 9437192 | tf_op jit(solution)/shard_map/ppermute | solution.py:17
  74.6 1.6 %copy-start.2 = (bf16[256,256]{1,0:T(8,128)(2,1)}, bf16[256,256]{1,0:T(8,128)(2,1)S(1)}, u32[]{:S(2)}) copy-start(bf16[256,256]{1,0:T(8,128)(2,1)S(1)} %copy.15.ctx_ref) | copy-start | bytes 393220
  74.6 54.0 %copy-start.1 = (bf16[1,256,384]{2,1,0:T(8,128)(2,1)S(1)}, bf16[1,256,384]{2,1,0:T(8,128)(2,1)}, u32[]{:S(2)}) copy-start(bf16[1,256,384]{2,1,0:T(8,128)(2,1)} %param.5) | copy-start | bytes 589828
  74.6 1.6 %collective-permute-start.1 = (bf16[256,256]{1,0:T(8,128)(2,1)S(1)}, bf16[256,256]{1,0:T(8,128)(2,1)}, u32[]{:S(2)}, u32[]{:S(2)}) collective-permute-start(bf16[256,256]{1,0:T(8,128)(2,1)S(1)} %copy.15.ctx_ref), channel_id=1, source_target_pairs={{0,1},{1,0},{2,3},{3,2},{4,5},{5,4},{6,7},{7,6},{8,9},{9,8},{10,11... | collective-permute-start | bytes 393224 | tf_op jit(solution)/shard_map/ppermute | solution.py:17
  74.9 1.7 %copy-start = (bf16[16,256,384]{2,1,0:T(8,128)(2,1)}, bf16[16,256,384]{2,1,0:T(8,128)(2,1)S(1)}, u32[]{:S(2)}) copy-start(bf16[16,256,384]{2,1,0:T(8,128)(2,1)S(1)} %collective-permute-done.2.w_sib_ref) | copy-start | bytes 9437188
  129.5 5.8 %collective-permute-start.3 = (bf16[256,384]{1,0:T(8,128)(2,1)S(1)}, bf16[256,384]{1,0:T(8,128)(2,1)S(1)}, u32[]{:S(2)}, u32[]{:S(2)}) collective-permute-start(bf16[256,384]{1,0:T(8,128)(2,1)S(1)} %fusion.4), channel_id=1, source_target_pairs={{0,128},{128,0},{1,129},{129,1},{2,130},{130,2},{3,131},{131,3},{4... | collective-permute-start | bytes 589832 | tf_op jit(solution)/shard_map/ppermute | solution.py:17
  132.0 7.0 %collective-permute-start.4 = (bf16[256,384]{1,0:T(8,128)(2,1)S(1)}, bf16[256,384]{1,0:T(8,128)(2,1)S(1)}, u32[]{:S(2)}, u32[]{:S(2)}) collective-permute-start(bf16[256,384]{1,0:T(8,128)(2,1)S(1)} %dynamic-slice_bitcast_fusion), channel_id=1, source_target_pairs={{0,130},{2,128},{128,2},{130,0},{1,131},{3,129},{129,3},{131,1},{4... | collective-permute-start | bytes 589832 | tf_op jit(solution)/shard_map/ppermute | solution.py:161
Sparse Core Ops, SparseCore 0:
  16.8 48.9 all-gather.2
  82.9 45.6 reduce-scatter.1

commit v20 on v17

--- a/solution.py
+++ b/solution.py
@@ -10,7 +10,7 @@
 LEN = 256
 N_Z, N_Y, N_C = 8, 2, 2
 GROUPS_PER_STEP = 16
-Z_PER_STEP = 8
+Z_PER_STEP = 4
 
 
 def swap(value, axis):

time: 148 us -> 147 us (level)
  transfers between devices with their start and end apart: 7 -> 7, of which waited for: 6 -> 6; matrix products, arithmetic and copies ran while one was open for 3% -> 3% of each run, Pallas kernels for 8% -> 7%
where the time goes in v20:
time: 147 us
  waiting for transfers between devices  100 us (68%)
  Pallas kernels  17.5 us (12%)
  between operations  13.5 us (9%)
  starting transfers between devices  7.17 us (5%)
  other arithmetic  3.49 us (2%)
  matrix products  2.88 us (2%)
  local copies, waits for them, and re-layouts  2.48 us (2%)
    reduce_scatter x1, waiting for transfers between devices, on_device(): part = lax.psum_scatter(part, 'tz', scatter_dimension=0, tiled=False)  46 us
    all_gather x1, waiting for transfers between devices, on_device(): gathered = lax.all_gather(gathered, ('tz', 'tc'), axis=0)  42.7 us
    ppermute x4, waiting for transfers between devices, swap(): return lax.ppermute(value, axis, [(0, 1), (1, 0)])  7.6 us
    pallas_call x1, Pallas kernels, out_proj(): pl.pallas_call(out_proj_kernel, out_shape=jax.ShapeDtypeStruct((n_groups,...  6.94 us
    pallas_call x1, Pallas kernels, gathered_proj(): pl.pallas_call(gathered_proj_kernel, out_shape=jax.ShapeDtypeStruct((weig...  6.6 us
    ppermute x4, starting transfers between devices, swap(): return lax.ppermute(value, axis, [(0, 1), (1, 0)])  5.04 us
    pallas_call x1, Pallas kernels, pick_columns(): pl.pallas_call(pick_kernel, out_shape=jax.ShapeDtypeStruct((n_groups, inn...  3.97 us
    ppermute x1, waiting for transfers between devices, on_device(): lax.ppermute(send, ('section', 'ty'), [(i, 3 - i) for i in range(4)])  3.67 us
  transfers between devices with their start and end apart: 7, of which 6 were waited for; matrix products, arithmetic and copies ran while one was open for 3% of the time, Pallas kernels for 7%

profile of v20, /device:TPU:2, one launch (start us, length us, event | category | flops | bytes accessed | tf_op | source)
XLA Modules:
  0.0 147.0 jit_solution(12650192640876120640)
XLA Ops:
  6.5 3.2 %collective-permute-start = (bf16[256,384]{1,0:T(8,128)(2,1)}, bf16[256,384]{1,0:T(8,128)(2,1)S(1)}, u32[]{:S(2)}, u32[]{:S(2)}) collective-permute-start(bf16[256,384]{1,0:T(8,128)(2,1)} %bitcast.63), channel_id=1, source_target_pairs={{0,2},{2,0},{1,3},{3,1},{4,6},{6,4},{5,7},{7,5},{8,10},{10,8},{9,1... | collective-permute-start | bytes 589832 | tf_op jit(solution)/shard_map/ppermute | solution.py:17
  9.7 5.2 %collective-permute-done = bf16[256,384]{1,0:T(8,128)(2,1)S(1)} collective-permute-done((bf16[256,384]{1,0:T(8,128)(2,1)}, bf16[256,384]{1,0:T(8,128)(2,1)S(1)}, u32[]{:S(2)}, u32[]{:S(2)}) %collective-permute-start) | collective-permute-done | bytes 196640 | tf_op jit(solution)/shard_map/ppermute | solution.py:17
  14.9 1.0 select_bitcast_fusion.1
  15.9 0.8 pad_maximum_fusion
  16.7 4.0 %shard_map.56 = bf16[16,256,384]{2,1,0:T(8,128)(2,1)} custom-call(s32[1]{0:T(128)S(6)} %sub.17.sel_ref, bf16[256,12288]{1,0:T(8,128)(2,1)} %bitcast.44, bf16[256,12288]{1,0:T(8,128)(2,1)} %bitcast.30, bf16[256,12288]{1,0:T(8,128)(2,1)} %bitcast.31, bf16[256,12288]{1,0:T(8,128)(2,1)} %bitcast.32, bf16[256,12288]{1,0:T(8,128)(2,1)} %bitcast.33, ...), custom_call_target="tpu_custom_call" | custom-call | tf_op jit(solution)/shard_map/pallas_call | solution.py:34
  20.8 0.9 reshape.65
  21.7 0.3 fusion.15
  22.1 1.0 fusion.3
  23.1 42.7 %all-gather.3.cloned.1.call-done.f_ref = bf16[32,256,384]{2,1,0:T(8,128)(2,1)} async-done(((bf16[2,256,384]{2,1,0:T(8,128)(2,1)}), bf16[32,256,384]{2,1,0:T(8,128)(2,1)}) %all-gather.3.cloned.1.call-update) | async-done | bytes 6291472 | tf_op jit(solution)/shard_map/all_gather | solution.py:133
  65.8 6.6 %shard_map.55 = bf16[256,256]{1,0:T(8,128)(2,1)} custom-call(bf16[32,256,384]{2,1,0:T(8,128)(2,1)} %all-gather.3.cloned.1.call-done.f_ref, bf16[12288,256]{1,0:T(8,128)(2,1)} %bitcast.62), custom_call_target="tpu_custom_call" | custom-call | tf_op jit(solution)/shard_map/pallas_call | solution.py:107
  72.4 1.5 %convolution_convert_fusion = bf16[2,128,256]{2,1,0:T(8,128)(2,1)S(1)} fusion(bf16[256,2,128]{0,2,1:T(8,128)(2,1)} %bitcast.64, f32[2,256]{1,0:T(2,128)S(1)} %fusion.15, f32[2,256,256]{1,2,0:T(8,128)} %fusion.3), kind=kOutput, calls=%fused_computation.5 | convolution fusion | flops 34013952 | bytes 788480 | tf_op jit(solution)/shard_map/bhqk,bkhd->bqhd/dot_general | solution.py:149
  73.9 0.1 copy.15.ctx_ref
  74.1 0.3 collective-permute-start.1
  74.4 1.2 collective-permute-done.1.ctx_sib_ref
  75.6 0.4 copy-done
  76.1 6.9 %shard_map.57 = bf16[16,256,384]{2,1,0:T(8,128)(2,1)} custom-call(s32[1]{0:T(128)} %bitcast.core_ref, bf16[256,256]{1,0:T(8,128)(2,1)} %copy-done.2, bf16[256,256]{1,0:T(8,128)(2,1)} %collective-permute-done.1.ctx_sib_ref, bf16[16,256,384]{2,1,0:T(8,128)(2,1)} %copy-done, bf16[256,12288]{1,0:T(8,128)(2,1)} %bitcast.45, bf16[256,12288]{1,0:T(8,128)(2,1)} %bitcast.46, ...), custom_call_target="tpu_custom_call" | custom-call | tf_op jit(solution)/shard_map/pallas_call | solution.py:60
  83.1 46.0 %reduce-scatter.2.cloned.1.call-done = bf16[1,2,256,384]{3,2,1,0:T(8,128)(2,1)} async-done(((bf16[8,2,256,384]{3,2,1,0:T(8,128)(2,1)}), bf16[1,2,256,384]{3,2,1,0:T(8,128)(2,1)}) %reduce-scatter.2.cloned.1.call-update) | async-done | bytes 393232 | tf_op jit(solution)/shard_map/reduce_scatter | solution.py:156
  129.0 1.0 fusion.4
  130.0 1.5 %collective-permute-start.3 = (bf16[256,384]{1,0:T(8,128)(2,1)S(1)}, bf16[256,384]{1,0:T(8,128)(2,1)S(1)}, u32[]{:S(2)}, u32[]{:S(2)}) collective-permute-start(bf16[256,384]{1,0:T(8,128)(2,1)S(1)} %fusion.4), channel_id=1, source_target_pairs={{0,128},{128,0},{1,129},{129,1},{2,130},{130,2},{3,131},{131,3},{4... | collective-permute-start | bytes 589832 | tf_op jit(solution)/shard_map/ppermute | solution.py:17
  131.5 0.9 dynamic-slice_bitcast_fusion
  132.5 2.1 %collective-permute-start.4 = (bf16[256,384]{1,0:T(8,128)(2,1)S(1)}, bf16[256,384]{1,0:T(8,128)(2,1)S(1)}, u32[]{:S(2)}, u32[]{:S(2)}) collective-permute-start(bf16[256,384]{1,0:T(8,128)(2,1)S(1)} %dynamic-slice_bitcast_fusion), channel_id=1, source_target_pairs={{0,130},{2,128},{128,2},{130,0},{1,131},{3,129},{129,3},{131,1},{4... | collective-permute-start | bytes 589832 | tf_op jit(solution)/shard_map/ppermute | solution.py:161
  134.5 1.2 collective-permute-done.3
  135.8 3.7 %collective-permute-done.4 = bf16[256,384]{1,0:T(8,128)(2,1)S(1)} collective-permute-done((bf16[256,384]{1,0:T(8,128)(2,1)S(1)}, bf16[256,384]{1,0:T(8,128)(2,1)S(1)}, u32[]{:S(2)}, u32[]{:S(2)}) %collective-permute-start.4) | collective-permute-done | bytes 196640 | tf_op jit(solution)/shard_map/ppermute | solution.py:161
  139.4 0.7 fusion.5
  (15 shorter events, 0.2 us)
Async XLA Ops:
  6.5 59.3 %all-gather.3.cloned.1.call-start = ((), (), s32[]{:S(2)}) async-start(), calls=%async_computation.2 | async-start | bytes 6684672 | tf_op jit(solution)/shard_map/all_gather | solution.py:133
  6.5 8.4 %collective-permute-start = (bf16[256,384]{1,0:T(8,128)(2,1)}, bf16[256,384]{1,0:T(8,128)(2,1)S(1)}, u32[]{:S(2)}, u32[]{:S(2)}) collective-permute-start(bf16[256,384]{1,0:T(8,128)(2,1)} %bitcast.63), channel_id=1, source_target_pairs={{0,2},{2,0},{1,3},{3,1},{4,6},{6,4},{5,7},{7,5},{8,10},{10,8},{9,1... | collective-permute-start | bytes 589832 | tf_op jit(solution)/shard_map/ppermute | solution.py:17
  16.7 112.3 %reduce-scatter.2.cloned.1.call-start = ((), (), s32[]{:S(2)}) async-start(), calls=%async_computation.1 | async-start | bytes 3538944 | tf_op jit(solution)/shard_map/reduce_scatter | solution.py:156
  16.7 4.0 %copy-start.3 = (bf16[1,256,256]{2,1,0:T(8,128)(2,1)S(1)}, bf16[1,256,256]{2,1,0:T(8,128)(2,1)}, u32[]{:S(2)}) copy-start(bf16[1,256,256]{2,1,0:T(8,128)(2,1)} %param.6) | copy-start | bytes 393220
  20.7 53.7 %collective-permute-start.2 = (bf16[16,256,384]{2,1,0:T(8,128)(2,1)}, bf16[16,256,384]{2,1,0:T(8,128)(2,1)S(1)}, u32[]{:S(2)}, u32[]{:S(2)}) collective-permute-start(bf16[16,256,384]{2,1,0:T(8,128)(2,1)} %shard_map.56), channel_id=1, source_target_pairs={{0,1},{1,0},{2,3},{3,2},{4,5},{5,4},{6,7},{7,6},{8,9},{9,8},{10,11... | collective-permute-start | bytes 9437192 | tf_op jit(solution)/shard_map/ppermute | solution.py:17
  74.1 1.6 %copy-start.2 = (bf16[256,256]{1,0:T(8,128)(2,1)}, bf16[256,256]{1,0:T(8,128)(2,1)S(1)}, u32[]{:S(2)}) copy-start(bf16[256,256]{1,0:T(8,128)(2,1)S(1)} %copy.15.ctx_ref) | copy-start | bytes 393220
  74.1 54.9 %copy-start.1 = (bf16[1,256,384]{2,1,0:T(8,128)(2,1)S(1)}, bf16[1,256,384]{2,1,0:T(8,128)(2,1)}, u32[]{:S(2)}) copy-start(bf16[1,256,384]{2,1,0:T(8,128)(2,1)} %param.5) | copy-start | bytes 589828
  74.1 1.6 %collective-permute-start.1 = (bf16[256,256]{1,0:T(8,128)(2,1)S(1)}, bf16[256,256]{1,0:T(8,128)(2,1)}, u32[]{:S(2)}, u32[]{:S(2)}) collective-permute-start(bf16[256,256]{1,0:T(8,128)(2,1)S(1)} %copy.15.ctx_ref), channel_id=1, source_target_pairs={{0,1},{1,0},{2,3},{3,2},{4,5},{5,4},{6,7},{7,6},{8,9},{9,8},{10,11... | collective-permute-start | bytes 393224 | tf_op jit(solution)/shard_map/ppermute | solution.py:17
  74.4 1.7 %copy-start = (bf16[16,256,384]{2,1,0:T(8,128)(2,1)}, bf16[16,256,384]{2,1,0:T(8,128)(2,1)S(1)}, u32[]{:S(2)}) copy-start(bf16[16,256,384]{2,1,0:T(8,128)(2,1)S(1)} %collective-permute-done.2.w_sib_ref) | copy-start | bytes 9437188
  130.0 5.8 %collective-permute-start.3 = (bf16[256,384]{1,0:T(8,128)(2,1)S(1)}, bf16[256,384]{1,0:T(8,128)(2,1)S(1)}, u32[]{:S(2)}, u32[]{:S(2)}) collective-permute-start(bf16[256,384]{1,0:T(8,128)(2,1)S(1)} %fusion.4), channel_id=1, source_target_pairs={{0,128},{128,0},{1,129},{129,1},{2,130},{130,2},{3,131},{131,3},{4... | collective-permute-start | bytes 589832 | tf_op jit(solution)/shard_map/ppermute | solution.py:17
  132.5 7.0 %collective-permute-start.4 = (bf16[256,384]{1,0:T(8,128)(2,1)S(1)}, bf16[256,384]{1,0:T(8,128)(2,1)S(1)}, u32[]{:S(2)}, u32[]{:S(2)}) collective-permute-start(bf16[256,384]{1,0:T(8,128)(2,1)S(1)} %dynamic-slice_bitcast_fusion), channel_id=1, source_target_pairs={{0,130},{2,128},{128,2},{130,0},{1,131},{3,129},{129,3},{131,1},{4... | collective-permute-start | bytes 589832 | tf_op jit(solution)/shard_map/ppermute | solution.py:161
Sparse Core Ops, SparseCore 0:
  16.8 48.9 all-gather.2
  83.2 45.7 reduce-scatter.1
